TPU v7x, 256 devices: a whole 4x4x8 slice. The times are simulated.
256 devices in a mesh: blk: 32 (over z, y_lo, core), grp: 8 (over x, y_hi).
Axes of the slice: x: 4, y: 4 (y_hi: 2, y_lo: 2; y = y_hi * 2 + y_lo), z: 8, core: 2. Of those that a mesh axis runs over, the one named last changes fastest.
Arguments:
- low_sites: float32 [8, 32768], P(None, ('blk', 'grp')), may hold values from -6 to 6
- low_probes: float32 [8, 32768], P(None, ('blk', 'grp')), may hold values from -0.03314563 to 0.03314563
- high_probes: float32 [8, 16384], P(None, ('blk', 'grp')), may hold values from -0.03314563 to 0.03314563
- nested: int32 [16384], P(('blk', 'grp')), may hold values from 0 to 32767, as said below
- inv_len_low: float32 [8], replicated, may hold values from 0.15 to 0.6
- inv_len_diff: float32 [8], replicated, may hold values from 0.2 to 0.8
Outputs:
- low_out: float32 [8, 32768], P(None, ('blk', 'grp'))
- high_out: float32 [8, 16384], P(None, ('blk', 'grp'))
Inputs may be any that keep to these rules, and one draw needn't show every extreme that they name: `nested`: entries are distinct; the high sites in the aligned block of 512 entries number b all lie among the low sites b * 1024 to (b + 1) * 1024 - 1.
All inputs are finite; a program needn't handle non-finite values.
Results may differ from a plain program's by a relative error of at most 0.00021.
Values sent between devices are 32-bit elements; how exact they have to be, the bound alone decides.
No kernel may reach another device: no remote copies, remote signals or barrier semaphores. Data moves between devices by JAX's collectives and lax.ppermute only.
A program may use at most 64 MiB of HBM per device.

v0:
```python
import functools

import jax
import jax.numpy as jnp
from jax import lax
from jax.experimental import pallas as pl
from jax.experimental.pallas import tpu as pltpu
from jax.sharding import PartitionSpec as P


RHO = 0.9
VAR_DIFF = 1.0
SQRT_THREE = 1.7320508075688772

GRP_BITS = (2, 0, 1)
BLK_BITS = (4, 3, 2, 1, 0)


COL_SUB = 512


def _accumulate(rows, rn, cols, w):
    inner = jnp.dot(rows, cols, precision=lax.Precision.HIGHEST, preferred_element_type=jnp.float32)
    cn = jnp.sum(cols * cols, axis=0, keepdims=True)
    square = rn + cn - 2.0 * inner
    dist = jnp.sqrt(jnp.maximum(square, 0.0))
    tile = (1.0 + SQRT_THREE * dist) * jnp.exp(-SQRT_THREE * dist)
    return lax.dot_general(
        w, tile, (((1,), (1,)), ((), ())),
        precision=lax.Precision.HIGH, preferred_element_type=jnp.float32,
    )


def _piece_kernel(rl_ref, rd_ref, sl_ref, sd_ref, x_ref, ol_ref, od_ref, *, nb, nh):
    @pl.when(pl.program_id(0) == 0)
    def _init():
        ol_ref[...] = jnp.zeros(ol_ref.shape, jnp.float32)
        od_ref[...] = jnp.zeros(od_ref.shape, jnp.float32)

    rows_l = rl_ref[...]
    rows_d = rd_ref[...]
    rn_l = jnp.sum(rows_l * rows_l, axis=1, keepdims=True)
    rn_d = jnp.sum(rows_d * rows_d, axis=1, keepdims=True)
    scale_l = sl_ref[...]
    scale_d = sd_ref[...]

    def one_block(b, carry):
        acc_l, acc_d = carry
        for c in range(0, nb, COL_SUB):
            cols = x_ref[b, :, c:c + COL_SUB] * scale_l
            w = x_ref[b, :, nb + c:nb + c + COL_SUB]
            acc_l = acc_l + _accumulate(rows_l, rn_l, cols, w)
        for c in range(0, nh, COL_SUB):
            cols = x_ref[b, :, 2 * nb + c:2 * nb + c + COL_SUB] * scale_d
            w = x_ref[b, :, 2 * nb + nh + c:2 * nb + nh + c + COL_SUB]
            acc_d = acc_d + _accumulate(rows_d, rn_d, cols, w)
        return acc_l, acc_d

    zero_l = jnp.zeros(ol_ref.shape, jnp.float32)
    zero_d = jnp.zeros(od_ref.shape, jnp.float32)
    acc_l, acc_d = lax.fori_loop(0, x_ref.shape[0], one_block, (zero_l, zero_d))
    ol_ref[...] += acc_l
    od_ref[...] += acc_d


def apply_piece(rows_low, rows_diff, inv_len_low, inv_len_diff, piece, nb, nh, interpret=False):
    n, feats, width = piece.shape
    probes = piece.shape[1]
    per = min(n, 4)
    rl, rd = rows_low.shape[1], rows_diff.shape[1]
    kern = functools.partial(_piece_kernel, nb=nb, nh=nh)
    full = lambda shape: pl.BlockSpec(shape, lambda j: (0,) * len(shape))
    return pl.pallas_call(
        kern,
        grid=(n // per,),
        in_specs=[
            full((rl, feats)),
            full((rd, feats)),
            full((feats, 1)),
            full((feats, 1)),
            pl.BlockSpec((per, feats, width), lambda j: (j, 0, 0)),
        ],
        out_specs=[full((probes, rl)), full((probes, rd))],
        out_shape=[
            jax.ShapeDtypeStruct((probes, rl), jnp.float32),
            jax.ShapeDtypeStruct((probes, rd), jnp.float32),
        ],
        compiler_params=pltpu.CompilerParams(dimension_semantics=("arbitrary",)),
        interpret=interpret,
    )(rows_low.T, rows_diff.T, inv_len_low[:, None], inv_len_diff[:, None], piece)


def gather_bits(x, axis, size, bits):
    me = lax.axis_index(axis)
    buf = x[None]
    for bit in bits:
        mask = 1 << bit
        other = lax.ppermute(buf, axis, [(i, i ^ mask) for i in range(size)])
        upper = ((me >> bit) & 1) == 1
        low = jnp.where(upper, other, buf)
        high = jnp.where(upper, buf, other)
        buf = jnp.concatenate([low, high], 0)
    k = len(bits)
    buf = buf.reshape((2,) * k + x.shape)
    order = sorted(range(k), key=lambda i: -bits[k - 1 - i])
    buf = buf.transpose(tuple(order) + tuple(range(k, k + x.ndim)))
    return buf.reshape((size,) + x.shape)


def per_device(low_sites, low_probes, high_probes, nested, inv_len_low, inv_len_diff):
    feats_n, rows_dev = low_sites.shape
    probes_n = low_probes.shape[0]
    highs_dev = high_probes.shape[1]
    grp_size = 1 << len(GRP_BITS)
    blk_size = 1 << len(BLK_BITS)

    packet = jnp.concatenate(
        [low_sites.reshape(-1), low_probes.reshape(-1), high_probes.reshape(-1), nested.astype(jnp.float32)]
    )
    got = gather_bits(packet, "grp", grp_size, GRP_BITS)
    cuts = [feats_n * rows_dev, probes_n * rows_dev, probes_n * highs_dev, highs_dev]
    pieces = []
    start = 0
    for c in cuts:
        pieces.append(got[:, start:start + c])
        start += c

    def unblock(piece, rows):
        return piece.reshape(grp_size, rows, -1).transpose(1, 0, 2).reshape(rows, -1)

    feats_block = unblock(pieces[0], feats_n)
    lowp_block = unblock(pieces[1], probes_n)
    highp_block = unblock(pieces[2], probes_n)
    nest_block = pieces[3].reshape(-1).astype(jnp.int32)

    width = feats_block.shape[1]
    base = lax.axis_index("blk") * width
    place_block = nest_block - base
    slots = lax.broadcasted_iota(jnp.int32, (width,), 0)
    pick = (slots[:, None] == place_block[None, :]).astype(jnp.float32)
    high_feats_block = jnp.dot(
        feats_block, pick, precision=lax.Precision.HIGHEST, preferred_element_type=jnp.float32
    )
    spread = lax.dot_general(
        highp_block, pick, (((1,), (1,)), ((), ())),
        precision=lax.Precision.HIGHEST, preferred_element_type=jnp.float32,
    )
    mixed_block = lowp_block + RHO * spread

    own_high = lax.axis_index("grp") * highs_dev
    high_feats = lax.dynamic_slice_in_dim(high_feats_block, own_high, highs_dev, 1)
    pick_own = lax.dynamic_slice_in_dim(pick, own_high, highs_dev, 1)

    wide = jnp.concatenate([feats_block, mixed_block, high_feats_block, highp_block], 1)
    nb = width
    nh = high_feats_block.shape[1]
    rows_low = low_sites * inv_len_low[:, None]
    rows_diff = high_feats * inv_len_diff[:, None]

    buf = wide[None]
    new_low, new_diff = apply_piece(rows_low, rows_diff, inv_len_low, inv_len_diff, buf, nb, nh)
    for bit in BLK_BITS:
        mask = 1 << bit
        other = lax.ppermute(buf, "blk", [(i, i ^ mask) for i in range(blk_size)])
        part_low, part_diff = apply_piece(rows_low, rows_diff, inv_len_low, inv_len_diff, other, nb, nh)
        new_low = new_low + part_low
        new_diff = new_diff + part_diff
        if bit != BLK_BITS[-1]:
            buf = jnp.concatenate([buf, other], 0)
    new_diff = VAR_DIFF * new_diff
    low_block = unblock(gather_bits(new_low, "grp", grp_size, GRP_BITS), probes_n)
    high_part = jnp.dot(
        low_block, pick_own, precision=lax.Precision.HIGHEST, preferred_element_type=jnp.float32
    )
    high_out = RHO * high_part + new_diff
    return (new_low, high_out)


def solution(mesh):
    return jax.shard_map(
        per_device,
        mesh=mesh,
        in_specs=(
            P(None, ("blk", "grp")),
            P(None, ("blk", "grp")),
            P(None, ("blk", "grp")),
            P(("blk", "grp")),
            P(),
            P(),
        ),
        out_specs=(P(None, ("blk", "grp")), P(None, ("blk", "grp"))),
        check_vma=False,
    )
```

profile of v0, /device:TPU:16, one launch (start us, length us, event | category | flops | bytes accessed | tf_op | source)
XLA Modules:
  0.0 142.5 jit_solution(8116057561895224668)
XLA Ops:
  0.6 0.8 reshape.60
  2.8 3.1 %collective-permute-start = (f32[1,2624]{1,0:T(1,128)S(1)}, f32[1,2624]{1,0:T(1,128)S(1)}, u32[]{:S(2)}, u32[]{:S(2)}) collective-permute-start(f32[1,2624]{1,0:T(1,128)S(1)} %broadcast_in_dim.10), channel_id=1, source_target_pairs={{0,4},{1,5},{2,6},{3,7},{4,0},{5,1},{6,2},{7,3},{8,12},{9,13},{10,... | collective-permute-start | bytes 31496 | tf_op jit(solution)/shard_map/ppermute | solution.py:98
  5.9 2.2 %collective-permute-done = f32[1,2624]{1,0:T(1,128)S(1)} collective-permute-done((f32[1,2624]{1,0:T(1,128)S(1)}, f32[1,2624]{1,0:T(1,128)S(1)}, u32[]{:S(2)}, u32[]{:S(2)}) %collective-permute-start) | collective-permute-done | bytes 10528 | tf_op jit(solution)/shard_map/ppermute | solution.py:98
  8.1 2.1 %collective-permute-start.1 = (f32[2,2624]{1,0:T(2,128)S(1)}, f32[2,2624]{1,0:T(2,128)S(1)}, u32[]{:S(2)}, u32[]{:S(2)}) collective-permute-start(f32[2,2624]{1,0:T(2,128)S(1)} %pad_maximum_fusion.6), channel_id=1, source_target_pairs={{0,1},{1,0},{2,3},{3,2},{4,5},{5,4},{6,7},{7,6},{8,9},{9,8},{10,11... | collective-permute-start | bytes 62984 | tf_op jit(solution)/shard_map/ppermute | solution.py:98
  10.2 3.3 %collective-permute-done.1 = f32[2,2624]{1,0:T(2,128)S(1)} collective-permute-done((f32[2,2624]{1,0:T(2,128)S(1)}, f32[2,2624]{1,0:T(2,128)S(1)}, u32[]{:S(2)}, u32[]{:S(2)}) %collective-permute-start.1) | collective-permute-done | bytes 21024 | tf_op jit(solution)/shard_map/ppermute | solution.py:98
  13.5 1.6 %collective-permute-start.2 = (f32[4,2624]{1,0:T(4,128)S(1)}, f32[4,2624]{1,0:T(4,128)S(1)}, u32[]{:S(2)}, u32[]{:S(2)}) collective-permute-start(f32[4,2624]{1,0:T(4,128)S(1)} %pad_maximum_fusion.4), channel_id=1, source_target_pairs={{0,2},{1,3},{2,0},{3,1},{4,6},{5,7},{6,4},{7,5},{8,10},{9,11},{10,... | collective-permute-start | bytes 125960 | tf_op jit(solution)/shard_map/ppermute | solution.py:98
  15.1 2.5 %collective-permute-done.2 = f32[4,2624]{1,0:T(4,128)S(1)} collective-permute-done((f32[4,2624]{1,0:T(4,128)S(1)}, f32[4,2624]{1,0:T(4,128)S(1)}, u32[]{:S(2)}, u32[]{:S(2)}) %collective-permute-start.2) | collective-permute-done | bytes 42016 | tf_op jit(solution)/shard_map/ppermute | solution.py:98
  18.2 0.7 fusion.1
  18.9 1.0 fusion
  20.0 7.3 %collective-permute-start.3 = (f32[1,8,3072]{2,1,0:T(8,128)S(1)}, f32[1,8,3072]{2,1,0:T(8,128)S(1)}, u32[]{:S(2)}, u32[]{:S(2)}) collective-permute-start(f32[1,8,3072]{2,1,0:T(8,128)S(1)} %maximum_bitcast_fusion.x_ref), channel_id=1, source_target_pairs={{0,128},{8,136},{16,144},{24,152},{32,160},{40,168},{48,176},{56,1... | collective-permute-start | bytes 294920 | tf_op jit(solution)/shard_map/ppermute | solution.py:164
  27.2 3.5 %collective-permute-done.3.x_ref = f32[1,8,3072]{2,1,0:T(8,128)S(1)} collective-permute-done((f32[1,8,3072]{2,1,0:T(8,128)S(1)}, f32[1,8,3072]{2,1,0:T(8,128)S(1)}, u32[]{:S(2)}, u32[]{:S(2)}) %collective-permute-start.3) | collective-permute-done | bytes 98336 | tf_op jit(solution)/shard_map/ppermute | solution.py:164
  30.8 1.3 collective-permute-start.4
  32.0 7.7 %collective-permute-done.4.x_ref = f32[2,8,3072]{2,1,0:T(8,128)S(1)} collective-permute-done((f32[2,8,3072]{2,1,0:T(8,128)S(1)}, f32[2,8,3072]{2,1,0:T(8,128)S(1)}, u32[]{:S(2)}, u32[]{:S(2)}) %collective-permute-start.4) | collective-permute-done | bytes 196640 | tf_op jit(solution)/shard_map/ppermute | solution.py:164
  40.5 8.8 %collective-permute-done.5.x_ref = f32[4,8,3072]{2,1,0:T(8,128)S(1)} collective-permute-done((f32[4,8,3072]{2,1,0:T(8,128)S(1)}, f32[4,8,3072]{2,1,0:T(8,128)S(1)}, u32[]{:S(2)}, u32[]{:S(2)}) %collective-permute-start.5) | collective-permute-done | bytes 393248 | tf_op jit(solution)/shard_map/ppermute | solution.py:164
  49.4 1.4 collective-permute-start.6
  52.1 0.8 constant_dynamic-update-slice_fusion.1
  52.9 13.6 %collective-permute-done.6.x_ref = f32[8,8,3072]{2,1,0:T(8,128)S(1)} collective-permute-done((f32[8,8,3072]{2,1,0:T(8,128)S(1)}, f32[8,8,3072]{2,1,0:T(8,128)S(1)}, u32[]{:S(2)}, u32[]{:S(2)}) %collective-permute-start.6) | collective-permute-done | bytes 786464 | tf_op jit(solution)/shard_map/ppermute | solution.py:164
  66.5 1.0 constant_dynamic-update-slice_fusion
  67.6 0.7 copy.62
  70.4 2.9 %shard_map.77 = (f32[8,128]{1,0:T(8,128)}, f32[8,64]{1,0:T(8,128)}) custom-call(f32[128,8]{1,0:T(8,128)} %bitcast.40, f32[64,8]{1,0:T(8,128)} %multiply_bitcast_fusion.rd_ref, f32[8,1]{1,0:T(8,128)} %copy.68.sl_ref, f32[8,1]{1,0:T(8,128)} %copy.69.sd_ref, f32[1,8,3072]{2,1,0:T(8,128)} %copy-done.3), custom_call_target="tpu_custom_call" | custom-call | tf_op jit(solution)/shard_map/pallas_call | solution.py:73
  73.3 2.9 %shard_map.78 = (f32[8,128]{1,0:T(8,128)}, f32[8,64]{1,0:T(8,128)}) custom-call(f32[128,8]{1,0:T(8,128)} %bitcast.41, f32[64,8]{1,0:T(8,128)} %multiply_bitcast_fusion.rd_ref, f32[8,1]{1,0:T(8,128)} %copy.68.sl_ref, f32[8,1]{1,0:T(8,128)} %copy.69.sd_ref, f32[1,8,3072]{2,1,0:T(8,128)} %copy-done.4), custom_call_target="tpu_custom_call" | custom-call | tf_op jit(solution)/shard_map/pallas_call | solution.py:73
  76.2 4.4 %shard_map.79 = (f32[8,128]{1,0:T(8,128)}, f32[8,64]{1,0:T(8,128)}) custom-call(f32[128,8]{1,0:T(8,128)} %bitcast.42, f32[64,8]{1,0:T(8,128)} %multiply_bitcast_fusion.rd_ref, f32[8,1]{1,0:T(8,128)} %copy.68.sl_ref, f32[8,1]{1,0:T(8,128)} %copy.69.sd_ref, f32[2,8,3072]{2,1,0:T(8,128)} %copy-done.2), custom_call_target="tpu_custom_call" | custom-call | tf_op jit(solution)/shard_map/pallas_call | solution.py:73
  80.6 7.3 %shard_map.80 = (f32[8,128]{1,0:T(8,128)}, f32[8,64]{1,0:T(8,128)}) custom-call(f32[128,8]{1,0:T(8,128)} %bitcast.43, f32[64,8]{1,0:T(8,128)} %multiply_bitcast_fusion.rd_ref, f32[8,1]{1,0:T(8,128)} %copy.68.sl_ref, f32[8,1]{1,0:T(8,128)} %copy.69.sd_ref, f32[4,8,3072]{2,1,0:T(8,128)} %copy-done), custom_call_target="tpu_custom_call" | custom-call | tf_op jit(solution)/shard_map/pallas_call | solution.py:73
  87.9 12.8 %shard_map.81 = (f32[8,128]{1,0:T(8,128)}, f32[8,64]{1,0:T(8,128)}) custom-call(f32[128,8]{1,0:T(8,128)} %bitcast.44, f32[64,8]{1,0:T(8,128)} %multiply_bitcast_fusion.rd_ref, f32[8,1]{1,0:T(8,128)} %copy.68.sl_ref, f32[8,1]{1,0:T(8,128)} %copy.69.sd_ref, f32[8,8,3072]{2,1,0:T(8,128)} %copy-done.1), custom_call_target="tpu_custom_call" | custom-call | tf_op jit(solution)/shard_map/pallas_call | solution.py:73
  100.8 1.2 copy-done.5
  101.9 24.0 %shard_map.82 = (f32[8,128]{1,0:T(8,128)}, f32[8,64]{1,0:T(8,128)}) custom-call(f32[128,8]{1,0:T(8,128)} %bitcast.45, f32[64,8]{1,0:T(8,128)} %multiply_bitcast_fusion.rd_ref, f32[8,1]{1,0:T(8,128)} %copy.68.sl_ref, f32[8,1]{1,0:T(8,128)} %copy.69.sd_ref, f32[16,8,3072]{2,1,0:T(8,128)} %copy-done.5), custom_call_target="tpu_custom_call" | custom-call | tf_op jit(solution)/shard_map/pallas_call | solution.py:73
  126.6 3.0 %collective-permute-start.8 = (f32[1,8,128]{2,1,0:T(8,128)S(1)}, f32[1,8,128]{2,1,0:T(8,128)S(1)}, u32[]{:S(2)}, u32[]{:S(2)}) collective-permute-start(f32[1,8,128]{2,1,0:T(8,128)S(1)} %bitcast.52), channel_id=1, source_target_pairs={{0,4},{1,5},{2,6},{3,7},{4,0},{5,1},{6,2},{7,3},{8,12},{9,13},{10,... | collective-permute-start | bytes 12296 | tf_op jit(solution)/shard_map/ppermute | solution.py:98
  129.7 2.1 %collective-permute-done.8 = f32[1,8,128]{2,1,0:T(8,128)S(1)} collective-permute-done((f32[1,8,128]{2,1,0:T(8,128)S(1)}, f32[1,8,128]{2,1,0:T(8,128)S(1)}, u32[]{:S(2)}, u32[]{:S(2)}) %collective-permute-start.8) | collective-permute-done | bytes 4128 | tf_op jit(solution)/shard_map/ppermute | solution.py:98
  132.1 4.8 %collective-permute-done.9 = f32[2,8,128]{2,1,0:T(8,128)S(1)} collective-permute-done((f32[2,8,128]{2,1,0:T(8,128)S(1)}, f32[2,8,128]{2,1,0:T(8,128)S(1)}, u32[]{:S(2)}, u32[]{:S(2)}) %collective-permute-start.9) | collective-permute-done | bytes 8224 | tf_op jit(solution)/shard_map/ppermute | solution.py:98
  136.9 1.6 %collective-permute-start.10 = (f32[4,8,128]{2,1,0:T(8,128)S(1)}, f32[4,8,128]{2,1,0:T(8,128)S(1)}, u32[]{:S(2)}, u32[]{:S(2)}) collective-permute-start(f32[4,8,128]{2,1,0:T(8,128)S(1)} %pad_maximum_fusion.7), channel_id=1, source_target_pairs={{0,2},{1,3},{2,0},{3,1},{4,6},{5,7},{6,4},{7,5},{8,10},{9,11},{10,... | collective-permute-start | bytes 49160 | tf_op jit(solution)/shard_map/ppermute | solution.py:98
  138.9 1.8 %collective-permute-done.10 = f32[4,8,128]{2,1,0:T(8,128)S(1)} collective-permute-done((f32[4,8,128]{2,1,0:T(8,128)S(1)}, f32[4,8,128]{2,1,0:T(8,128)S(1)}, u32[]{:S(2)}, u32[]{:S(2)}) %collective-permute-start.10) | collective-permute-done | bytes 16416 | tf_op jit(solution)/shard_map/ppermute | solution.py:98
  141.2 1.3 add_add_fusion
  (86 shorter events, 8.2 us)
Async XLA Ops:
  2.8 5.3 %collective-permute-start = (f32[1,2624]{1,0:T(1,128)S(1)}, f32[1,2624]{1,0:T(1,128)S(1)}, u32[]{:S(2)}, u32[]{:S(2)}) collective-permute-start(f32[1,2624]{1,0:T(1,128)S(1)} %broadcast_in_dim.10), channel_id=1, source_target_pairs={{0,4},{1,5},{2,6},{3,7},{4,0},{5,1},{6,2},{7,3},{8,12},{9,13},{10,... | collective-permute-start | bytes 31496 | tf_op jit(solution)/shard_map/ppermute | solution.py:98
  8.1 5.4 %collective-permute-start.1 = (f32[2,2624]{1,0:T(2,128)S(1)}, f32[2,2624]{1,0:T(2,128)S(1)}, u32[]{:S(2)}, u32[]{:S(2)}) collective-permute-start(f32[2,2624]{1,0:T(2,128)S(1)} %pad_maximum_fusion.6), channel_id=1, source_target_pairs={{0,1},{1,0},{2,3},{3,2},{4,5},{5,4},{6,7},{7,6},{8,9},{9,8},{10,11... | collective-permute-start | bytes 62984 | tf_op jit(solution)/shard_map/ppermute | solution.py:98
  13.5 4.1 %collective-permute-start.2 = (f32[4,2624]{1,0:T(4,128)S(1)}, f32[4,2624]{1,0:T(4,128)S(1)}, u32[]{:S(2)}, u32[]{:S(2)}) collective-permute-start(f32[4,2624]{1,0:T(4,128)S(1)} %pad_maximum_fusion.4), channel_id=1, source_target_pairs={{0,2},{1,3},{2,0},{3,1},{4,6},{5,7},{6,4},{7,5},{8,10},{9,11},{10,... | collective-permute-start | bytes 125960 | tf_op jit(solution)/shard_map/ppermute | solution.py:98
  20.0 31.5 %copy-start.3 = (f32[1,8,3072]{2,1,0:T(8,128)}, f32[1,8,3072]{2,1,0:T(8,128)S(1)}, u32[]{:S(2)}) copy-start(f32[1,8,3072]{2,1,0:T(8,128)S(1)} %maximum_bitcast_fusion.x_ref) | copy-start | bytes 294916
  20.0 10.8 %collective-permute-start.3 = (f32[1,8,3072]{2,1,0:T(8,128)S(1)}, f32[1,8,3072]{2,1,0:T(8,128)S(1)}, u32[]{:S(2)}, u32[]{:S(2)}) collective-permute-start(f32[1,8,3072]{2,1,0:T(8,128)S(1)} %maximum_bitcast_fusion.x_ref), channel_id=1, source_target_pairs={{0,128},{8,136},{16,144},{24,152},{32,160},{40,168},{48,176},{56,1... | collective-permute-start | bytes 294920 | tf_op jit(solution)/shard_map/ppermute | solution.py:164
  30.7 20.7 %copy-start.4 = (f32[1,8,3072]{2,1,0:T(8,128)}, f32[1,8,3072]{2,1,0:T(8,128)S(1)}, u32[]{:S(2)}) copy-start(f32[1,8,3072]{2,1,0:T(8,128)S(1)} %collective-permute-done.3.x_ref) | copy-start | bytes 294916
  30.8 9.0 %collective-permute-start.4 = (f32[2,8,3072]{2,1,0:T(8,128)S(1)}, f32[2,8,3072]{2,1,0:T(8,128)S(1)}, u32[]{:S(2)}, u32[]{:S(2)}) collective-permute-start(f32[2,8,3072]{2,1,0:T(8,128)S(1)} %pad_maximum_fusion.2), channel_id=1, source_target_pairs={{0,64},{8,72},{16,80},{24,88},{32,96},{40,104},{48,112},{56,120},{... | collective-permute-start | bytes 589832 | tf_op jit(solution)/shard_map/ppermute | solution.py:164
  39.8 12.4 %copy-start.2 = (f32[2,8,3072]{2,1,0:T(8,128)}, f32[2,8,3072]{2,1,0:T(8,128)S(1)}, u32[]{:S(2)}) copy-start(f32[2,8,3072]{2,1,0:T(8,128)S(1)} %collective-permute-done.4.x_ref) | copy-start | bytes 589828
  39.8 9.5 %collective-permute-start.5 = (f32[4,8,3072]{2,1,0:T(8,128)S(1)}, f32[4,8,3072]{2,1,0:T(8,128)S(1)}, u32[]{:S(2)}, u32[]{:S(2)}) collective-permute-start(f32[4,8,3072]{2,1,0:T(8,128)S(1)} %pad_maximum_fusion.1), channel_id=1, source_target_pairs={{0,32},{8,40},{16,48},{24,56},{32,0},{40,8},{48,16},{56,24},{64,96... | collective-permute-start | bytes 1179656 | tf_op jit(solution)/shard_map/ppermute | solution.py:164
  49.3 18.2 %copy-start = (f32[4,8,3072]{2,1,0:T(8,128)}, f32[4,8,3072]{2,1,0:T(8,128)S(1)}, u32[]{:S(2)}) copy-start(f32[4,8,3072]{2,1,0:T(8,128)S(1)} %collective-permute-done.5.x_ref) | copy-start | bytes 1179652
  49.4 18.1 %copy-start.7 = (f32[8,128]{1,0:T(8,128)S(1)}, f32[8,128]{1,0:T(8,128)}, u32[]{:S(2)}) copy-start(f32[8,128]{1,0:T(8,128)} %param.6) | copy-start | bytes 12292
  49.4 18.1 %copy-start.19 = (f32[8]{0:T(128)S(1)}, f32[8]{0:T(128)}, u32[]{:S(2)}) copy-start(f32[8]{0:T(128)} %param.10) | copy-start | bytes 100
  49.4 19.6 %copy-start.18 = (f32[8]{0:T(128)S(1)}, f32[8]{0:T(128)}, u32[]{:S(2)}) copy-start(f32[8]{0:T(128)} %param.11) | copy-start | bytes 100
  49.4 17.1 %collective-permute-start.6 = (f32[8,8,3072]{2,1,0:T(8,128)S(1)}, f32[8,8,3072]{2,1,0:T(8,128)S(1)}, u32[]{:S(2)}, u32[]{:S(2)}) collective-permute-start(f32[8,8,3072]{2,1,0:T(8,128)S(1)} %pad_maximum_fusion), channel_id=1, source_target_pairs={{0,16},{8,24},{16,0},{24,8},{32,48},{40,56},{48,32},{56,40},{64,80... | collective-permute-start | bytes 2359304 | tf_op jit(solution)/shard_map/ppermute | solution.py:164
  66.5 21.4 %copy-start.1 = (f32[8,8,3072]{2,1,0:T(8,128)}, f32[8,8,3072]{2,1,0:T(8,128)S(1)}, u32[]{:S(2)}) copy-start(f32[8,8,3072]{2,1,0:T(8,128)S(1)} %collective-permute-done.6.x_ref) | copy-start | bytes 2359300
  67.5 33.2 %collective-permute-start.7 = (f32[16,8,3072]{2,1,0:T(8,128)}, f32[16,8,3072]{2,1,0:T(8,128)S(1)}, u32[]{:S(2)}, u32[]{:S(2)}) collective-permute-start(f32[16,8,3072]{2,1,0:T(8,128)} %constant_dynamic-update-slice_fusion), channel_id=1, source_target_pairs={{0,8},{8,0},{16,24},{24,16},{32,40},{40,32},{48,56},{56,48},{64,72... | collective-permute-start | bytes 4718600 | tf_op jit(solution)/shard_map/ppermute | solution.py:164
  80.6 45.2 %copy-start.8 = (f32[8,128]{1,0:T(8,128)S(1)}, f32[8,128]{1,0:T(8,128)}, u32[]{:S(2)}) copy-start(f32[8,128]{1,0:T(8,128)} %get-tuple-element.14) | copy-start | bytes 12292
  80.6 45.3 %copy-start.9 = (f32[8,128]{1,0:T(8,128)S(1)}, f32[8,128]{1,0:T(8,128)}, u32[]{:S(2)}) copy-start(f32[8,128]{1,0:T(8,128)} %get-tuple-element.15) | copy-start | bytes 12292
  80.6 45.3 %copy-start.10 = (f32[8,128]{1,0:T(8,128)S(1)}, f32[8,128]{1,0:T(8,128)}, u32[]{:S(2)}) copy-start(f32[8,128]{1,0:T(8,128)} %get-tuple-element.16) | copy-start | bytes 12292
  87.9 38.0 %copy-start.11 = (f32[8,128]{1,0:T(8,128)S(1)}, f32[8,128]{1,0:T(8,128)}, u32[]{:S(2)}) copy-start(f32[8,128]{1,0:T(8,128)} %get-tuple-element.17) | copy-start | bytes 12292
  100.7 25.2 %copy-start.12 = (f32[8,128]{1,0:T(8,128)S(1)}, f32[8,128]{1,0:T(8,128)}, u32[]{:S(2)}) copy-start(f32[8,128]{1,0:T(8,128)} %get-tuple-element.18) | copy-start | bytes 12292
  100.7 40.4 %copy-start.13 = (f32[8,64]{1,0:T(8,128)S(1)}, f32[8,64]{1,0:T(8,128)}, u32[]{:S(2)}) copy-start(f32[8,64]{1,0:T(8,128)} %get-tuple-element.20) | copy-start | bytes 6148
  100.7 40.4 %copy-start.14 = (f32[8,64]{1,0:T(8,128)S(1)}, f32[8,64]{1,0:T(8,128)}, u32[]{:S(2)}) copy-start(f32[8,64]{1,0:T(8,128)} %get-tuple-element.21) | copy-start | bytes 6148
  100.7 40.4 %copy-start.15 = (f32[8,64]{1,0:T(8,128)S(1)}, f32[8,64]{1,0:T(8,128)}, u32[]{:S(2)}) copy-start(f32[8,64]{1,0:T(8,128)} %get-tuple-element.22) | copy-start | bytes 6148
  100.7 40.4 %copy-start.16 = (f32[8,64]{1,0:T(8,128)S(1)}, f32[8,64]{1,0:T(8,128)}, u32[]{:S(2)}) copy-start(f32[8,64]{1,0:T(8,128)} %get-tuple-element.23) | copy-start | bytes 6148
  100.7 40.4 %copy-start.17 = (f32[8,64]{1,0:T(8,128)S(1)}, f32[8,64]{1,0:T(8,128)}, u32[]{:S(2)}) copy-start(f32[8,64]{1,0:T(8,128)} %get-tuple-element.24) | copy-start | bytes 6148
  100.7 1.2 copy-start.5
  126.6 15.9 %copy-start.6 = (f32[8,128]{1,0:T(8,128)}, f32[8,128]{1,0:T(8,128)S(1)}, u32[]{:S(2)}) copy-start(f32[8,128]{1,0:T(8,128)S(1)} %add_add_fusion.1) | copy-start | bytes 12292
  126.6 5.1 %collective-permute-start.8 = (f32[1,8,128]{2,1,0:T(8,128)S(1)}, f32[1,8,128]{2,1,0:T(8,128)S(1)}, u32[]{:S(2)}, u32[]{:S(2)}) collective-permute-start(f32[1,8,128]{2,1,0:T(8,128)S(1)} %bitcast.52), channel_id=1, source_target_pairs={{0,4},{1,5},{2,6},{3,7},{4,0},{5,1},{6,2},{7,3},{8,12},{9,13},{10,... | collective-permute-start | bytes 12296 | tf_op jit(solution)/shard_map/ppermute | solution.py:98
  131.7 5.2 %collective-permute-start.9 = (f32[2,8,128]{2,1,0:T(8,128)S(1)}, f32[2,8,128]{2,1,0:T(8,128)S(1)}, u32[]{:S(2)}, u32[]{:S(2)}) collective-permute-start(f32[2,8,128]{2,1,0:T(8,128)S(1)} %pad_maximum_fusion.9), channel_id=1, source_target_pairs={{0,1},{1,0},{2,3},{3,2},{4,5},{5,4},{6,7},{7,6},{8,9},{9,8},{10,11... | collective-permute-start | bytes 24584 | tf_op jit(solution)/shard_map/ppermute | solution.py:98
  136.9 3.8 %collective-permute-start.10 = (f32[4,8,128]{2,1,0:T(8,128)S(1)}, f32[4,8,128]{2,1,0:T(8,128)S(1)}, u32[]{:S(2)}, u32[]{:S(2)}) collective-permute-start(f32[4,8,128]{2,1,0:T(8,128)S(1)} %pad_maximum_fusion.7), channel_id=1, source_target_pairs={{0,2},{1,3},{2,0},{3,1},{4,6},{5,7},{6,4},{7,5},{8,10},{9,11},{10,... | collective-permute-start | bytes 49160 | tf_op jit(solution)/shard_map/ppermute | solution.py:98
where the time goes:
time: 143 us; the launch traced here: 142 us
  Pallas kernels  54.2 us (38%)
  waiting for transfers between devices  50.3 us (35%)
  starting transfers between devices  21.8 us (15%)
  local copies, waits for them, and re-layouts  7.79 us (5%)
  other arithmetic  5.33 us (4%)
  matrix products  2.13 us (1%)
    pallas_call x6, Pallas kernels, apply_piece(): pl.pallas_call(kern, grid=(n // per,), in_specs=[full((rl, feats)), full(...  54.2 us
    ppermute x5, waiting for transfers between devices, per_device(): other = lax.ppermute(buf, 'blk', [(i, i ^ mask) for i in range(blk_size)])  33.6 us
    ppermute x6, waiting for transfers between devices, gather_bits(): other = lax.ppermute(buf, axis, [(i, i ^ mask) for i in range(size)])  16.7 us
    ppermute x6, starting transfers between devices, gather_bits(): other = lax.ppermute(buf, axis, [(i, i ^ mask) for i in range(size)])  11.8 us
    ppermute x5, starting transfers between devices, per_device(): other = lax.ppermute(buf, 'blk', [(i, i ^ mask) for i in range(blk_size)])  10 us
    unnamed x44, local copies, waits for them, and re-layouts  3.45 us
  transfers between devices with their start and end apart: 11, of which 10 were waited for; matrix products, arithmetic and copies ran while one was open for 4% of the time, Pallas kernels for 21%

commit v1 on v0

--- a/solution.py
+++ b/solution.py
@@ -11,6 +11,7 @@
 RHO = 0.9
 VAR_DIFF = 1.0
 SQRT_THREE = 1.7320508075688772
+
 
 GRP_BITS = (2, 0, 1)
 BLK_BITS = (4, 3, 2, 1, 0)
@@ -90,21 +91,13 @@
     )(rows_low.T, rows_diff.T, inv_len_low[:, None], inv_len_diff[:, None], piece)
 
 
-def gather_bits(x, axis, size, bits):
+def gather_direct(x, axis, size):
     me = lax.axis_index(axis)
-    buf = x[None]
-    for bit in bits:
-        mask = 1 << bit
-        other = lax.ppermute(buf, axis, [(i, i ^ mask) for i in range(size)])
-        upper = ((me >> bit) & 1) == 1
-        low = jnp.where(upper, other, buf)
-        high = jnp.where(upper, buf, other)
-        buf = jnp.concatenate([low, high], 0)
-    k = len(bits)
-    buf = buf.reshape((2,) * k + x.shape)
-    order = sorted(range(k), key=lambda i: -bits[k - 1 - i])
-    buf = buf.transpose(tuple(order) + tuple(range(k, k + x.ndim)))
-    return buf.reshape((size,) + x.shape)
+    recv = [x]
+    for s in range(1, size):
+        recv.append(lax.ppermute(x, axis, [(i, i ^ s) for i in range(size)]))
+    stacked = jnp.stack(recv)
+    return jnp.take(stacked, me ^ jnp.arange(size, dtype=jnp.int32), axis=0)
 
 
 def per_device(low_sites, low_probes, high_probes, nested, inv_len_low, inv_len_diff):
@@ -117,7 +110,7 @@
     packet = jnp.concatenate(
         [low_sites.reshape(-1), low_probes.reshape(-1), high_probes.reshape(-1), nested.astype(jnp.float32)]
     )
-    got = gather_bits(packet, "grp", grp_size, GRP_BITS)
+    got = gather_direct(packet, "grp", grp_size)
     cuts = [feats_n * rows_dev, probes_n * rows_dev, probes_n * highs_dev, highs_dev]
     pieces = []
     start = 0
@@ -168,7 +161,7 @@
         if bit != BLK_BITS[-1]:
             buf = jnp.concatenate([buf, other], 0)
     new_diff = VAR_DIFF * new_diff
-    low_block = unblock(gather_bits(new_low, "grp", grp_size, GRP_BITS), probes_n)
+    low_block = unblock(gather_direct(new_low, "grp", grp_size), probes_n)
     high_part = jnp.dot(
         low_block, pick_own, precision=lax.Precision.HIGHEST, preferred_element_type=jnp.float32
     )

time: 143 us -> 153 us (1.070)
  starting transfers between devices: 21.8 us -> 40.6 us
  waiting for transfers between devices: 50.3 us -> 40.5 us
    ppermute x6 -> x14, starting transfers between devices: 11.8 us -> 28.5 us  [gather_direct(): recv.append(lax.ppermute(x, axis, [(i, i ^ s) for i in range(size)]))]
    ppermute x6 -> x14, waiting for transfers between devices: 16.7 us -> 8.27 us  [gather_direct(): recv.append(lax.ppermute(x, axis, [(i, i ^ s) for i in range(size)]))]
    ppermute x5, starting transfers between devices: 10 us -> 12.1 us  [per_device(): other = lax.ppermute(buf, 'blk', [(i, i ^ mask) for i in range(blk_size)])]
    add x2 -> x0, other arithmetic: 1.98 us -> none  [the longest x1 1.29 us: per_device(): high_out = RHO * high_part + new_diff]
    unnamed x44 -> x50, local copies, waits for them, and re-layouts: 3.45 us -> 3.48 us
  transfers between devices with their start and end apart: 11 -> 19, of which waited for: 10 -> 8; matrix products, arithmetic and copies ran while one was open for 4% -> 4% of each run, Pallas kernels for 21% -> 20%
where the time goes in v1:
time: 153 us
  Pallas kernels  54.2 us (35%)
  starting transfers between devices  40.6 us (27%)
  waiting for transfers between devices  40.5 us (26%)
  local copies, waits for them, and re-layouts  8.99 us (6%)
  other arithmetic  3.98 us (3%)
  matrix products  3.44 us (2%)
    pallas_call x6, Pallas kernels, apply_piece(): pl.pallas_call(kern, grid=(n // per,), in_specs=[full((rl, feats)), full(...  54.2 us
    ppermute x5, waiting for transfers between devices, per_device(): other = lax.ppermute(buf, 'blk', [(i, i ^ mask) for i in range(blk_size)])  32.2 us
    ppermute x14, starting transfers between devices, gather_direct(): recv.append(lax.ppermute(x, axis, [(i, i ^ s) for i in range(size)]))  28.5 us
    ppermute x5, starting transfers between devices, per_device(): other = lax.ppermute(buf, 'blk', [(i, i ^ mask) for i in range(blk_size)])  12.1 us
    ppermute x14, waiting for transfers between devices, gather_direct(): recv.append(lax.ppermute(x, axis, [(i, i ^ s) for i in range(size)]))  8.27 us
    unnamed x50, local copies, waits for them, and re-layouts  3.48 us
  transfers between devices with their start and end apart: 19, of which 8 were waited for; matrix products, arithmetic and copies ran while one was open for 4% of the time, Pallas kernels for 20%

profile of v1, /device:TPU:16, one launch (start us, length us, event | category | flops | bytes accessed | tf_op | source)
XLA Modules:
  0.0 152.7 jit_solution(6890469263707459441)
XLA Ops:
  2.8 2.0 %collective-permute-start = (f32[2624]{0:T(1024)S(1)}, f32[2624]{0:T(1024)S(1)}, u32[]{:S(2)}, u32[]{:S(2)}) collective-permute-start(f32[2624]{0:T(1024)S(1)} %pad_maximum_fusion.3), channel_id=1, source_target_pairs={{0,1},{1,0},{2,3},{3,2},{4,5},{5,4},{6,7},{7,6},{8,9},{9,8},{10,11... | collective-permute-start | bytes 31496 | tf_op jit(solution)/shard_map/ppermute | solution.py:98
  4.8 2.9 %collective-permute-start.2 = (f32[2624]{0:T(1024)S(1)}, f32[2624]{0:T(1024)S(1)}, u32[]{:S(2)}, u32[]{:S(2)}) collective-permute-start(f32[2624]{0:T(1024)S(1)} %pad_maximum_fusion.3), channel_id=1, source_target_pairs={{0,3},{1,2},{2,1},{3,0},{4,7},{5,6},{6,5},{7,4},{8,11},{9,10},{10,... | collective-permute-start | bytes 31496 | tf_op jit(solution)/shard_map/ppermute | solution.py:98
  7.8 3.0 %collective-permute-start.3 = (f32[2624]{0:T(1024)S(1)}, f32[2624]{0:T(1024)S(1)}, u32[]{:S(2)}, u32[]{:S(2)}) collective-permute-start(f32[2624]{0:T(1024)S(1)} %pad_maximum_fusion.3), channel_id=1, source_target_pairs={{0,4},{1,5},{2,6},{3,7},{4,0},{5,1},{6,2},{7,3},{8,12},{9,13},{10,... | collective-permute-start | bytes 31496 | tf_op jit(solution)/shard_map/ppermute | solution.py:98
  10.8 2.0 %collective-permute-start.4 = (f32[2624]{0:T(1024)S(1)}, f32[2624]{0:T(1024)S(1)}, u32[]{:S(2)}, u32[]{:S(2)}) collective-permute-start(f32[2624]{0:T(1024)S(1)} %pad_maximum_fusion.3), channel_id=1, source_target_pairs={{0,5},{1,4},{2,7},{3,6},{4,1},{5,0},{6,3},{7,2},{8,13},{9,12},{10,... | collective-permute-start | bytes 31496 | tf_op jit(solution)/shard_map/ppermute | solution.py:98
  12.8 1.1 collective-permute-start.5
  13.9 3.1 %collective-permute-start.6 = (f32[2624]{0:T(1024)S(1)}, f32[2624]{0:T(1024)S(1)}, u32[]{:S(2)}, u32[]{:S(2)}) collective-permute-start(f32[2624]{0:T(1024)S(1)} %pad_maximum_fusion.3), channel_id=1, source_target_pairs={{0,7},{1,6},{2,5},{3,4},{4,3},{5,2},{6,1},{7,0},{8,15},{9,14},{10,... | collective-permute-start | bytes 31496 | tf_op jit(solution)/shard_map/ppermute | solution.py:98
  17.2 1.2 collective-permute-done.4
  18.4 2.8 %collective-permute-done.6 = f32[2624]{0:T(1024)S(1)} collective-permute-done((f32[2624]{0:T(1024)S(1)}, f32[2624]{0:T(1024)S(1)}, u32[]{:S(2)}, u32[]{:S(2)}) %collective-permute-start.6) | collective-permute-done | bytes 10528 | tf_op jit(solution)/shard_map/ppermute | solution.py:98
  23.1 1.0 fusion
  24.1 7.3 %collective-permute-start.7 = (f32[1,8,3072]{2,1,0:T(8,128)S(1)}, f32[1,8,3072]{2,1,0:T(8,128)S(1)}, u32[]{:S(2)}, u32[]{:S(2)}) collective-permute-start(f32[1,8,3072]{2,1,0:T(8,128)S(1)} %maximum_bitcast_fusion.x_ref), channel_id=1, source_target_pairs={{0,128},{8,136},{16,144},{24,152},{32,160},{40,168},{48,176},{56,1... | collective-permute-start | bytes 294920 | tf_op jit(solution)/shard_map/ppermute | solution.py:157
  31.4 3.6 %collective-permute-done.7.x_ref = f32[1,8,3072]{2,1,0:T(8,128)S(1)} collective-permute-done((f32[1,8,3072]{2,1,0:T(8,128)S(1)}, f32[1,8,3072]{2,1,0:T(8,128)S(1)}, u32[]{:S(2)}, u32[]{:S(2)}) %collective-permute-start.7) | collective-permute-done | bytes 98336 | tf_op jit(solution)/shard_map/ppermute | solution.py:157
  35.0 2.2 %collective-permute-start.8 = (f32[2,8,3072]{2,1,0:T(8,128)S(1)}, f32[2,8,3072]{2,1,0:T(8,128)S(1)}, u32[]{:S(2)}, u32[]{:S(2)}) collective-permute-start(f32[2,8,3072]{2,1,0:T(8,128)S(1)} %pad_maximum_fusion.2), channel_id=1, source_target_pairs={{0,64},{8,72},{16,80},{24,88},{32,96},{40,104},{48,112},{56,120},{... | collective-permute-start | bytes 589832 | tf_op jit(solution)/shard_map/ppermute | solution.py:157
  37.2 6.8 %collective-permute-done.8.x_ref = f32[2,8,3072]{2,1,0:T(8,128)S(1)} collective-permute-done((f32[2,8,3072]{2,1,0:T(8,128)S(1)}, f32[2,8,3072]{2,1,0:T(8,128)S(1)}, u32[]{:S(2)}, u32[]{:S(2)}) %collective-permute-start.8) | collective-permute-done | bytes 196640 | tf_op jit(solution)/shard_map/ppermute | solution.py:157
  44.8 8.6 %collective-permute-done.9.x_ref = f32[4,8,3072]{2,1,0:T(8,128)S(1)} collective-permute-done((f32[4,8,3072]{2,1,0:T(8,128)S(1)}, f32[4,8,3072]{2,1,0:T(8,128)S(1)}, u32[]{:S(2)}, u32[]{:S(2)}) %collective-permute-start.9) | collective-permute-done | bytes 393248 | tf_op jit(solution)/shard_map/ppermute | solution.py:157
  53.5 2.5 %collective-permute-start.10 = (f32[8,8,3072]{2,1,0:T(8,128)S(1)}, f32[8,8,3072]{2,1,0:T(8,128)S(1)}, u32[]{:S(2)}, u32[]{:S(2)}) collective-permute-start(f32[8,8,3072]{2,1,0:T(8,128)S(1)} %pad_maximum_fusion), channel_id=1, source_target_pairs={{0,16},{8,24},{16,0},{24,8},{32,48},{40,56},{48,32},{56,40},{64,80... | collective-permute-start | bytes 2359304 | tf_op jit(solution)/shard_map/ppermute | solution.py:157
  57.3 0.8 constant_dynamic-update-slice_fusion.1
  58.1 13.2 %collective-permute-done.10.x_ref = f32[8,8,3072]{2,1,0:T(8,128)S(1)} collective-permute-done((f32[8,8,3072]{2,1,0:T(8,128)S(1)}, f32[8,8,3072]{2,1,0:T(8,128)S(1)}, u32[]{:S(2)}, u32[]{:S(2)}) %collective-permute-start.10) | collective-permute-done | bytes 786464 | tf_op jit(solution)/shard_map/ppermute | solution.py:157
  71.4 1.0 constant_dynamic-update-slice_fusion
  75.3 2.9 %shard_map.77 = (f32[8,128]{1,0:T(8,128)}, f32[8,64]{1,0:T(8,128)}) custom-call(f32[128,8]{1,0:T(8,128)} %bitcast.54, f32[64,8]{1,0:T(8,128)} %multiply_bitcast_fusion.rd_ref, f32[8,1]{1,0:T(8,128)} %copy.31.sl_ref, f32[8,1]{1,0:T(8,128)} %copy.32.sd_ref, f32[1,8,3072]{2,1,0:T(8,128)} %copy-done.3), custom_call_target="tpu_custom_call" | custom-call | tf_op jit(solution)/shard_map/pallas_call | solution.py:74
  78.2 2.9 %shard_map.78 = (f32[8,128]{1,0:T(8,128)}, f32[8,64]{1,0:T(8,128)}) custom-call(f32[128,8]{1,0:T(8,128)} %bitcast.55, f32[64,8]{1,0:T(8,128)} %multiply_bitcast_fusion.rd_ref, f32[8,1]{1,0:T(8,128)} %copy.31.sl_ref, f32[8,1]{1,0:T(8,128)} %copy.32.sd_ref, f32[1,8,3072]{2,1,0:T(8,128)} %copy-done.4), custom_call_target="tpu_custom_call" | custom-call | tf_op jit(solution)/shard_map/pallas_call | solution.py:74
  81.1 4.4 %shard_map.79 = (f32[8,128]{1,0:T(8,128)}, f32[8,64]{1,0:T(8,128)}) custom-call(f32[128,8]{1,0:T(8,128)} %bitcast.56, f32[64,8]{1,0:T(8,128)} %multiply_bitcast_fusion.rd_ref, f32[8,1]{1,0:T(8,128)} %copy.31.sl_ref, f32[8,1]{1,0:T(8,128)} %copy.32.sd_ref, f32[2,8,3072]{2,1,0:T(8,128)} %copy-done.2), custom_call_target="tpu_custom_call" | custom-call | tf_op jit(solution)/shard_map/pallas_call | solution.py:74
  85.5 7.3 %shard_map.80 = (f32[8,128]{1,0:T(8,128)}, f32[8,64]{1,0:T(8,128)}) custom-call(f32[128,8]{1,0:T(8,128)} %bitcast.57, f32[64,8]{1,0:T(8,128)} %multiply_bitcast_fusion.rd_ref, f32[8,1]{1,0:T(8,128)} %copy.31.sl_ref, f32[8,1]{1,0:T(8,128)} %copy.32.sd_ref, f32[4,8,3072]{2,1,0:T(8,128)} %copy-done), custom_call_target="tpu_custom_call" | custom-call | tf_op jit(solution)/shard_map/pallas_call | solution.py:74
  92.8 12.8 %shard_map.81 = (f32[8,128]{1,0:T(8,128)}, f32[8,64]{1,0:T(8,128)}) custom-call(f32[128,8]{1,0:T(8,128)} %bitcast.58, f32[64,8]{1,0:T(8,128)} %multiply_bitcast_fusion.rd_ref, f32[8,1]{1,0:T(8,128)} %copy.31.sl_ref, f32[8,1]{1,0:T(8,128)} %copy.32.sd_ref, f32[8,8,3072]{2,1,0:T(8,128)} %copy-done.1), custom_call_target="tpu_custom_call" | custom-call | tf_op jit(solution)/shard_map/pallas_call | solution.py:74
  105.6 1.2 copy-done.5
  106.8 23.9 %shard_map.82 = (f32[8,128]{1,0:T(8,128)}, f32[8,64]{1,0:T(8,128)}) custom-call(f32[128,8]{1,0:T(8,128)} %bitcast.59, f32[64,8]{1,0:T(8,128)} %multiply_bitcast_fusion.rd_ref, f32[8,1]{1,0:T(8,128)} %copy.31.sl_ref, f32[8,1]{1,0:T(8,128)} %copy.32.sd_ref, f32[16,8,3072]{2,1,0:T(8,128)} %copy-done.5), custom_call_target="tpu_custom_call" | custom-call | tf_op jit(solution)/shard_map/pallas_call | solution.py:74
  131.5 2.8 %collective-permute-start.12 = (f32[8,128]{1,0:T(8,128)S(1)}, f32[8,128]{1,0:T(8,128)S(1)}, u32[]{:S(2)}, u32[]{:S(2)}) collective-permute-start(f32[8,128]{1,0:T(8,128)S(1)} %get-tuple-element.27), channel_id=1, source_target_pairs={{0,1},{1,0},{2,3},{3,2},{4,5},{5,4},{6,7},{7,6},{8,9},{9,8},{10,11... | collective-permute-start | bytes 12296 | tf_op jit(solution)/shard_map/ppermute | solution.py:98
  134.7 2.2 %collective-permute-start.14 = (f32[8,128]{1,0:T(8,128)S(1)}, f32[8,128]{1,0:T(8,128)S(1)}, u32[]{:S(2)}, u32[]{:S(2)}) collective-permute-start(f32[8,128]{1,0:T(8,128)S(1)} %get-tuple-element.27), channel_id=1, source_target_pairs={{0,3},{1,2},{2,1},{3,0},{4,7},{5,6},{6,5},{7,4},{8,11},{9,10},{10,... | collective-permute-start | bytes 12296 | tf_op jit(solution)/shard_map/ppermute | solution.py:98
  136.9 5.7 %collective-permute-start.16 = (f32[8,128]{1,0:T(8,128)S(1)}, f32[8,128]{1,0:T(8,128)S(1)}, u32[]{:S(2)}, u32[]{:S(2)}) collective-permute-start(f32[8,128]{1,0:T(8,128)S(1)} %get-tuple-element.27), channel_id=1, source_target_pairs={{0,5},{1,4},{2,7},{3,6},{4,1},{5,0},{6,3},{7,2},{8,13},{9,12},{10,... | collective-permute-start | bytes 12296 | tf_op jit(solution)/shard_map/ppermute | solution.py:98
  143.1 3.0 %collective-permute-start.18 = (f32[8,128]{1,0:T(8,128)S(1)}, f32[8,128]{1,0:T(8,128)S(1)}, u32[]{:S(2)}, u32[]{:S(2)}) collective-permute-start(f32[8,128]{1,0:T(8,128)S(1)} %get-tuple-element.27), channel_id=1, source_target_pairs={{0,7},{1,6},{2,5},{3,4},{4,3},{5,2},{6,1},{7,0},{8,15},{9,14},{10,... | collective-permute-start | bytes 12296 | tf_op jit(solution)/shard_map/ppermute | solution.py:98
  146.2 1.3 collective-permute-done.17
  147.5 2.9 %collective-permute-done.18 = f32[8,128]{1,0:T(8,128)S(1)} collective-permute-done((f32[8,128]{1,0:T(8,128)S(1)}, f32[8,128]{1,0:T(8,128)S(1)}, u32[]{:S(2)}, u32[]{:S(2)}) %collective-permute-start.18) | collective-permute-done | bytes 4128 | tf_op jit(solution)/shard_map/ppermute | solution.py:98
  151.0 1.7 %fusion.6 = f32[8,64]{1,0:T(8,128)} fusion(pred[1024,512]{1,0:T(32,128)(4,1)S(1)} %iota_compare_fusion, s32[]{:T(128)S(6)} %select_n.37, f32[8,8,128]{2,1,0:T(8,128)S(1)} %gather_fusion.1, pred[8]{0:T(512)(128)(4,1)S(1)} %compare_and_fusion, f32[8,64]{1,0:T(8,128)} %get-tuple-element.25, f32[8,64]{1,0:T(8,128)S(1)} %copy-done.11, ...), kind=kOutput, calls=%fused_computation.18 | convolution fusion | flops 6303232 | bytes 188932 | tf_op jit(solution)/shard_map/dot_general | solution.py:165
  (106 shorter events, 11.5 us)
Async XLA Ops:
  2.8 10.0 %collective-permute-start = (f32[2624]{0:T(1024)S(1)}, f32[2624]{0:T(1024)S(1)}, u32[]{:S(2)}, u32[]{:S(2)}) collective-permute-start(f32[2624]{0:T(1024)S(1)} %pad_maximum_fusion.3), channel_id=1, source_target_pairs={{0,1},{1,0},{2,3},{3,2},{4,5},{5,4},{6,7},{7,6},{8,9},{9,8},{10,11... | collective-permute-start | bytes 31496 | tf_op jit(solution)/shard_map/ppermute | solution.py:98
  4.8 9.1 %collective-permute-start.1 = (f32[2624]{0:T(1024)S(1)}, f32[2624]{0:T(1024)S(1)}, u32[]{:S(2)}, u32[]{:S(2)}) collective-permute-start(f32[2624]{0:T(1024)S(1)} %pad_maximum_fusion.3), channel_id=1, source_target_pairs={{0,2},{1,3},{2,0},{3,1},{4,6},{5,7},{6,4},{7,5},{8,10},{9,11},{10,... | collective-permute-start | bytes 31496 | tf_op jit(solution)/shard_map/ppermute | solution.py:98
  4.8 12.3 %collective-permute-start.2 = (f32[2624]{0:T(1024)S(1)}, f32[2624]{0:T(1024)S(1)}, u32[]{:S(2)}, u32[]{:S(2)}) collective-permute-start(f32[2624]{0:T(1024)S(1)} %pad_maximum_fusion.3), channel_id=1, source_target_pairs={{0,3},{1,2},{2,1},{3,0},{4,7},{5,6},{6,5},{7,4},{8,11},{9,10},{10,... | collective-permute-start | bytes 31496 | tf_op jit(solution)/shard_map/ppermute | solution.py:98
  7.8 9.4 %collective-permute-start.3 = (f32[2624]{0:T(1024)S(1)}, f32[2624]{0:T(1024)S(1)}, u32[]{:S(2)}, u32[]{:S(2)}) collective-permute-start(f32[2624]{0:T(1024)S(1)} %pad_maximum_fusion.3), channel_id=1, source_target_pairs={{0,4},{1,5},{2,6},{3,7},{4,0},{5,1},{6,2},{7,3},{8,12},{9,13},{10,... | collective-permute-start | bytes 31496 | tf_op jit(solution)/shard_map/ppermute | solution.py:98
  10.8 7.6 %collective-permute-start.4 = (f32[2624]{0:T(1024)S(1)}, f32[2624]{0:T(1024)S(1)}, u32[]{:S(2)}, u32[]{:S(2)}) collective-permute-start(f32[2624]{0:T(1024)S(1)} %pad_maximum_fusion.3), channel_id=1, source_target_pairs={{0,5},{1,4},{2,7},{3,6},{4,1},{5,0},{6,3},{7,2},{8,13},{9,12},{10,... | collective-permute-start | bytes 31496 | tf_op jit(solution)/shard_map/ppermute | solution.py:98
  12.8 5.6 %collective-permute-start.5 = (f32[2624]{0:T(1024)S(1)}, f32[2624]{0:T(1024)S(1)}, u32[]{:S(2)}, u32[]{:S(2)}) collective-permute-start(f32[2624]{0:T(1024)S(1)} %pad_maximum_fusion.3), channel_id=1, source_target_pairs={{0,6},{1,7},{2,4},{3,5},{4,2},{5,3},{6,0},{7,1},{8,14},{9,15},{10,... | collective-permute-start | bytes 31496 | tf_op jit(solution)/shard_map/ppermute | solution.py:98
  13.9 7.3 %collective-permute-start.6 = (f32[2624]{0:T(1024)S(1)}, f32[2624]{0:T(1024)S(1)}, u32[]{:S(2)}, u32[]{:S(2)}) collective-permute-start(f32[2624]{0:T(1024)S(1)} %pad_maximum_fusion.3), channel_id=1, source_target_pairs={{0,7},{1,6},{2,5},{3,4},{4,3},{5,2},{6,1},{7,0},{8,15},{9,14},{10,... | collective-permute-start | bytes 31496 | tf_op jit(solution)/shard_map/ppermute | solution.py:98
  24.1 32.5 %copy-start.3 = (f32[1,8,3072]{2,1,0:T(8,128)}, f32[1,8,3072]{2,1,0:T(8,128)S(1)}, u32[]{:S(2)}) copy-start(f32[1,8,3072]{2,1,0:T(8,128)S(1)} %maximum_bitcast_fusion.x_ref) | copy-start | bytes 294916
  24.1 10.9 %collective-permute-start.7 = (f32[1,8,3072]{2,1,0:T(8,128)S(1)}, f32[1,8,3072]{2,1,0:T(8,128)S(1)}, u32[]{:S(2)}, u32[]{:S(2)}) collective-permute-start(f32[1,8,3072]{2,1,0:T(8,128)S(1)} %maximum_bitcast_fusion.x_ref), channel_id=1, source_target_pairs={{0,128},{8,136},{16,144},{24,152},{32,160},{40,168},{48,176},{56,1... | collective-permute-start | bytes 294920 | tf_op jit(solution)/shard_map/ppermute | solution.py:157
  35.0 21.6 %copy-start.4 = (f32[1,8,3072]{2,1,0:T(8,128)}, f32[1,8,3072]{2,1,0:T(8,128)S(1)}, u32[]{:S(2)}) copy-start(f32[1,8,3072]{2,1,0:T(8,128)S(1)} %collective-permute-done.7.x_ref) | copy-start | bytes 294916
  35.0 8.9 %collective-permute-start.8 = (f32[2,8,3072]{2,1,0:T(8,128)S(1)}, f32[2,8,3072]{2,1,0:T(8,128)S(1)}, u32[]{:S(2)}, u32[]{:S(2)}) collective-permute-start(f32[2,8,3072]{2,1,0:T(8,128)S(1)} %pad_maximum_fusion.2), channel_id=1, source_target_pairs={{0,64},{8,72},{16,80},{24,88},{32,96},{40,104},{48,112},{56,120},{... | collective-permute-start | bytes 589832 | tf_op jit(solution)/shard_map/ppermute | solution.py:157
  44.0 9.4 %collective-permute-start.9 = (f32[4,8,3072]{2,1,0:T(8,128)S(1)}, f32[4,8,3072]{2,1,0:T(8,128)S(1)}, u32[]{:S(2)}, u32[]{:S(2)}) collective-permute-start(f32[4,8,3072]{2,1,0:T(8,128)S(1)} %pad_maximum_fusion.1), channel_id=1, source_target_pairs={{0,32},{8,40},{16,48},{24,56},{32,0},{40,8},{48,16},{56,24},{64,96... | collective-permute-start | bytes 1179656 | tf_op jit(solution)/shard_map/ppermute | solution.py:157
  53.5 17.9 %collective-permute-start.10 = (f32[8,8,3072]{2,1,0:T(8,128)S(1)}, f32[8,8,3072]{2,1,0:T(8,128)S(1)}, u32[]{:S(2)}, u32[]{:S(2)}) collective-permute-start(f32[8,8,3072]{2,1,0:T(8,128)S(1)} %pad_maximum_fusion), channel_id=1, source_target_pairs={{0,16},{8,24},{16,0},{24,8},{32,48},{40,56},{48,32},{56,40},{64,80... | collective-permute-start | bytes 2359304 | tf_op jit(solution)/shard_map/ppermute | solution.py:157
  71.4 21.4 %copy-start.1 = (f32[8,8,3072]{2,1,0:T(8,128)}, f32[8,8,3072]{2,1,0:T(8,128)S(1)}, u32[]{:S(2)}) copy-start(f32[8,8,3072]{2,1,0:T(8,128)S(1)} %collective-permute-done.10.x_ref) | copy-start | bytes 2359300
  72.4 33.3 %collective-permute-start.11 = (f32[16,8,3072]{2,1,0:T(8,128)}, f32[16,8,3072]{2,1,0:T(8,128)S(1)}, u32[]{:S(2)}, u32[]{:S(2)}) collective-permute-start(f32[16,8,3072]{2,1,0:T(8,128)} %constant_dynamic-update-slice_fusion), channel_id=1, source_target_pairs={{0,8},{8,0},{16,24},{24,16},{32,40},{40,32},{48,56},{56,48},{64,72... | collective-permute-start | bytes 4718600 | tf_op jit(solution)/shard_map/ppermute | solution.py:157
  85.5 45.2 %copy-start.13 = (f32[8,128]{1,0:T(8,128)S(1)}, f32[8,128]{1,0:T(8,128)}, u32[]{:S(2)}) copy-start(f32[8,128]{1,0:T(8,128)} %get-tuple-element.14) | copy-start | bytes 12292
  85.5 45.2 %copy-start.14 = (f32[8,128]{1,0:T(8,128)S(1)}, f32[8,128]{1,0:T(8,128)}, u32[]{:S(2)}) copy-start(f32[8,128]{1,0:T(8,128)} %get-tuple-element.15) | copy-start | bytes 12292
  85.5 45.2 %copy-start.15 = (f32[8,128]{1,0:T(8,128)S(1)}, f32[8,128]{1,0:T(8,128)}, u32[]{:S(2)}) copy-start(f32[8,128]{1,0:T(8,128)} %get-tuple-element.16) | copy-start | bytes 12292
  92.8 38.0 %copy-start.16 = (f32[8,128]{1,0:T(8,128)S(1)}, f32[8,128]{1,0:T(8,128)}, u32[]{:S(2)}) copy-start(f32[8,128]{1,0:T(8,128)} %get-tuple-element.17) | copy-start | bytes 12292
  92.8 58.1 %copy-start.7 = (f32[8,64]{1,0:T(8,128)S(1)}, f32[8,64]{1,0:T(8,128)}, u32[]{:S(2)}) copy-start(f32[8,64]{1,0:T(8,128)} %get-tuple-element.20) | copy-start | bytes 6148
  92.8 58.1 %copy-start.8 = (f32[8,64]{1,0:T(8,128)S(1)}, f32[8,64]{1,0:T(8,128)}, u32[]{:S(2)}) copy-start(f32[8,64]{1,0:T(8,128)} %get-tuple-element.21) | copy-start | bytes 6148
  92.8 58.1 %copy-start.9 = (f32[8,64]{1,0:T(8,128)S(1)}, f32[8,64]{1,0:T(8,128)}, u32[]{:S(2)}) copy-start(f32[8,64]{1,0:T(8,128)} %get-tuple-element.22) | copy-start | bytes 6148
  92.8 58.1 %copy-start.10 = (f32[8,64]{1,0:T(8,128)S(1)}, f32[8,64]{1,0:T(8,128)}, u32[]{:S(2)}) copy-start(f32[8,64]{1,0:T(8,128)} %get-tuple-element.23) | copy-start | bytes 6148
  105.6 25.2 %copy-start.17 = (f32[8,128]{1,0:T(8,128)S(1)}, f32[8,128]{1,0:T(8,128)}, u32[]{:S(2)}) copy-start(f32[8,128]{1,0:T(8,128)} %get-tuple-element.18) | copy-start | bytes 12292
  105.6 45.4 %copy-start.11 = (f32[8,64]{1,0:T(8,128)S(1)}, f32[8,64]{1,0:T(8,128)}, u32[]{:S(2)}) copy-start(f32[8,64]{1,0:T(8,128)} %get-tuple-element.24) | copy-start | bytes 6148
  131.5 11.2 %collective-permute-start.12 = (f32[8,128]{1,0:T(8,128)S(1)}, f32[8,128]{1,0:T(8,128)S(1)}, u32[]{:S(2)}, u32[]{:S(2)}) collective-permute-start(f32[8,128]{1,0:T(8,128)S(1)} %get-tuple-element.27), channel_id=1, source_target_pairs={{0,1},{1,0},{2,3},{3,2},{4,5},{5,4},{6,7},{7,6},{8,9},{9,8},{10,11... | collective-permute-start | bytes 12296 | tf_op jit(solution)/shard_map/ppermute | solution.py:98
  134.6 8.5 %collective-permute-start.13 = (f32[8,128]{1,0:T(8,128)S(1)}, f32[8,128]{1,0:T(8,128)S(1)}, u32[]{:S(2)}, u32[]{:S(2)}) collective-permute-start(f32[8,128]{1,0:T(8,128)S(1)} %get-tuple-element.27), channel_id=1, source_target_pairs={{0,2},{1,3},{2,0},{3,1},{4,6},{5,7},{6,4},{7,5},{8,10},{9,11},{10,... | collective-permute-start | bytes 12296 | tf_op jit(solution)/shard_map/ppermute | solution.py:98
  134.7 11.4 %collective-permute-start.14 = (f32[8,128]{1,0:T(8,128)S(1)}, f32[8,128]{1,0:T(8,128)S(1)}, u32[]{:S(2)}, u32[]{:S(2)}) collective-permute-start(f32[8,128]{1,0:T(8,128)S(1)} %get-tuple-element.27), channel_id=1, source_target_pairs={{0,3},{1,2},{2,1},{3,0},{4,7},{5,6},{6,5},{7,4},{8,11},{9,10},{10,... | collective-permute-start | bytes 12296 | tf_op jit(solution)/shard_map/ppermute | solution.py:98
  136.9 9.2 %collective-permute-start.15 = (f32[8,128]{1,0:T(8,128)S(1)}, f32[8,128]{1,0:T(8,128)S(1)}, u32[]{:S(2)}, u32[]{:S(2)}) collective-permute-start(f32[8,128]{1,0:T(8,128)S(1)} %get-tuple-element.27), channel_id=1, source_target_pairs={{0,4},{1,5},{2,6},{3,7},{4,0},{5,1},{6,2},{7,3},{8,12},{9,13},{10,... | collective-permute-start | bytes 12296 | tf_op jit(solution)/shard_map/ppermute | solution.py:98
  136.9 9.2 %collective-permute-start.16 = (f32[8,128]{1,0:T(8,128)S(1)}, f32[8,128]{1,0:T(8,128)S(1)}, u32[]{:S(2)}, u32[]{:S(2)}) collective-permute-start(f32[8,128]{1,0:T(8,128)S(1)} %get-tuple-element.27), channel_id=1, source_target_pairs={{0,5},{1,4},{2,7},{3,6},{4,1},{5,0},{6,3},{7,2},{8,13},{9,12},{10,... | collective-permute-start | bytes 12296 | tf_op jit(solution)/shard_map/ppermute | solution.py:98
  142.7 4.8 %collective-permute-start.17 = (f32[8,128]{1,0:T(8,128)S(1)}, f32[8,128]{1,0:T(8,128)S(1)}, u32[]{:S(2)}, u32[]{:S(2)}) collective-permute-start(f32[8,128]{1,0:T(8,128)S(1)} %get-tuple-element.27), channel_id=1, source_target_pairs={{0,6},{1,7},{2,4},{3,5},{4,2},{5,3},{6,0},{7,1},{8,14},{9,15},{10,... | collective-permute-start | bytes 12296 | tf_op jit(solution)/shard_map/ppermute | solution.py:98
  143.1 7.2 %collective-permute-start.18 = (f32[8,128]{1,0:T(8,128)S(1)}, f32[8,128]{1,0:T(8,128)S(1)}, u32[]{:S(2)}, u32[]{:S(2)}) collective-permute-start(f32[8,128]{1,0:T(8,128)S(1)} %get-tuple-element.27), channel_id=1, source_target_pairs={{0,7},{1,6},{2,5},{3,4},{4,3},{5,2},{6,1},{7,0},{8,15},{9,14},{10,... | collective-permute-start | bytes 12296 | tf_op jit(solution)/shard_map/ppermute | solution.py:98
  (7 other events, 113.0 us)

commit v2 on v0

--- a/solution.py
+++ b/solution.py
@@ -20,15 +20,15 @@
 
 
 def _accumulate(rows, rn, cols, w):
-    inner = jnp.dot(rows, cols, precision=lax.Precision.HIGHEST, preferred_element_type=jnp.float32)
-    cn = jnp.sum(cols * cols, axis=0, keepdims=True)
+    inner = lax.dot_general(
+        cols, rows, (((0,), (0,)), ((), ())),
+        precision=lax.Precision.HIGHEST, preferred_element_type=jnp.float32,
+    )
+    cn = jnp.sum(cols * cols, axis=0, keepdims=True).T
     square = rn + cn - 2.0 * inner
     dist = jnp.sqrt(jnp.maximum(square, 0.0))
     tile = (1.0 + SQRT_THREE * dist) * jnp.exp(-SQRT_THREE * dist)
-    return lax.dot_general(
-        w, tile, (((1,), (1,)), ((), ())),
-        precision=lax.Precision.HIGH, preferred_element_type=jnp.float32,
-    )
+    return jnp.dot(w, tile, precision=lax.Precision.HIGH, preferred_element_type=jnp.float32)
 
 
 def _piece_kernel(rl_ref, rd_ref, sl_ref, sd_ref, x_ref, ol_ref, od_ref, *, nb, nh):
@@ -39,8 +39,8 @@
 
     rows_l = rl_ref[...]
     rows_d = rd_ref[...]
-    rn_l = jnp.sum(rows_l * rows_l, axis=1, keepdims=True)
-    rn_d = jnp.sum(rows_d * rows_d, axis=1, keepdims=True)
+    rn_l = jnp.sum(rows_l * rows_l, axis=0, keepdims=True)
+    rn_d = jnp.sum(rows_d * rows_d, axis=0, keepdims=True)
     scale_l = sl_ref[...]
     scale_d = sd_ref[...]
 
@@ -74,8 +74,8 @@
         kern,
         grid=(n // per,),
         in_specs=[
-            full((rl, feats)),
-            full((rd, feats)),
+            full((feats, rl)),
+            full((feats, rd)),
             full((feats, 1)),
             full((feats, 1)),
             pl.BlockSpec((per, feats, width), lambda j: (j, 0, 0)),
@@ -87,7 +87,7 @@
         ],
         compiler_params=pltpu.CompilerParams(dimension_semantics=("arbitrary",)),
         interpret=interpret,
-    )(rows_low.T, rows_diff.T, inv_len_low[:, None], inv_len_diff[:, None], piece)
+    )(rows_low, rows_diff, inv_len_low[:, None], inv_len_diff[:, None], piece)
 
 
 def gather_bits(x, axis, size, bits):

time: 143 us -> 167 us (1.17)
  Pallas kernels: 54.2 us -> 78.4 us
    pallas_call x6, Pallas kernels: 54.2 us -> 78.4 us  [apply_piece(): pl.pallas_call(kern, grid=(n // per,), in_specs=[full((feats, rl)), full(...]
    unnamed x44 -> x43, local copies, waits for them, and re-layouts: 3.45 us -> 3.36 us
  transfers between devices with their start and end apart: 11 -> 11, of which waited for: 10 -> 10; matrix products, arithmetic and copies ran while one was open for 4% -> 3% of each run, Pallas kernels for 21% -> 25%
where the time goes in v2:
time: 167 us; the launch traced here: 166 us
  Pallas kernels  78.4 us (47%)
  waiting for transfers between devices  50.3 us (30%)
  starting transfers between devices  21.8 us (13%)
  local copies, waits for them, and re-layouts  6.91 us (4%)
  other arithmetic  5.98 us (4%)
  matrix products  2.13 us (1%)
    pallas_call x6, Pallas kernels, apply_piece(): pl.pallas_call(kern, grid=(n // per,), in_specs=[full((feats, rl)), full(...  78.4 us
    ppermute x5, waiting for transfers between devices, per_device(): other = lax.ppermute(buf, 'blk', [(i, i ^ mask) for i in range(blk_size)])  33.6 us
    ppermute x6, waiting for transfers between devices, gather_bits(): other = lax.ppermute(buf, axis, [(i, i ^ mask) for i in range(size)])  16.7 us
    ppermute x6, starting transfers between devices, gather_bits(): other = lax.ppermute(buf, axis, [(i, i ^ mask) for i in range(size)])  11.7 us
    ppermute x5, starting transfers between devices, per_device(): other = lax.ppermute(buf, 'blk', [(i, i ^ mask) for i in range(blk_size)])  10 us
    unnamed x43, local copies, waits for them, and re-layouts  3.36 us
  transfers between devices with their start and end apart: 11, of which 10 were waited for; matrix products, arithmetic and copies ran while one was open for 3% of the time, Pallas kernels for 25%

profile of v2, /device:TPU:16, one launch (start us, length us, event | category | flops | bytes accessed | tf_op | source)
XLA Modules:
  0.0 166.5 jit_solution(1263823956334817697)
XLA Ops:
  0.6 0.8 reshape.60
  2.0 0.7 pad_maximum_fusion.8
  2.8 3.1 %collective-permute-start = (f32[1,2624]{1,0:T(1,128)S(1)}, f32[1,2624]{1,0:T(1,128)S(1)}, u32[]{:S(2)}, u32[]{:S(2)}) collective-permute-start(f32[1,2624]{1,0:T(1,128)S(1)} %broadcast_in_dim.10), channel_id=1, source_target_pairs={{0,4},{1,5},{2,6},{3,7},{4,0},{5,1},{6,2},{7,3},{8,12},{9,13},{10,... | collective-permute-start | bytes 31496 | tf_op jit(solution)/shard_map/ppermute | solution.py:98
  5.9 2.2 %collective-permute-done = f32[1,2624]{1,0:T(1,128)S(1)} collective-permute-done((f32[1,2624]{1,0:T(1,128)S(1)}, f32[1,2624]{1,0:T(1,128)S(1)}, u32[]{:S(2)}, u32[]{:S(2)}) %collective-permute-start) | collective-permute-done | bytes 10528 | tf_op jit(solution)/shard_map/ppermute | solution.py:98
  8.1 2.1 %collective-permute-start.1 = (f32[2,2624]{1,0:T(2,128)S(1)}, f32[2,2624]{1,0:T(2,128)S(1)}, u32[]{:S(2)}, u32[]{:S(2)}) collective-permute-start(f32[2,2624]{1,0:T(2,128)S(1)} %pad_maximum_fusion.6), channel_id=1, source_target_pairs={{0,1},{1,0},{2,3},{3,2},{4,5},{5,4},{6,7},{7,6},{8,9},{9,8},{10,11... | collective-permute-start | bytes 62984 | tf_op jit(solution)/shard_map/ppermute | solution.py:98
  10.2 3.3 %collective-permute-done.1 = f32[2,2624]{1,0:T(2,128)S(1)} collective-permute-done((f32[2,2624]{1,0:T(2,128)S(1)}, f32[2,2624]{1,0:T(2,128)S(1)}, u32[]{:S(2)}, u32[]{:S(2)}) %collective-permute-start.1) | collective-permute-done | bytes 21024 | tf_op jit(solution)/shard_map/ppermute | solution.py:98
  13.5 1.6 collective-permute-start.2
  15.1 2.5 %collective-permute-done.2 = f32[4,2624]{1,0:T(4,128)S(1)} collective-permute-done((f32[4,2624]{1,0:T(4,128)S(1)}, f32[4,2624]{1,0:T(4,128)S(1)}, u32[]{:S(2)}, u32[]{:S(2)}) %collective-permute-start.2) | collective-permute-done | bytes 42016 | tf_op jit(solution)/shard_map/ppermute | solution.py:98
  18.2 0.7 fusion.1
  18.9 1.0 fusion
  20.0 7.3 %collective-permute-start.3 = (f32[1,8,3072]{2,1,0:T(8,128)S(1)}, f32[1,8,3072]{2,1,0:T(8,128)S(1)}, u32[]{:S(2)}, u32[]{:S(2)}) collective-permute-start(f32[1,8,3072]{2,1,0:T(8,128)S(1)} %maximum_bitcast_fusion.x_ref), channel_id=1, source_target_pairs={{0,128},{8,136},{16,144},{24,152},{32,160},{40,168},{48,176},{56,1... | collective-permute-start | bytes 294920 | tf_op jit(solution)/shard_map/ppermute | solution.py:164
  27.2 3.5 %collective-permute-done.3.x_ref = f32[1,8,3072]{2,1,0:T(8,128)S(1)} collective-permute-done((f32[1,8,3072]{2,1,0:T(8,128)S(1)}, f32[1,8,3072]{2,1,0:T(8,128)S(1)}, u32[]{:S(2)}, u32[]{:S(2)}) %collective-permute-start.3) | collective-permute-done | bytes 98336 | tf_op jit(solution)/shard_map/ppermute | solution.py:164
  30.8 1.3 collective-permute-start.4
  32.0 7.7 %collective-permute-done.4.x_ref = f32[2,8,3072]{2,1,0:T(8,128)S(1)} collective-permute-done((f32[2,8,3072]{2,1,0:T(8,128)S(1)}, f32[2,8,3072]{2,1,0:T(8,128)S(1)}, u32[]{:S(2)}, u32[]{:S(2)}) %collective-permute-start.4) | collective-permute-done | bytes 196640 | tf_op jit(solution)/shard_map/ppermute | solution.py:164
  40.5 8.8 %collective-permute-done.5.x_ref = f32[4,8,3072]{2,1,0:T(8,128)S(1)} collective-permute-done((f32[4,8,3072]{2,1,0:T(8,128)S(1)}, f32[4,8,3072]{2,1,0:T(8,128)S(1)}, u32[]{:S(2)}, u32[]{:S(2)}) %collective-permute-start.5) | collective-permute-done | bytes 393248 | tf_op jit(solution)/shard_map/ppermute | solution.py:164
  49.4 1.4 collective-permute-start.6
  52.1 0.8 constant_dynamic-update-slice_fusion.1
  52.9 13.6 %collective-permute-done.6.x_ref = f32[8,8,3072]{2,1,0:T(8,128)S(1)} collective-permute-done((f32[8,8,3072]{2,1,0:T(8,128)S(1)}, f32[8,8,3072]{2,1,0:T(8,128)S(1)}, u32[]{:S(2)}, u32[]{:S(2)}) %collective-permute-start.6) | collective-permute-done | bytes 786464 | tf_op jit(solution)/shard_map/ppermute | solution.py:164
  66.5 1.0 constant_dynamic-update-slice_fusion
  70.2 3.3 %shard_map.77 = (f32[8,128]{1,0:T(8,128)}, f32[8,64]{1,0:T(8,128)}) custom-call(f32[8,128]{1,0:T(8,128)} %broadcast_multiply_fusion.rl_ref, f32[8,64]{1,0:T(8,128)} %dynamic-slice_multiply_fusion.rd_ref, f32[8,1]{1,0:T(8,128)} %copy.40.sl_ref, f32[8,1]{1,0:T(8,128)} %copy.41.sd_ref, f32[1,8,3072]{2,1,0:T(8,128)} %copy-done.3), custom_call_target="tpu_custom_call" | custom-call | tf_op jit(solution)/shard_map/pallas_call | solution.py:73
  73.5 3.3 %shard_map.78 = (f32[8,128]{1,0:T(8,128)}, f32[8,64]{1,0:T(8,128)}) custom-call(f32[8,128]{1,0:T(8,128)} %broadcast_multiply_fusion.rl_ref, f32[8,64]{1,0:T(8,128)} %dynamic-slice_multiply_fusion.rd_ref, f32[8,1]{1,0:T(8,128)} %copy.40.sl_ref, f32[8,1]{1,0:T(8,128)} %copy.41.sd_ref, f32[1,8,3072]{2,1,0:T(8,128)} %copy-done.4), custom_call_target="tpu_custom_call" | custom-call | tf_op jit(solution)/shard_map/pallas_call | solution.py:73
  76.9 5.9 %shard_map.79 = (f32[8,128]{1,0:T(8,128)}, f32[8,64]{1,0:T(8,128)}) custom-call(f32[8,128]{1,0:T(8,128)} %broadcast_multiply_fusion.rl_ref, f32[8,64]{1,0:T(8,128)} %dynamic-slice_multiply_fusion.rd_ref, f32[8,1]{1,0:T(8,128)} %copy.40.sl_ref, f32[8,1]{1,0:T(8,128)} %copy.41.sd_ref, f32[2,8,3072]{2,1,0:T(8,128)} %copy-done.2), custom_call_target="tpu_custom_call" | custom-call | tf_op jit(solution)/shard_map/pallas_call | solution.py:73
  82.8 10.3 %shard_map.80 = (f32[8,128]{1,0:T(8,128)}, f32[8,64]{1,0:T(8,128)}) custom-call(f32[8,128]{1,0:T(8,128)} %broadcast_multiply_fusion.rl_ref, f32[8,64]{1,0:T(8,128)} %dynamic-slice_multiply_fusion.rd_ref, f32[8,1]{1,0:T(8,128)} %copy.40.sl_ref, f32[8,1]{1,0:T(8,128)} %copy.41.sd_ref, f32[4,8,3072]{2,1,0:T(8,128)} %copy-done), custom_call_target="tpu_custom_call" | custom-call | tf_op jit(solution)/shard_map/pallas_call | solution.py:73
  93.2 19.0 %shard_map.81 = (f32[8,128]{1,0:T(8,128)}, f32[8,64]{1,0:T(8,128)}) custom-call(f32[8,128]{1,0:T(8,128)} %broadcast_multiply_fusion.rl_ref, f32[8,64]{1,0:T(8,128)} %dynamic-slice_multiply_fusion.rd_ref, f32[8,1]{1,0:T(8,128)} %copy.40.sl_ref, f32[8,1]{1,0:T(8,128)} %copy.41.sd_ref, f32[8,8,3072]{2,1,0:T(8,128)} %copy-done.1), custom_call_target="tpu_custom_call" | custom-call | tf_op jit(solution)/shard_map/pallas_call | solution.py:73
  112.3 1.2 copy-done.5
  113.4 36.5 %shard_map.82 = (f32[8,128]{1,0:T(8,128)}, f32[8,64]{1,0:T(8,128)}) custom-call(f32[8,128]{1,0:T(8,128)} %broadcast_multiply_fusion.rl_ref, f32[8,64]{1,0:T(8,128)} %dynamic-slice_multiply_fusion.rd_ref, f32[8,1]{1,0:T(8,128)} %copy.40.sl_ref, f32[8,1]{1,0:T(8,128)} %copy.41.sd_ref, f32[16,8,3072]{2,1,0:T(8,128)} %copy-done.5), custom_call_target="tpu_custom_call" | custom-call | tf_op jit(solution)/shard_map/pallas_call | solution.py:73
  150.6 3.0 %collective-permute-start.8 = (f32[1,8,128]{2,1,0:T(8,128)S(1)}, f32[1,8,128]{2,1,0:T(8,128)S(1)}, u32[]{:S(2)}, u32[]{:S(2)}) collective-permute-start(f32[1,8,128]{2,1,0:T(8,128)S(1)} %bitcast.43), channel_id=1, source_target_pairs={{0,4},{1,5},{2,6},{3,7},{4,0},{5,1},{6,2},{7,3},{8,12},{9,13},{10,... | collective-permute-start | bytes 12296 | tf_op jit(solution)/shard_map/ppermute | solution.py:98
  153.6 2.1 %collective-permute-done.8 = f32[1,8,128]{2,1,0:T(8,128)S(1)} collective-permute-done((f32[1,8,128]{2,1,0:T(8,128)S(1)}, f32[1,8,128]{2,1,0:T(8,128)S(1)}, u32[]{:S(2)}, u32[]{:S(2)}) %collective-permute-start.8) | collective-permute-done | bytes 4128 | tf_op jit(solution)/shard_map/ppermute | solution.py:98
  156.1 4.8 %collective-permute-done.9 = f32[2,8,128]{2,1,0:T(8,128)S(1)} collective-permute-done((f32[2,8,128]{2,1,0:T(8,128)S(1)}, f32[2,8,128]{2,1,0:T(8,128)S(1)}, u32[]{:S(2)}, u32[]{:S(2)}) %collective-permute-start.9) | collective-permute-done | bytes 8224 | tf_op jit(solution)/shard_map/ppermute | solution.py:98
  160.9 1.6 collective-permute-start.10
  162.8 1.9 %collective-permute-done.10 = f32[4,8,128]{2,1,0:T(8,128)S(1)} collective-permute-done((f32[4,8,128]{2,1,0:T(8,128)S(1)}, f32[4,8,128]{2,1,0:T(8,128)S(1)}, u32[]{:S(2)}, u32[]{:S(2)}) %collective-permute-start.10) | collective-permute-done | bytes 16416 | tf_op jit(solution)/shard_map/ppermute | solution.py:98
  165.2 1.3 add_add_fusion
  (83 shorter events, 8.0 us)
Async XLA Ops:
  2.8 5.3 %collective-permute-start = (f32[1,2624]{1,0:T(1,128)S(1)}, f32[1,2624]{1,0:T(1,128)S(1)}, u32[]{:S(2)}, u32[]{:S(2)}) collective-permute-start(f32[1,2624]{1,0:T(1,128)S(1)} %broadcast_in_dim.10), channel_id=1, source_target_pairs={{0,4},{1,5},{2,6},{3,7},{4,0},{5,1},{6,2},{7,3},{8,12},{9,13},{10,... | collective-permute-start | bytes 31496 | tf_op jit(solution)/shard_map/ppermute | solution.py:98
  8.1 5.4 %collective-permute-start.1 = (f32[2,2624]{1,0:T(2,128)S(1)}, f32[2,2624]{1,0:T(2,128)S(1)}, u32[]{:S(2)}, u32[]{:S(2)}) collective-permute-start(f32[2,2624]{1,0:T(2,128)S(1)} %pad_maximum_fusion.6), channel_id=1, source_target_pairs={{0,1},{1,0},{2,3},{3,2},{4,5},{5,4},{6,7},{7,6},{8,9},{9,8},{10,11... | collective-permute-start | bytes 62984 | tf_op jit(solution)/shard_map/ppermute | solution.py:98
  13.5 4.1 %collective-permute-start.2 = (f32[4,2624]{1,0:T(4,128)S(1)}, f32[4,2624]{1,0:T(4,128)S(1)}, u32[]{:S(2)}, u32[]{:S(2)}) collective-permute-start(f32[4,2624]{1,0:T(4,128)S(1)} %pad_maximum_fusion.4), channel_id=1, source_target_pairs={{0,2},{1,3},{2,0},{3,1},{4,6},{5,7},{6,4},{7,5},{8,10},{9,11},{10,... | collective-permute-start | bytes 125960 | tf_op jit(solution)/shard_map/ppermute | solution.py:98
  20.0 31.5 %copy-start.3 = (f32[1,8,3072]{2,1,0:T(8,128)}, f32[1,8,3072]{2,1,0:T(8,128)S(1)}, u32[]{:S(2)}) copy-start(f32[1,8,3072]{2,1,0:T(8,128)S(1)} %maximum_bitcast_fusion.x_ref) | copy-start | bytes 294916
  20.0 10.8 %collective-permute-start.3 = (f32[1,8,3072]{2,1,0:T(8,128)S(1)}, f32[1,8,3072]{2,1,0:T(8,128)S(1)}, u32[]{:S(2)}, u32[]{:S(2)}) collective-permute-start(f32[1,8,3072]{2,1,0:T(8,128)S(1)} %maximum_bitcast_fusion.x_ref), channel_id=1, source_target_pairs={{0,128},{8,136},{16,144},{24,152},{32,160},{40,168},{48,176},{56,1... | collective-permute-start | bytes 294920 | tf_op jit(solution)/shard_map/ppermute | solution.py:164
  30.7 20.7 %copy-start.4 = (f32[1,8,3072]{2,1,0:T(8,128)}, f32[1,8,3072]{2,1,0:T(8,128)S(1)}, u32[]{:S(2)}) copy-start(f32[1,8,3072]{2,1,0:T(8,128)S(1)} %collective-permute-done.3.x_ref) | copy-start | bytes 294916
  30.8 9.0 %collective-permute-start.4 = (f32[2,8,3072]{2,1,0:T(8,128)S(1)}, f32[2,8,3072]{2,1,0:T(8,128)S(1)}, u32[]{:S(2)}, u32[]{:S(2)}) collective-permute-start(f32[2,8,3072]{2,1,0:T(8,128)S(1)} %pad_maximum_fusion.2), channel_id=1, source_target_pairs={{0,64},{8,72},{16,80},{24,88},{32,96},{40,104},{48,112},{56,120},{... | collective-permute-start | bytes 589832 | tf_op jit(solution)/shard_map/ppermute | solution.py:164
  39.8 12.4 %copy-start.2 = (f32[2,8,3072]{2,1,0:T(8,128)}, f32[2,8,3072]{2,1,0:T(8,128)S(1)}, u32[]{:S(2)}) copy-start(f32[2,8,3072]{2,1,0:T(8,128)S(1)} %collective-permute-done.4.x_ref) | copy-start | bytes 589828
  39.8 9.5 %collective-permute-start.5 = (f32[4,8,3072]{2,1,0:T(8,128)S(1)}, f32[4,8,3072]{2,1,0:T(8,128)S(1)}, u32[]{:S(2)}, u32[]{:S(2)}) collective-permute-start(f32[4,8,3072]{2,1,0:T(8,128)S(1)} %pad_maximum_fusion.1), channel_id=1, source_target_pairs={{0,32},{8,40},{16,48},{24,56},{32,0},{40,8},{48,16},{56,24},{64,96... | collective-permute-start | bytes 1179656 | tf_op jit(solution)/shard_map/ppermute | solution.py:164
  49.3 18.2 %copy-start = (f32[4,8,3072]{2,1,0:T(8,128)}, f32[4,8,3072]{2,1,0:T(8,128)S(1)}, u32[]{:S(2)}) copy-start(f32[4,8,3072]{2,1,0:T(8,128)S(1)} %collective-permute-done.5.x_ref) | copy-start | bytes 1179652
  49.4 18.1 %copy-start.18 = (f32[8]{0:T(128)S(1)}, f32[8]{0:T(128)}, u32[]{:S(2)}) copy-start(f32[8]{0:T(128)} %param.10) | copy-start | bytes 100
  49.4 18.8 %copy-start.19 = (f32[8]{0:T(128)S(1)}, f32[8]{0:T(128)}, u32[]{:S(2)}) copy-start(f32[8]{0:T(128)} %param.11) | copy-start | bytes 100
  49.4 19.5 %copy-start.7 = (f32[8,128]{1,0:T(8,128)S(1)}, f32[8,128]{1,0:T(8,128)}, u32[]{:S(2)}) copy-start(f32[8,128]{1,0:T(8,128)} %param.6) | copy-start | bytes 12292
  49.4 17.1 %collective-permute-start.6 = (f32[8,8,3072]{2,1,0:T(8,128)S(1)}, f32[8,8,3072]{2,1,0:T(8,128)S(1)}, u32[]{:S(2)}, u32[]{:S(2)}) collective-permute-start(f32[8,8,3072]{2,1,0:T(8,128)S(1)} %pad_maximum_fusion), channel_id=1, source_target_pairs={{0,16},{8,24},{16,0},{24,8},{32,48},{40,56},{48,32},{56,40},{64,80... | collective-permute-start | bytes 2359304 | tf_op jit(solution)/shard_map/ppermute | solution.py:164
  66.5 26.6 %copy-start.1 = (f32[8,8,3072]{2,1,0:T(8,128)}, f32[8,8,3072]{2,1,0:T(8,128)S(1)}, u32[]{:S(2)}) copy-start(f32[8,8,3072]{2,1,0:T(8,128)S(1)} %collective-permute-done.6.x_ref) | copy-start | bytes 2359300
  67.5 44.7 %collective-permute-start.7 = (f32[16,8,3072]{2,1,0:T(8,128)}, f32[16,8,3072]{2,1,0:T(8,128)S(1)}, u32[]{:S(2)}, u32[]{:S(2)}) collective-permute-start(f32[16,8,3072]{2,1,0:T(8,128)} %constant_dynamic-update-slice_fusion), channel_id=1, source_target_pairs={{0,8},{8,0},{16,24},{24,16},{32,40},{40,32},{48,56},{56,48},{64,72... | collective-permute-start | bytes 4718600 | tf_op jit(solution)/shard_map/ppermute | solution.py:164
  73.5 76.3 %copy-start.8 = (f32[8,128]{1,0:T(8,128)S(1)}, f32[8,128]{1,0:T(8,128)}, u32[]{:S(2)}) copy-start(f32[8,128]{1,0:T(8,128)} %get-tuple-element.14) | copy-start | bytes 12292
  76.9 73.0 %copy-start.9 = (f32[8,128]{1,0:T(8,128)S(1)}, f32[8,128]{1,0:T(8,128)}, u32[]{:S(2)}) copy-start(f32[8,128]{1,0:T(8,128)} %get-tuple-element.15) | copy-start | bytes 12292
  82.8 67.1 %copy-start.10 = (f32[8,128]{1,0:T(8,128)S(1)}, f32[8,128]{1,0:T(8,128)}, u32[]{:S(2)}) copy-start(f32[8,128]{1,0:T(8,128)} %get-tuple-element.16) | copy-start | bytes 12292
  93.1 56.7 %copy-start.11 = (f32[8,128]{1,0:T(8,128)S(1)}, f32[8,128]{1,0:T(8,128)}, u32[]{:S(2)}) copy-start(f32[8,128]{1,0:T(8,128)} %get-tuple-element.17) | copy-start | bytes 12292
  93.1 72.0 %copy-start.13 = (f32[8,64]{1,0:T(8,128)S(1)}, f32[8,64]{1,0:T(8,128)}, u32[]{:S(2)}) copy-start(f32[8,64]{1,0:T(8,128)} %get-tuple-element.20) | copy-start | bytes 6148
  93.2 72.0 %copy-start.14 = (f32[8,64]{1,0:T(8,128)S(1)}, f32[8,64]{1,0:T(8,128)}, u32[]{:S(2)}) copy-start(f32[8,64]{1,0:T(8,128)} %get-tuple-element.21) | copy-start | bytes 6148
  93.2 72.0 %copy-start.15 = (f32[8,64]{1,0:T(8,128)S(1)}, f32[8,64]{1,0:T(8,128)}, u32[]{:S(2)}) copy-start(f32[8,64]{1,0:T(8,128)} %get-tuple-element.22) | copy-start | bytes 6148
  93.2 72.0 %copy-start.16 = (f32[8,64]{1,0:T(8,128)S(1)}, f32[8,64]{1,0:T(8,128)}, u32[]{:S(2)}) copy-start(f32[8,64]{1,0:T(8,128)} %get-tuple-element.23) | copy-start | bytes 6148
  112.2 37.7 %copy-start.12 = (f32[8,128]{1,0:T(8,128)S(1)}, f32[8,128]{1,0:T(8,128)}, u32[]{:S(2)}) copy-start(f32[8,128]{1,0:T(8,128)} %get-tuple-element.18) | copy-start | bytes 12292
  112.2 52.9 %copy-start.17 = (f32[8,64]{1,0:T(8,128)S(1)}, f32[8,64]{1,0:T(8,128)}, u32[]{:S(2)}) copy-start(f32[8,64]{1,0:T(8,128)} %get-tuple-element.24) | copy-start | bytes 6148
  112.2 1.2 copy-start.5
  150.6 15.9 %copy-start.6 = (f32[8,128]{1,0:T(8,128)}, f32[8,128]{1,0:T(8,128)S(1)}, u32[]{:S(2)}) copy-start(f32[8,128]{1,0:T(8,128)S(1)} %add_add_fusion.1) | copy-start | bytes 12292
  150.6 5.1 %collective-permute-start.8 = (f32[1,8,128]{2,1,0:T(8,128)S(1)}, f32[1,8,128]{2,1,0:T(8,128)S(1)}, u32[]{:S(2)}, u32[]{:S(2)}) collective-permute-start(f32[1,8,128]{2,1,0:T(8,128)S(1)} %bitcast.43), channel_id=1, source_target_pairs={{0,4},{1,5},{2,6},{3,7},{4,0},{5,1},{6,2},{7,3},{8,12},{9,13},{10,... | collective-permute-start | bytes 12296 | tf_op jit(solution)/shard_map/ppermute | solution.py:98
  155.7 5.2 %collective-permute-start.9 = (f32[2,8,128]{2,1,0:T(8,128)S(1)}, f32[2,8,128]{2,1,0:T(8,128)S(1)}, u32[]{:S(2)}, u32[]{:S(2)}) collective-permute-start(f32[2,8,128]{2,1,0:T(8,128)S(1)} %pad_maximum_fusion.9), channel_id=1, source_target_pairs={{0,1},{1,0},{2,3},{3,2},{4,5},{5,4},{6,7},{7,6},{8,9},{9,8},{10,11... | collective-permute-start | bytes 24584 | tf_op jit(solution)/shard_map/ppermute | solution.py:98
  160.9 3.8 %collective-permute-start.10 = (f32[4,8,128]{2,1,0:T(8,128)S(1)}, f32[4,8,128]{2,1,0:T(8,128)S(1)}, u32[]{:S(2)}, u32[]{:S(2)}) collective-permute-start(f32[4,8,128]{2,1,0:T(8,128)S(1)} %pad_maximum_fusion.7), channel_id=1, source_target_pairs={{0,2},{1,3},{2,0},{3,1},{4,6},{5,7},{6,4},{7,5},{8,10},{9,11},{10,... | collective-permute-start | bytes 49160 | tf_op jit(solution)/shard_map/ppermute | solution.py:98

commit v3 on v0

--- a/solution.py
+++ b/solution.py
@@ -16,7 +16,7 @@
 BLK_BITS = (4, 3, 2, 1, 0)
 
 
-COL_SUB = 512
+COL_SUB = 256
 
 
 def _accumulate(rows, rn, cols, w):
@@ -24,7 +24,8 @@
     cn = jnp.sum(cols * cols, axis=0, keepdims=True)
     square = rn + cn - 2.0 * inner
     dist = jnp.sqrt(jnp.maximum(square, 0.0))
-    tile = (1.0 + SQRT_THREE * dist) * jnp.exp(-SQRT_THREE * dist)
+    scaled = SQRT_THREE * dist
+    tile = (1.0 + scaled) * jnp.exp(-scaled)
     return lax.dot_general(
         w, tile, (((1,), (1,)), ((), ())),
         precision=lax.Precision.HIGH, preferred_element_type=jnp.float32,

time: 143 us -> 157 us (1.098)
  Pallas kernels: 54.2 us -> 68.4 us
    pallas_call x6, Pallas kernels: 54.2 us -> 68.4 us  [apply_piece(): pl.pallas_call(kern, grid=(n // per,), in_specs=[full((rl, feats)), full(...]
  transfers between devices with their start and end apart: 11 -> 11, of which waited for: 10 -> 10; matrix products, arithmetic and copies ran while one was open for 4% -> 4% of each run, Pallas kernels for 21% -> 24%
where the time goes in v3:
time: 157 us
  Pallas kernels  68.4 us (44%)
  waiting for transfers between devices  50.3 us (32%)
  starting transfers between devices  21.8 us (14%)
  local copies, waits for them, and re-layouts  7.79 us (5%)
  other arithmetic  5.33 us (3%)
  matrix products  2.13 us (1%)
    pallas_call x6, Pallas kernels, apply_piece(): pl.pallas_call(kern, grid=(n // per,), in_specs=[full((rl, feats)), full(...  68.4 us
    ppermute x5, waiting for transfers between devices, per_device(): other = lax.ppermute(buf, 'blk', [(i, i ^ mask) for i in range(blk_size)])  33.6 us
    ppermute x6, waiting for transfers between devices, gather_bits(): other = lax.ppermute(buf, axis, [(i, i ^ mask) for i in range(size)])  16.7 us
    ppermute x6, starting transfers between devices, gather_bits(): other = lax.ppermute(buf, axis, [(i, i ^ mask) for i in range(size)])  11.8 us
    ppermute x5, starting transfers between devices, per_device(): other = lax.ppermute(buf, 'blk', [(i, i ^ mask) for i in range(blk_size)])  10 us
    unnamed x44, local copies, waits for them, and re-layouts  3.45 us
  transfers between devices with their start and end apart: 11, of which 10 were waited for; matrix products, arithmetic and copies ran while one was open for 4% of the time, Pallas kernels for 24%

profile of v3, /device:TPU:16, one launch (start us, length us, event | category | flops | bytes accessed | tf_op | source)
XLA Modules:
  0.0 156.7 jit_solution(16297854864573212059)
XLA Ops:
  0.6 0.8 reshape.60
  2.8 3.1 %collective-permute-start = (f32[1,2624]{1,0:T(1,128)S(1)}, f32[1,2624]{1,0:T(1,128)S(1)}, u32[]{:S(2)}, u32[]{:S(2)}) collective-permute-start(f32[1,2624]{1,0:T(1,128)S(1)} %broadcast_in_dim.10), channel_id=1, source_target_pairs={{0,4},{1,5},{2,6},{3,7},{4,0},{5,1},{6,2},{7,3},{8,12},{9,13},{10,... | collective-permute-start | bytes 31496 | tf_op jit(solution)/shard_map/ppermute | solution.py:99
  5.9 2.2 %collective-permute-done = f32[1,2624]{1,0:T(1,128)S(1)} collective-permute-done((f32[1,2624]{1,0:T(1,128)S(1)}, f32[1,2624]{1,0:T(1,128)S(1)}, u32[]{:S(2)}, u32[]{:S(2)}) %collective-permute-start) | collective-permute-done | bytes 10528 | tf_op jit(solution)/shard_map/ppermute | solution.py:99
  8.1 2.1 %collective-permute-start.1 = (f32[2,2624]{1,0:T(2,128)S(1)}, f32[2,2624]{1,0:T(2,128)S(1)}, u32[]{:S(2)}, u32[]{:S(2)}) collective-permute-start(f32[2,2624]{1,0:T(2,128)S(1)} %pad_maximum_fusion.6), channel_id=1, source_target_pairs={{0,1},{1,0},{2,3},{3,2},{4,5},{5,4},{6,7},{7,6},{8,9},{9,8},{10,11... | collective-permute-start | bytes 62984 | tf_op jit(solution)/shard_map/ppermute | solution.py:99
  10.2 3.3 %collective-permute-done.1 = f32[2,2624]{1,0:T(2,128)S(1)} collective-permute-done((f32[2,2624]{1,0:T(2,128)S(1)}, f32[2,2624]{1,0:T(2,128)S(1)}, u32[]{:S(2)}, u32[]{:S(2)}) %collective-permute-start.1) | collective-permute-done | bytes 21024 | tf_op jit(solution)/shard_map/ppermute | solution.py:99
  13.5 1.6 %collective-permute-start.2 = (f32[4,2624]{1,0:T(4,128)S(1)}, f32[4,2624]{1,0:T(4,128)S(1)}, u32[]{:S(2)}, u32[]{:S(2)}) collective-permute-start(f32[4,2624]{1,0:T(4,128)S(1)} %pad_maximum_fusion.4), channel_id=1, source_target_pairs={{0,2},{1,3},{2,0},{3,1},{4,6},{5,7},{6,4},{7,5},{8,10},{9,11},{10,... | collective-permute-start | bytes 125960 | tf_op jit(solution)/shard_map/ppermute | solution.py:99
  15.1 2.5 %collective-permute-done.2 = f32[4,2624]{1,0:T(4,128)S(1)} collective-permute-done((f32[4,2624]{1,0:T(4,128)S(1)}, f32[4,2624]{1,0:T(4,128)S(1)}, u32[]{:S(2)}, u32[]{:S(2)}) %collective-permute-start.2) | collective-permute-done | bytes 42016 | tf_op jit(solution)/shard_map/ppermute | solution.py:99
  18.2 0.7 fusion.1
  18.9 1.0 fusion
  20.0 7.3 %collective-permute-start.3 = (f32[1,8,3072]{2,1,0:T(8,128)S(1)}, f32[1,8,3072]{2,1,0:T(8,128)S(1)}, u32[]{:S(2)}, u32[]{:S(2)}) collective-permute-start(f32[1,8,3072]{2,1,0:T(8,128)S(1)} %maximum_bitcast_fusion.x_ref), channel_id=1, source_target_pairs={{0,128},{8,136},{16,144},{24,152},{32,160},{40,168},{48,176},{56,1... | collective-permute-start | bytes 294920 | tf_op jit(solution)/shard_map/ppermute | solution.py:165
  27.2 3.5 %collective-permute-done.3.x_ref = f32[1,8,3072]{2,1,0:T(8,128)S(1)} collective-permute-done((f32[1,8,3072]{2,1,0:T(8,128)S(1)}, f32[1,8,3072]{2,1,0:T(8,128)S(1)}, u32[]{:S(2)}, u32[]{:S(2)}) %collective-permute-start.3) | collective-permute-done | bytes 98336 | tf_op jit(solution)/shard_map/ppermute | solution.py:165
  30.8 1.3 collective-permute-start.4
  32.0 7.7 %collective-permute-done.4.x_ref = f32[2,8,3072]{2,1,0:T(8,128)S(1)} collective-permute-done((f32[2,8,3072]{2,1,0:T(8,128)S(1)}, f32[2,8,3072]{2,1,0:T(8,128)S(1)}, u32[]{:S(2)}, u32[]{:S(2)}) %collective-permute-start.4) | collective-permute-done | bytes 196640 | tf_op jit(solution)/shard_map/ppermute | solution.py:165
  40.5 8.8 %collective-permute-done.5.x_ref = f32[4,8,3072]{2,1,0:T(8,128)S(1)} collective-permute-done((f32[4,8,3072]{2,1,0:T(8,128)S(1)}, f32[4,8,3072]{2,1,0:T(8,128)S(1)}, u32[]{:S(2)}, u32[]{:S(2)}) %collective-permute-start.5) | collective-permute-done | bytes 393248 | tf_op jit(solution)/shard_map/ppermute | solution.py:165
  49.4 1.4 collective-permute-start.6
  52.1 0.8 constant_dynamic-update-slice_fusion.1
  52.9 13.6 %collective-permute-done.6.x_ref = f32[8,8,3072]{2,1,0:T(8,128)S(1)} collective-permute-done((f32[8,8,3072]{2,1,0:T(8,128)S(1)}, f32[8,8,3072]{2,1,0:T(8,128)S(1)}, u32[]{:S(2)}, u32[]{:S(2)}) %collective-permute-start.6) | collective-permute-done | bytes 786464 | tf_op jit(solution)/shard_map/ppermute | solution.py:165
  66.5 1.0 constant_dynamic-update-slice_fusion
  67.6 0.7 copy.62
  70.4 3.4 %shard_map.77 = (f32[8,128]{1,0:T(8,128)}, f32[8,64]{1,0:T(8,128)}) custom-call(f32[128,8]{1,0:T(8,128)} %bitcast.40, f32[64,8]{1,0:T(8,128)} %multiply_bitcast_fusion.rd_ref, f32[8,1]{1,0:T(8,128)} %copy.68.sl_ref, f32[8,1]{1,0:T(8,128)} %copy.69.sd_ref, f32[1,8,3072]{2,1,0:T(8,128)} %copy-done.3), custom_call_target="tpu_custom_call" | custom-call | tf_op jit(solution)/shard_map/pallas_call | solution.py:74
  73.8 3.4 %shard_map.78 = (f32[8,128]{1,0:T(8,128)}, f32[8,64]{1,0:T(8,128)}) custom-call(f32[128,8]{1,0:T(8,128)} %bitcast.41, f32[64,8]{1,0:T(8,128)} %multiply_bitcast_fusion.rd_ref, f32[8,1]{1,0:T(8,128)} %copy.68.sl_ref, f32[8,1]{1,0:T(8,128)} %copy.69.sd_ref, f32[1,8,3072]{2,1,0:T(8,128)} %copy-done.4), custom_call_target="tpu_custom_call" | custom-call | tf_op jit(solution)/shard_map/pallas_call | solution.py:74
  77.2 5.3 %shard_map.79 = (f32[8,128]{1,0:T(8,128)}, f32[8,64]{1,0:T(8,128)}) custom-call(f32[128,8]{1,0:T(8,128)} %bitcast.42, f32[64,8]{1,0:T(8,128)} %multiply_bitcast_fusion.rd_ref, f32[8,1]{1,0:T(8,128)} %copy.68.sl_ref, f32[8,1]{1,0:T(8,128)} %copy.69.sd_ref, f32[2,8,3072]{2,1,0:T(8,128)} %copy-done.2), custom_call_target="tpu_custom_call" | custom-call | tf_op jit(solution)/shard_map/pallas_call | solution.py:74
  82.6 9.0 %shard_map.80 = (f32[8,128]{1,0:T(8,128)}, f32[8,64]{1,0:T(8,128)}) custom-call(f32[128,8]{1,0:T(8,128)} %bitcast.43, f32[64,8]{1,0:T(8,128)} %multiply_bitcast_fusion.rd_ref, f32[8,1]{1,0:T(8,128)} %copy.68.sl_ref, f32[8,1]{1,0:T(8,128)} %copy.69.sd_ref, f32[4,8,3072]{2,1,0:T(8,128)} %copy-done), custom_call_target="tpu_custom_call" | custom-call | tf_op jit(solution)/shard_map/pallas_call | solution.py:74
  91.6 16.3 %shard_map.81 = (f32[8,128]{1,0:T(8,128)}, f32[8,64]{1,0:T(8,128)}) custom-call(f32[128,8]{1,0:T(8,128)} %bitcast.44, f32[64,8]{1,0:T(8,128)} %multiply_bitcast_fusion.rd_ref, f32[8,1]{1,0:T(8,128)} %copy.68.sl_ref, f32[8,1]{1,0:T(8,128)} %copy.69.sd_ref, f32[8,8,3072]{2,1,0:T(8,128)} %copy-done.1), custom_call_target="tpu_custom_call" | custom-call | tf_op jit(solution)/shard_map/pallas_call | solution.py:74
  108.0 1.2 copy-done.5
  109.1 31.0 %shard_map.82 = (f32[8,128]{1,0:T(8,128)}, f32[8,64]{1,0:T(8,128)}) custom-call(f32[128,8]{1,0:T(8,128)} %bitcast.45, f32[64,8]{1,0:T(8,128)} %multiply_bitcast_fusion.rd_ref, f32[8,1]{1,0:T(8,128)} %copy.68.sl_ref, f32[8,1]{1,0:T(8,128)} %copy.69.sd_ref, f32[16,8,3072]{2,1,0:T(8,128)} %copy-done.5), custom_call_target="tpu_custom_call" | custom-call | tf_op jit(solution)/shard_map/pallas_call | solution.py:74
  140.8 3.0 %collective-permute-start.8 = (f32[1,8,128]{2,1,0:T(8,128)S(1)}, f32[1,8,128]{2,1,0:T(8,128)S(1)}, u32[]{:S(2)}, u32[]{:S(2)}) collective-permute-start(f32[1,8,128]{2,1,0:T(8,128)S(1)} %bitcast.52), channel_id=1, source_target_pairs={{0,4},{1,5},{2,6},{3,7},{4,0},{5,1},{6,2},{7,3},{8,12},{9,13},{10,... | collective-permute-start | bytes 12296 | tf_op jit(solution)/shard_map/ppermute | solution.py:99
  143.9 2.1 %collective-permute-done.8 = f32[1,8,128]{2,1,0:T(8,128)S(1)} collective-permute-done((f32[1,8,128]{2,1,0:T(8,128)S(1)}, f32[1,8,128]{2,1,0:T(8,128)S(1)}, u32[]{:S(2)}, u32[]{:S(2)}) %collective-permute-start.8) | collective-permute-done | bytes 4128 | tf_op jit(solution)/shard_map/ppermute | solution.py:99
  146.3 4.8 %collective-permute-done.9 = f32[2,8,128]{2,1,0:T(8,128)S(1)} collective-permute-done((f32[2,8,128]{2,1,0:T(8,128)S(1)}, f32[2,8,128]{2,1,0:T(8,128)S(1)}, u32[]{:S(2)}, u32[]{:S(2)}) %collective-permute-start.9) | collective-permute-done | bytes 8224 | tf_op jit(solution)/shard_map/ppermute | solution.py:99
  151.1 1.6 %collective-permute-start.10 = (f32[4,8,128]{2,1,0:T(8,128)S(1)}, f32[4,8,128]{2,1,0:T(8,128)S(1)}, u32[]{:S(2)}, u32[]{:S(2)}) collective-permute-start(f32[4,8,128]{2,1,0:T(8,128)S(1)} %pad_maximum_fusion.7), channel_id=1, source_target_pairs={{0,2},{1,3},{2,0},{3,1},{4,6},{5,7},{6,4},{7,5},{8,10},{9,11},{10,... | collective-permute-start | bytes 49160 | tf_op jit(solution)/shard_map/ppermute | solution.py:99
  153.1 1.9 %collective-permute-done.10 = f32[4,8,128]{2,1,0:T(8,128)S(1)} collective-permute-done((f32[4,8,128]{2,1,0:T(8,128)S(1)}, f32[4,8,128]{2,1,0:T(8,128)S(1)}, u32[]{:S(2)}, u32[]{:S(2)}) %collective-permute-start.10) | collective-permute-done | bytes 16416 | tf_op jit(solution)/shard_map/ppermute | solution.py:99
  155.4 1.3 add_add_fusion
  (86 shorter events, 8.2 us)
Async XLA Ops:
  2.8 5.3 %collective-permute-start = (f32[1,2624]{1,0:T(1,128)S(1)}, f32[1,2624]{1,0:T(1,128)S(1)}, u32[]{:S(2)}, u32[]{:S(2)}) collective-permute-start(f32[1,2624]{1,0:T(1,128)S(1)} %broadcast_in_dim.10), channel_id=1, source_target_pairs={{0,4},{1,5},{2,6},{3,7},{4,0},{5,1},{6,2},{7,3},{8,12},{9,13},{10,... | collective-permute-start | bytes 31496 | tf_op jit(solution)/shard_map/ppermute | solution.py:99
  8.1 5.4 %collective-permute-start.1 = (f32[2,2624]{1,0:T(2,128)S(1)}, f32[2,2624]{1,0:T(2,128)S(1)}, u32[]{:S(2)}, u32[]{:S(2)}) collective-permute-start(f32[2,2624]{1,0:T(2,128)S(1)} %pad_maximum_fusion.6), channel_id=1, source_target_pairs={{0,1},{1,0},{2,3},{3,2},{4,5},{5,4},{6,7},{7,6},{8,9},{9,8},{10,11... | collective-permute-start | bytes 62984 | tf_op jit(solution)/shard_map/ppermute | solution.py:99
  13.5 4.1 %collective-permute-start.2 = (f32[4,2624]{1,0:T(4,128)S(1)}, f32[4,2624]{1,0:T(4,128)S(1)}, u32[]{:S(2)}, u32[]{:S(2)}) collective-permute-start(f32[4,2624]{1,0:T(4,128)S(1)} %pad_maximum_fusion.4), channel_id=1, source_target_pairs={{0,2},{1,3},{2,0},{3,1},{4,6},{5,7},{6,4},{7,5},{8,10},{9,11},{10,... | collective-permute-start | bytes 125960 | tf_op jit(solution)/shard_map/ppermute | solution.py:99
  20.0 31.5 %copy-start.3 = (f32[1,8,3072]{2,1,0:T(8,128)}, f32[1,8,3072]{2,1,0:T(8,128)S(1)}, u32[]{:S(2)}) copy-start(f32[1,8,3072]{2,1,0:T(8,128)S(1)} %maximum_bitcast_fusion.x_ref) | copy-start | bytes 294916
  20.0 10.8 %collective-permute-start.3 = (f32[1,8,3072]{2,1,0:T(8,128)S(1)}, f32[1,8,3072]{2,1,0:T(8,128)S(1)}, u32[]{:S(2)}, u32[]{:S(2)}) collective-permute-start(f32[1,8,3072]{2,1,0:T(8,128)S(1)} %maximum_bitcast_fusion.x_ref), channel_id=1, source_target_pairs={{0,128},{8,136},{16,144},{24,152},{32,160},{40,168},{48,176},{56,1... | collective-permute-start | bytes 294920 | tf_op jit(solution)/shard_map/ppermute | solution.py:165
  30.7 20.7 %copy-start.4 = (f32[1,8,3072]{2,1,0:T(8,128)}, f32[1,8,3072]{2,1,0:T(8,128)S(1)}, u32[]{:S(2)}) copy-start(f32[1,8,3072]{2,1,0:T(8,128)S(1)} %collective-permute-done.3.x_ref) | copy-start | bytes 294916
  30.8 9.0 %collective-permute-start.4 = (f32[2,8,3072]{2,1,0:T(8,128)S(1)}, f32[2,8,3072]{2,1,0:T(8,128)S(1)}, u32[]{:S(2)}, u32[]{:S(2)}) collective-permute-start(f32[2,8,3072]{2,1,0:T(8,128)S(1)} %pad_maximum_fusion.2), channel_id=1, source_target_pairs={{0,64},{8,72},{16,80},{24,88},{32,96},{40,104},{48,112},{56,120},{... | collective-permute-start | bytes 589832 | tf_op jit(solution)/shard_map/ppermute | solution.py:165
  39.8 12.4 %copy-start.2 = (f32[2,8,3072]{2,1,0:T(8,128)}, f32[2,8,3072]{2,1,0:T(8,128)S(1)}, u32[]{:S(2)}) copy-start(f32[2,8,3072]{2,1,0:T(8,128)S(1)} %collective-permute-done.4.x_ref) | copy-start | bytes 589828
  39.8 9.5 %collective-permute-start.5 = (f32[4,8,3072]{2,1,0:T(8,128)S(1)}, f32[4,8,3072]{2,1,0:T(8,128)S(1)}, u32[]{:S(2)}, u32[]{:S(2)}) collective-permute-start(f32[4,8,3072]{2,1,0:T(8,128)S(1)} %pad_maximum_fusion.1), channel_id=1, source_target_pairs={{0,32},{8,40},{16,48},{24,56},{32,0},{40,8},{48,16},{56,24},{64,96... | collective-permute-start | bytes 1179656 | tf_op jit(solution)/shard_map/ppermute | solution.py:165
  49.3 18.2 %copy-start = (f32[4,8,3072]{2,1,0:T(8,128)}, f32[4,8,3072]{2,1,0:T(8,128)S(1)}, u32[]{:S(2)}) copy-start(f32[4,8,3072]{2,1,0:T(8,128)S(1)} %collective-permute-done.5.x_ref) | copy-start | bytes 1179652
  49.4 18.1 %copy-start.7 = (f32[8,128]{1,0:T(8,128)S(1)}, f32[8,128]{1,0:T(8,128)}, u32[]{:S(2)}) copy-start(f32[8,128]{1,0:T(8,128)} %param.6) | copy-start | bytes 12292
  49.4 18.1 %copy-start.19 = (f32[8]{0:T(128)S(1)}, f32[8]{0:T(128)}, u32[]{:S(2)}) copy-start(f32[8]{0:T(128)} %param.10) | copy-start | bytes 100
  49.4 19.6 %copy-start.18 = (f32[8]{0:T(128)S(1)}, f32[8]{0:T(128)}, u32[]{:S(2)}) copy-start(f32[8]{0:T(128)} %param.11) | copy-start | bytes 100
  49.4 17.1 %collective-permute-start.6 = (f32[8,8,3072]{2,1,0:T(8,128)S(1)}, f32[8,8,3072]{2,1,0:T(8,128)S(1)}, u32[]{:S(2)}, u32[]{:S(2)}) collective-permute-start(f32[8,8,3072]{2,1,0:T(8,128)S(1)} %pad_maximum_fusion), channel_id=1, source_target_pairs={{0,16},{8,24},{16,0},{24,8},{32,48},{40,56},{48,32},{56,40},{64,80... | collective-permute-start | bytes 2359304 | tf_op jit(solution)/shard_map/ppermute | solution.py:165
  66.5 25.1 %copy-start.1 = (f32[8,8,3072]{2,1,0:T(8,128)}, f32[8,8,3072]{2,1,0:T(8,128)S(1)}, u32[]{:S(2)}) copy-start(f32[8,8,3072]{2,1,0:T(8,128)S(1)} %collective-permute-done.6.x_ref) | copy-start | bytes 2359300
  67.5 40.4 %collective-permute-start.7 = (f32[16,8,3072]{2,1,0:T(8,128)}, f32[16,8,3072]{2,1,0:T(8,128)S(1)}, u32[]{:S(2)}, u32[]{:S(2)}) collective-permute-start(f32[16,8,3072]{2,1,0:T(8,128)} %constant_dynamic-update-slice_fusion), channel_id=1, source_target_pairs={{0,8},{8,0},{16,24},{24,16},{32,40},{40,32},{48,56},{56,48},{64,72... | collective-permute-start | bytes 4718600 | tf_op jit(solution)/shard_map/ppermute | solution.py:165
  82.6 57.5 %copy-start.8 = (f32[8,128]{1,0:T(8,128)S(1)}, f32[8,128]{1,0:T(8,128)}, u32[]{:S(2)}) copy-start(f32[8,128]{1,0:T(8,128)} %get-tuple-element.14) | copy-start | bytes 12292
  82.6 57.5 %copy-start.9 = (f32[8,128]{1,0:T(8,128)S(1)}, f32[8,128]{1,0:T(8,128)}, u32[]{:S(2)}) copy-start(f32[8,128]{1,0:T(8,128)} %get-tuple-element.15) | copy-start | bytes 12292
  82.6 57.5 %copy-start.10 = (f32[8,128]{1,0:T(8,128)S(1)}, f32[8,128]{1,0:T(8,128)}, u32[]{:S(2)}) copy-start(f32[8,128]{1,0:T(8,128)} %get-tuple-element.16) | copy-start | bytes 12292
  91.6 48.5 %copy-start.11 = (f32[8,128]{1,0:T(8,128)S(1)}, f32[8,128]{1,0:T(8,128)}, u32[]{:S(2)}) copy-start(f32[8,128]{1,0:T(8,128)} %get-tuple-element.17) | copy-start | bytes 12292
  107.9 32.2 %copy-start.12 = (f32[8,128]{1,0:T(8,128)S(1)}, f32[8,128]{1,0:T(8,128)}, u32[]{:S(2)}) copy-start(f32[8,128]{1,0:T(8,128)} %get-tuple-element.18) | copy-start | bytes 12292
  107.9 47.4 %copy-start.13 = (f32[8,64]{1,0:T(8,128)S(1)}, f32[8,64]{1,0:T(8,128)}, u32[]{:S(2)}) copy-start(f32[8,64]{1,0:T(8,128)} %get-tuple-element.20) | copy-start | bytes 6148
  107.9 47.5 %copy-start.14 = (f32[8,64]{1,0:T(8,128)S(1)}, f32[8,64]{1,0:T(8,128)}, u32[]{:S(2)}) copy-start(f32[8,64]{1,0:T(8,128)} %get-tuple-element.21) | copy-start | bytes 6148
  107.9 47.5 %copy-start.15 = (f32[8,64]{1,0:T(8,128)S(1)}, f32[8,64]{1,0:T(8,128)}, u32[]{:S(2)}) copy-start(f32[8,64]{1,0:T(8,128)} %get-tuple-element.22) | copy-start | bytes 6148
  107.9 47.5 %copy-start.16 = (f32[8,64]{1,0:T(8,128)S(1)}, f32[8,64]{1,0:T(8,128)}, u32[]{:S(2)}) copy-start(f32[8,64]{1,0:T(8,128)} %get-tuple-element.23) | copy-start | bytes 6148
  107.9 47.5 %copy-start.17 = (f32[8,64]{1,0:T(8,128)S(1)}, f32[8,64]{1,0:T(8,128)}, u32[]{:S(2)}) copy-start(f32[8,64]{1,0:T(8,128)} %get-tuple-element.24) | copy-start | bytes 6148
  108.0 1.2 copy-start.5
  140.8 15.9 %copy-start.6 = (f32[8,128]{1,0:T(8,128)}, f32[8,128]{1,0:T(8,128)S(1)}, u32[]{:S(2)}) copy-start(f32[8,128]{1,0:T(8,128)S(1)} %add_add_fusion.1) | copy-start | bytes 12292
  140.8 5.1 %collective-permute-start.8 = (f32[1,8,128]{2,1,0:T(8,128)S(1)}, f32[1,8,128]{2,1,0:T(8,128)S(1)}, u32[]{:S(2)}, u32[]{:S(2)}) collective-permute-start(f32[1,8,128]{2,1,0:T(8,128)S(1)} %bitcast.52), channel_id=1, source_target_pairs={{0,4},{1,5},{2,6},{3,7},{4,0},{5,1},{6,2},{7,3},{8,12},{9,13},{10,... | collective-permute-start | bytes 12296 | tf_op jit(solution)/shard_map/ppermute | solution.py:99
  146.0 5.2 %collective-permute-start.9 = (f32[2,8,128]{2,1,0:T(8,128)S(1)}, f32[2,8,128]{2,1,0:T(8,128)S(1)}, u32[]{:S(2)}, u32[]{:S(2)}) collective-permute-start(f32[2,8,128]{2,1,0:T(8,128)S(1)} %pad_maximum_fusion.9), channel_id=1, source_target_pairs={{0,1},{1,0},{2,3},{3,2},{4,5},{5,4},{6,7},{7,6},{8,9},{9,8},{10,11... | collective-permute-start | bytes 24584 | tf_op jit(solution)/shard_map/ppermute | solution.py:99
  151.1 3.8 %collective-permute-start.10 = (f32[4,8,128]{2,1,0:T(8,128)S(1)}, f32[4,8,128]{2,1,0:T(8,128)S(1)}, u32[]{:S(2)}, u32[]{:S(2)}) collective-permute-start(f32[4,8,128]{2,1,0:T(8,128)S(1)} %pad_maximum_fusion.7), channel_id=1, source_target_pairs={{0,2},{1,3},{2,0},{3,1},{4,6},{5,7},{6,4},{7,5},{8,10},{9,11},{10,... | collective-permute-start | bytes 49160 | tf_op jit(solution)/shard_map/ppermute | solution.py:99

commit v4 on v0

--- a/solution.py
+++ b/solution.py
@@ -16,7 +16,7 @@
 BLK_BITS = (4, 3, 2, 1, 0)
 
 
-COL_SUB = 512
+COL_SUB = 1024
 
 
 def _accumulate(rows, rn, cols, w):
@@ -46,13 +46,15 @@
 
     def one_block(b, carry):
         acc_l, acc_d = carry
-        for c in range(0, nb, COL_SUB):
-            cols = x_ref[b, :, c:c + COL_SUB] * scale_l
-            w = x_ref[b, :, nb + c:nb + c + COL_SUB]
+        sub_l = min(COL_SUB, nb)
+        sub_h = min(COL_SUB, nh)
+        for c in range(0, nb, sub_l):
+            cols = x_ref[b, :, c:c + sub_l] * scale_l
+            w = x_ref[b, :, nb + c:nb + c + sub_l]
             acc_l = acc_l + _accumulate(rows_l, rn_l, cols, w)
-        for c in range(0, nh, COL_SUB):
-            cols = x_ref[b, :, 2 * nb + c:2 * nb + c + COL_SUB] * scale_d
-            w = x_ref[b, :, 2 * nb + nh + c:2 * nb + nh + c + COL_SUB]
+        for c in range(0, nh, sub_h):
+            cols = x_ref[b, :, 2 * nb + c:2 * nb + c + sub_h] * scale_d
+            w = x_ref[b, :, 2 * nb + nh + c:2 * nb + nh + c + sub_h]
             acc_d = acc_d + _accumulate(rows_d, rn_d, cols, w)
         return acc_l, acc_d
 

time: 143 us -> 138 us (0.965)
  Pallas kernels: 54.2 us -> 48.9 us
    pallas_call x6, Pallas kernels: 54.2 us -> 48.9 us  [apply_piece(): pl.pallas_call(kern, grid=(n // per,), in_specs=[full((rl, feats)), full(...]
  transfers between devices with their start and end apart: 11 -> 11, of which waited for: 10 -> 10; matrix products, arithmetic and copies ran while one was open for 4% -> 4% of each run, Pallas kernels for 21% -> 20%
where the time goes in v4:
time: 138 us; the launch traced here: 137 us
  waiting for transfers between devices  50.3 us (36%)
  Pallas kernels  48.9 us (35%)
  starting transfers between devices  21.8 us (16%)
  local copies, waits for them, and re-layouts  7.79 us (6%)
  other arithmetic  5.33 us (4%)
  matrix products  2.13 us (2%)
    pallas_call x6, Pallas kernels, apply_piece(): pl.pallas_call(kern, grid=(n // per,), in_specs=[full((rl, feats)), full(...  48.9 us
    ppermute x5, waiting for transfers between devices, per_device(): other = lax.ppermute(buf, 'blk', [(i, i ^ mask) for i in range(blk_size)])  33.6 us
    ppermute x6, waiting for transfers between devices, gather_bits(): other = lax.ppermute(buf, axis, [(i, i ^ mask) for i in range(size)])  16.7 us
    ppermute x6, starting transfers between devices, gather_bits(): other = lax.ppermute(buf, axis, [(i, i ^ mask) for i in range(size)])  11.8 us
    ppermute x5, starting transfers between devices, per_device(): other = lax.ppermute(buf, 'blk', [(i, i ^ mask) for i in range(blk_size)])  10 us
    unnamed x44, local copies, waits for them, and re-layouts  3.45 us
  transfers between devices with their start and end apart: 11, of which 10 were waited for; matrix products, arithmetic and copies ran while one was open for 4% of the time, Pallas kernels for 20%

profile of v4, /device:TPU:16, one launch (start us, length us, event | category | flops | bytes accessed | tf_op | source)
XLA Modules:
  0.0 137.2 jit_solution(7735410670450328819)
XLA Ops:
  0.6 0.8 reshape.60
  2.8 3.1 %collective-permute-start = (f32[1,2624]{1,0:T(1,128)S(1)}, f32[1,2624]{1,0:T(1,128)S(1)}, u32[]{:S(2)}, u32[]{:S(2)}) collective-permute-start(f32[1,2624]{1,0:T(1,128)S(1)} %broadcast_in_dim.10), channel_id=1, source_target_pairs={{0,4},{1,5},{2,6},{3,7},{4,0},{5,1},{6,2},{7,3},{8,12},{9,13},{10,... | collective-permute-start | bytes 31496 | tf_op jit(solution)/shard_map/ppermute | solution.py:100
  5.9 2.2 %collective-permute-done = f32[1,2624]{1,0:T(1,128)S(1)} collective-permute-done((f32[1,2624]{1,0:T(1,128)S(1)}, f32[1,2624]{1,0:T(1,128)S(1)}, u32[]{:S(2)}, u32[]{:S(2)}) %collective-permute-start) | collective-permute-done | bytes 10528 | tf_op jit(solution)/shard_map/ppermute | solution.py:100
  8.1 2.1 %collective-permute-start.1 = (f32[2,2624]{1,0:T(2,128)S(1)}, f32[2,2624]{1,0:T(2,128)S(1)}, u32[]{:S(2)}, u32[]{:S(2)}) collective-permute-start(f32[2,2624]{1,0:T(2,128)S(1)} %pad_maximum_fusion.6), channel_id=1, source_target_pairs={{0,1},{1,0},{2,3},{3,2},{4,5},{5,4},{6,7},{7,6},{8,9},{9,8},{10,11... | collective-permute-start | bytes 62984 | tf_op jit(solution)/shard_map/ppermute | solution.py:100
  10.2 3.3 %collective-permute-done.1 = f32[2,2624]{1,0:T(2,128)S(1)} collective-permute-done((f32[2,2624]{1,0:T(2,128)S(1)}, f32[2,2624]{1,0:T(2,128)S(1)}, u32[]{:S(2)}, u32[]{:S(2)}) %collective-permute-start.1) | collective-permute-done | bytes 21024 | tf_op jit(solution)/shard_map/ppermute | solution.py:100
  13.5 1.6 %collective-permute-start.2 = (f32[4,2624]{1,0:T(4,128)S(1)}, f32[4,2624]{1,0:T(4,128)S(1)}, u32[]{:S(2)}, u32[]{:S(2)}) collective-permute-start(f32[4,2624]{1,0:T(4,128)S(1)} %pad_maximum_fusion.4), channel_id=1, source_target_pairs={{0,2},{1,3},{2,0},{3,1},{4,6},{5,7},{6,4},{7,5},{8,10},{9,11},{10,... | collective-permute-start | bytes 125960 | tf_op jit(solution)/shard_map/ppermute | solution.py:100
  15.1 2.5 %collective-permute-done.2 = f32[4,2624]{1,0:T(4,128)S(1)} collective-permute-done((f32[4,2624]{1,0:T(4,128)S(1)}, f32[4,2624]{1,0:T(4,128)S(1)}, u32[]{:S(2)}, u32[]{:S(2)}) %collective-permute-start.2) | collective-permute-done | bytes 42016 | tf_op jit(solution)/shard_map/ppermute | solution.py:100
  18.2 0.7 fusion.1
  18.9 1.0 fusion
  20.0 7.3 %collective-permute-start.3 = (f32[1,8,3072]{2,1,0:T(8,128)S(1)}, f32[1,8,3072]{2,1,0:T(8,128)S(1)}, u32[]{:S(2)}, u32[]{:S(2)}) collective-permute-start(f32[1,8,3072]{2,1,0:T(8,128)S(1)} %maximum_bitcast_fusion.x_ref), channel_id=1, source_target_pairs={{0,128},{8,136},{16,144},{24,152},{32,160},{40,168},{48,176},{56,1... | collective-permute-start | bytes 294920 | tf_op jit(solution)/shard_map/ppermute | solution.py:166
  27.2 3.5 %collective-permute-done.3.x_ref = f32[1,8,3072]{2,1,0:T(8,128)S(1)} collective-permute-done((f32[1,8,3072]{2,1,0:T(8,128)S(1)}, f32[1,8,3072]{2,1,0:T(8,128)S(1)}, u32[]{:S(2)}, u32[]{:S(2)}) %collective-permute-start.3) | collective-permute-done | bytes 98336 | tf_op jit(solution)/shard_map/ppermute | solution.py:166
  30.8 1.3 collective-permute-start.4
  32.0 7.7 %collective-permute-done.4.x_ref = f32[2,8,3072]{2,1,0:T(8,128)S(1)} collective-permute-done((f32[2,8,3072]{2,1,0:T(8,128)S(1)}, f32[2,8,3072]{2,1,0:T(8,128)S(1)}, u32[]{:S(2)}, u32[]{:S(2)}) %collective-permute-start.4) | collective-permute-done | bytes 196640 | tf_op jit(solution)/shard_map/ppermute | solution.py:166
  40.5 8.8 %collective-permute-done.5.x_ref = f32[4,8,3072]{2,1,0:T(8,128)S(1)} collective-permute-done((f32[4,8,3072]{2,1,0:T(8,128)S(1)}, f32[4,8,3072]{2,1,0:T(8,128)S(1)}, u32[]{:S(2)}, u32[]{:S(2)}) %collective-permute-start.5) | collective-permute-done | bytes 393248 | tf_op jit(solution)/shard_map/ppermute | solution.py:166
  49.4 1.4 collective-permute-start.6
  52.1 0.8 constant_dynamic-update-slice_fusion.1
  52.9 13.6 %collective-permute-done.6.x_ref = f32[8,8,3072]{2,1,0:T(8,128)S(1)} collective-permute-done((f32[8,8,3072]{2,1,0:T(8,128)S(1)}, f32[8,8,3072]{2,1,0:T(8,128)S(1)}, u32[]{:S(2)}, u32[]{:S(2)}) %collective-permute-start.6) | collective-permute-done | bytes 786464 | tf_op jit(solution)/shard_map/ppermute | solution.py:166
  66.5 1.0 constant_dynamic-update-slice_fusion
  67.6 0.7 copy.62
  70.4 2.8 %shard_map.77 = (f32[8,128]{1,0:T(8,128)}, f32[8,64]{1,0:T(8,128)}) custom-call(f32[128,8]{1,0:T(8,128)} %bitcast.40, f32[64,8]{1,0:T(8,128)} %multiply_bitcast_fusion.rd_ref, f32[8,1]{1,0:T(8,128)} %copy.68.sl_ref, f32[8,1]{1,0:T(8,128)} %copy.69.sd_ref, f32[1,8,3072]{2,1,0:T(8,128)} %copy-done.3), custom_call_target="tpu_custom_call" | custom-call | tf_op jit(solution)/shard_map/pallas_call | solution.py:75
  73.2 2.8 %shard_map.78 = (f32[8,128]{1,0:T(8,128)}, f32[8,64]{1,0:T(8,128)}) custom-call(f32[128,8]{1,0:T(8,128)} %bitcast.41, f32[64,8]{1,0:T(8,128)} %multiply_bitcast_fusion.rd_ref, f32[8,1]{1,0:T(8,128)} %copy.68.sl_ref, f32[8,1]{1,0:T(8,128)} %copy.69.sd_ref, f32[1,8,3072]{2,1,0:T(8,128)} %copy-done.4), custom_call_target="tpu_custom_call" | custom-call | tf_op jit(solution)/shard_map/pallas_call | solution.py:75
  76.0 4.1 %shard_map.79 = (f32[8,128]{1,0:T(8,128)}, f32[8,64]{1,0:T(8,128)}) custom-call(f32[128,8]{1,0:T(8,128)} %bitcast.42, f32[64,8]{1,0:T(8,128)} %multiply_bitcast_fusion.rd_ref, f32[8,1]{1,0:T(8,128)} %copy.68.sl_ref, f32[8,1]{1,0:T(8,128)} %copy.69.sd_ref, f32[2,8,3072]{2,1,0:T(8,128)} %copy-done.2), custom_call_target="tpu_custom_call" | custom-call | tf_op jit(solution)/shard_map/pallas_call | solution.py:75
  80.1 6.6 %shard_map.80 = (f32[8,128]{1,0:T(8,128)}, f32[8,64]{1,0:T(8,128)}) custom-call(f32[128,8]{1,0:T(8,128)} %bitcast.43, f32[64,8]{1,0:T(8,128)} %multiply_bitcast_fusion.rd_ref, f32[8,1]{1,0:T(8,128)} %copy.68.sl_ref, f32[8,1]{1,0:T(8,128)} %copy.69.sd_ref, f32[4,8,3072]{2,1,0:T(8,128)} %copy-done), custom_call_target="tpu_custom_call" | custom-call | tf_op jit(solution)/shard_map/pallas_call | solution.py:75
  86.7 11.4 %shard_map.81 = (f32[8,128]{1,0:T(8,128)}, f32[8,64]{1,0:T(8,128)}) custom-call(f32[128,8]{1,0:T(8,128)} %bitcast.44, f32[64,8]{1,0:T(8,128)} %multiply_bitcast_fusion.rd_ref, f32[8,1]{1,0:T(8,128)} %copy.68.sl_ref, f32[8,1]{1,0:T(8,128)} %copy.69.sd_ref, f32[8,8,3072]{2,1,0:T(8,128)} %copy-done.1), custom_call_target="tpu_custom_call" | custom-call | tf_op jit(solution)/shard_map/pallas_call | solution.py:75
  98.2 1.2 copy-done.5
  99.3 21.2 %shard_map.82 = (f32[8,128]{1,0:T(8,128)}, f32[8,64]{1,0:T(8,128)}) custom-call(f32[128,8]{1,0:T(8,128)} %bitcast.45, f32[64,8]{1,0:T(8,128)} %multiply_bitcast_fusion.rd_ref, f32[8,1]{1,0:T(8,128)} %copy.68.sl_ref, f32[8,1]{1,0:T(8,128)} %copy.69.sd_ref, f32[16,8,3072]{2,1,0:T(8,128)} %copy-done.5), custom_call_target="tpu_custom_call" | custom-call | tf_op jit(solution)/shard_map/pallas_call | solution.py:75
  121.3 3.0 %collective-permute-start.8 = (f32[1,8,128]{2,1,0:T(8,128)S(1)}, f32[1,8,128]{2,1,0:T(8,128)S(1)}, u32[]{:S(2)}, u32[]{:S(2)}) collective-permute-start(f32[1,8,128]{2,1,0:T(8,128)S(1)} %bitcast.52), channel_id=1, source_target_pairs={{0,4},{1,5},{2,6},{3,7},{4,0},{5,1},{6,2},{7,3},{8,12},{9,13},{10,... | collective-permute-start | bytes 12296 | tf_op jit(solution)/shard_map/ppermute | solution.py:100
  124.3 2.1 %collective-permute-done.8 = f32[1,8,128]{2,1,0:T(8,128)S(1)} collective-permute-done((f32[1,8,128]{2,1,0:T(8,128)S(1)}, f32[1,8,128]{2,1,0:T(8,128)S(1)}, u32[]{:S(2)}, u32[]{:S(2)}) %collective-permute-start.8) | collective-permute-done | bytes 4128 | tf_op jit(solution)/shard_map/ppermute | solution.py:100
  126.8 4.8 %collective-permute-done.9 = f32[2,8,128]{2,1,0:T(8,128)S(1)} collective-permute-done((f32[2,8,128]{2,1,0:T(8,128)S(1)}, f32[2,8,128]{2,1,0:T(8,128)S(1)}, u32[]{:S(2)}, u32[]{:S(2)}) %collective-permute-start.9) | collective-permute-done | bytes 8224 | tf_op jit(solution)/shard_map/ppermute | solution.py:100
  131.6 1.6 %collective-permute-start.10 = (f32[4,8,128]{2,1,0:T(8,128)S(1)}, f32[4,8,128]{2,1,0:T(8,128)S(1)}, u32[]{:S(2)}, u32[]{:S(2)}) collective-permute-start(f32[4,8,128]{2,1,0:T(8,128)S(1)} %pad_maximum_fusion.7), channel_id=1, source_target_pairs={{0,2},{1,3},{2,0},{3,1},{4,6},{5,7},{6,4},{7,5},{8,10},{9,11},{10,... | collective-permute-start | bytes 49160 | tf_op jit(solution)/shard_map/ppermute | solution.py:100
  133.5 1.9 %collective-permute-done.10 = f32[4,8,128]{2,1,0:T(8,128)S(1)} collective-permute-done((f32[4,8,128]{2,1,0:T(8,128)S(1)}, f32[4,8,128]{2,1,0:T(8,128)S(1)}, u32[]{:S(2)}, u32[]{:S(2)}) %collective-permute-start.10) | collective-permute-done | bytes 16416 | tf_op jit(solution)/shard_map/ppermute | solution.py:100
  135.9 1.3 add_add_fusion
  (86 shorter events, 8.2 us)
Async XLA Ops:
  2.8 5.3 %collective-permute-start = (f32[1,2624]{1,0:T(1,128)S(1)}, f32[1,2624]{1,0:T(1,128)S(1)}, u32[]{:S(2)}, u32[]{:S(2)}) collective-permute-start(f32[1,2624]{1,0:T(1,128)S(1)} %broadcast_in_dim.10), channel_id=1, source_target_pairs={{0,4},{1,5},{2,6},{3,7},{4,0},{5,1},{6,2},{7,3},{8,12},{9,13},{10,... | collective-permute-start | bytes 31496 | tf_op jit(solution)/shard_map/ppermute | solution.py:100
  8.1 5.4 %collective-permute-start.1 = (f32[2,2624]{1,0:T(2,128)S(1)}, f32[2,2624]{1,0:T(2,128)S(1)}, u32[]{:S(2)}, u32[]{:S(2)}) collective-permute-start(f32[2,2624]{1,0:T(2,128)S(1)} %pad_maximum_fusion.6), channel_id=1, source_target_pairs={{0,1},{1,0},{2,3},{3,2},{4,5},{5,4},{6,7},{7,6},{8,9},{9,8},{10,11... | collective-permute-start | bytes 62984 | tf_op jit(solution)/shard_map/ppermute | solution.py:100
  13.5 4.1 %collective-permute-start.2 = (f32[4,2624]{1,0:T(4,128)S(1)}, f32[4,2624]{1,0:T(4,128)S(1)}, u32[]{:S(2)}, u32[]{:S(2)}) collective-permute-start(f32[4,2624]{1,0:T(4,128)S(1)} %pad_maximum_fusion.4), channel_id=1, source_target_pairs={{0,2},{1,3},{2,0},{3,1},{4,6},{5,7},{6,4},{7,5},{8,10},{9,11},{10,... | collective-permute-start | bytes 125960 | tf_op jit(solution)/shard_map/ppermute | solution.py:100
  20.0 31.5 %copy-start.3 = (f32[1,8,3072]{2,1,0:T(8,128)}, f32[1,8,3072]{2,1,0:T(8,128)S(1)}, u32[]{:S(2)}) copy-start(f32[1,8,3072]{2,1,0:T(8,128)S(1)} %maximum_bitcast_fusion.x_ref) | copy-start | bytes 294916
  20.0 10.8 %collective-permute-start.3 = (f32[1,8,3072]{2,1,0:T(8,128)S(1)}, f32[1,8,3072]{2,1,0:T(8,128)S(1)}, u32[]{:S(2)}, u32[]{:S(2)}) collective-permute-start(f32[1,8,3072]{2,1,0:T(8,128)S(1)} %maximum_bitcast_fusion.x_ref), channel_id=1, source_target_pairs={{0,128},{8,136},{16,144},{24,152},{32,160},{40,168},{48,176},{56,1... | collective-permute-start | bytes 294920 | tf_op jit(solution)/shard_map/ppermute | solution.py:166
  30.7 20.7 %copy-start.4 = (f32[1,8,3072]{2,1,0:T(8,128)}, f32[1,8,3072]{2,1,0:T(8,128)S(1)}, u32[]{:S(2)}) copy-start(f32[1,8,3072]{2,1,0:T(8,128)S(1)} %collective-permute-done.3.x_ref) | copy-start | bytes 294916
  30.8 9.0 %collective-permute-start.4 = (f32[2,8,3072]{2,1,0:T(8,128)S(1)}, f32[2,8,3072]{2,1,0:T(8,128)S(1)}, u32[]{:S(2)}, u32[]{:S(2)}) collective-permute-start(f32[2,8,3072]{2,1,0:T(8,128)S(1)} %pad_maximum_fusion.2), channel_id=1, source_target_pairs={{0,64},{8,72},{16,80},{24,88},{32,96},{40,104},{48,112},{56,120},{... | collective-permute-start | bytes 589832 | tf_op jit(solution)/shard_map/ppermute | solution.py:166
  39.8 12.4 %copy-start.2 = (f32[2,8,3072]{2,1,0:T(8,128)}, f32[2,8,3072]{2,1,0:T(8,128)S(1)}, u32[]{:S(2)}) copy-start(f32[2,8,3072]{2,1,0:T(8,128)S(1)} %collective-permute-done.4.x_ref) | copy-start | bytes 589828
  39.8 9.5 %collective-permute-start.5 = (f32[4,8,3072]{2,1,0:T(8,128)S(1)}, f32[4,8,3072]{2,1,0:T(8,128)S(1)}, u32[]{:S(2)}, u32[]{:S(2)}) collective-permute-start(f32[4,8,3072]{2,1,0:T(8,128)S(1)} %pad_maximum_fusion.1), channel_id=1, source_target_pairs={{0,32},{8,40},{16,48},{24,56},{32,0},{40,8},{48,16},{56,24},{64,96... | collective-permute-start | bytes 1179656 | tf_op jit(solution)/shard_map/ppermute | solution.py:166
  49.3 18.2 %copy-start = (f32[4,8,3072]{2,1,0:T(8,128)}, f32[4,8,3072]{2,1,0:T(8,128)S(1)}, u32[]{:S(2)}) copy-start(f32[4,8,3072]{2,1,0:T(8,128)S(1)} %collective-permute-done.5.x_ref) | copy-start | bytes 1179652
  49.4 18.1 %copy-start.7 = (f32[8,128]{1,0:T(8,128)S(1)}, f32[8,128]{1,0:T(8,128)}, u32[]{:S(2)}) copy-start(f32[8,128]{1,0:T(8,128)} %param.6) | copy-start | bytes 12292
  49.4 18.1 %copy-start.19 = (f32[8]{0:T(128)S(1)}, f32[8]{0:T(128)}, u32[]{:S(2)}) copy-start(f32[8]{0:T(128)} %param.10) | copy-start | bytes 100
  49.4 19.6 %copy-start.18 = (f32[8]{0:T(128)S(1)}, f32[8]{0:T(128)}, u32[]{:S(2)}) copy-start(f32[8]{0:T(128)} %param.11) | copy-start | bytes 100
  49.4 17.1 %collective-permute-start.6 = (f32[8,8,3072]{2,1,0:T(8,128)S(1)}, f32[8,8,3072]{2,1,0:T(8,128)S(1)}, u32[]{:S(2)}, u32[]{:S(2)}) collective-permute-start(f32[8,8,3072]{2,1,0:T(8,128)S(1)} %pad_maximum_fusion), channel_id=1, source_target_pairs={{0,16},{8,24},{16,0},{24,8},{32,48},{40,56},{48,32},{56,40},{64,80... | collective-permute-start | bytes 2359304 | tf_op jit(solution)/shard_map/ppermute | solution.py:166
  66.5 20.2 %copy-start.1 = (f32[8,8,3072]{2,1,0:T(8,128)}, f32[8,8,3072]{2,1,0:T(8,128)S(1)}, u32[]{:S(2)}) copy-start(f32[8,8,3072]{2,1,0:T(8,128)S(1)} %collective-permute-done.6.x_ref) | copy-start | bytes 2359300
  67.5 30.6 %collective-permute-start.7 = (f32[16,8,3072]{2,1,0:T(8,128)}, f32[16,8,3072]{2,1,0:T(8,128)S(1)}, u32[]{:S(2)}, u32[]{:S(2)}) collective-permute-start(f32[16,8,3072]{2,1,0:T(8,128)} %constant_dynamic-update-slice_fusion), channel_id=1, source_target_pairs={{0,8},{8,0},{16,24},{24,16},{32,40},{40,32},{48,56},{56,48},{64,72... | collective-permute-start | bytes 4718600 | tf_op jit(solution)/shard_map/ppermute | solution.py:166
  80.1 40.5 %copy-start.8 = (f32[8,128]{1,0:T(8,128)S(1)}, f32[8,128]{1,0:T(8,128)}, u32[]{:S(2)}) copy-start(f32[8,128]{1,0:T(8,128)} %get-tuple-element.14) | copy-start | bytes 12292
  80.1 40.5 %copy-start.9 = (f32[8,128]{1,0:T(8,128)S(1)}, f32[8,128]{1,0:T(8,128)}, u32[]{:S(2)}) copy-start(f32[8,128]{1,0:T(8,128)} %get-tuple-element.15) | copy-start | bytes 12292
  80.1 40.5 %copy-start.10 = (f32[8,128]{1,0:T(8,128)S(1)}, f32[8,128]{1,0:T(8,128)}, u32[]{:S(2)}) copy-start(f32[8,128]{1,0:T(8,128)} %get-tuple-element.16) | copy-start | bytes 12292
  86.7 33.9 %copy-start.11 = (f32[8,128]{1,0:T(8,128)S(1)}, f32[8,128]{1,0:T(8,128)}, u32[]{:S(2)}) copy-start(f32[8,128]{1,0:T(8,128)} %get-tuple-element.17) | copy-start | bytes 12292
  98.1 22.5 %copy-start.12 = (f32[8,128]{1,0:T(8,128)S(1)}, f32[8,128]{1,0:T(8,128)}, u32[]{:S(2)}) copy-start(f32[8,128]{1,0:T(8,128)} %get-tuple-element.18) | copy-start | bytes 12292
  98.1 37.7 %copy-start.13 = (f32[8,64]{1,0:T(8,128)S(1)}, f32[8,64]{1,0:T(8,128)}, u32[]{:S(2)}) copy-start(f32[8,64]{1,0:T(8,128)} %get-tuple-element.20) | copy-start | bytes 6148
  98.1 37.7 %copy-start.14 = (f32[8,64]{1,0:T(8,128)S(1)}, f32[8,64]{1,0:T(8,128)}, u32[]{:S(2)}) copy-start(f32[8,64]{1,0:T(8,128)} %get-tuple-element.21) | copy-start | bytes 6148
  98.1 37.7 %copy-start.15 = (f32[8,64]{1,0:T(8,128)S(1)}, f32[8,64]{1,0:T(8,128)}, u32[]{:S(2)}) copy-start(f32[8,64]{1,0:T(8,128)} %get-tuple-element.22) | copy-start | bytes 6148
  98.1 37.7 %copy-start.16 = (f32[8,64]{1,0:T(8,128)S(1)}, f32[8,64]{1,0:T(8,128)}, u32[]{:S(2)}) copy-start(f32[8,64]{1,0:T(8,128)} %get-tuple-element.23) | copy-start | bytes 6148
  98.1 37.7 %copy-start.17 = (f32[8,64]{1,0:T(8,128)S(1)}, f32[8,64]{1,0:T(8,128)}, u32[]{:S(2)}) copy-start(f32[8,64]{1,0:T(8,128)} %get-tuple-element.24) | copy-start | bytes 6148
  98.2 1.2 copy-start.5
  121.3 15.9 %copy-start.6 = (f32[8,128]{1,0:T(8,128)}, f32[8,128]{1,0:T(8,128)S(1)}, u32[]{:S(2)}) copy-start(f32[8,128]{1,0:T(8,128)S(1)} %add_add_fusion.1) | copy-start | bytes 12292
  121.3 5.1 %collective-permute-start.8 = (f32[1,8,128]{2,1,0:T(8,128)S(1)}, f32[1,8,128]{2,1,0:T(8,128)S(1)}, u32[]{:S(2)}, u32[]{:S(2)}) collective-permute-start(f32[1,8,128]{2,1,0:T(8,128)S(1)} %bitcast.52), channel_id=1, source_target_pairs={{0,4},{1,5},{2,6},{3,7},{4,0},{5,1},{6,2},{7,3},{8,12},{9,13},{10,... | collective-permute-start | bytes 12296 | tf_op jit(solution)/shard_map/ppermute | solution.py:100
  126.4 5.2 %collective-permute-start.9 = (f32[2,8,128]{2,1,0:T(8,128)S(1)}, f32[2,8,128]{2,1,0:T(8,128)S(1)}, u32[]{:S(2)}, u32[]{:S(2)}) collective-permute-start(f32[2,8,128]{2,1,0:T(8,128)S(1)} %pad_maximum_fusion.9), channel_id=1, source_target_pairs={{0,1},{1,0},{2,3},{3,2},{4,5},{5,4},{6,7},{7,6},{8,9},{9,8},{10,11... | collective-permute-start | bytes 24584 | tf_op jit(solution)/shard_map/ppermute | solution.py:100
  131.6 3.8 %collective-permute-start.10 = (f32[4,8,128]{2,1,0:T(8,128)S(1)}, f32[4,8,128]{2,1,0:T(8,128)S(1)}, u32[]{:S(2)}, u32[]{:S(2)}) collective-permute-start(f32[4,8,128]{2,1,0:T(8,128)S(1)} %pad_maximum_fusion.7), channel_id=1, source_target_pairs={{0,2},{1,3},{2,0},{3,1},{4,6},{5,7},{6,4},{7,5},{8,10},{9,11},{10,... | collective-permute-start | bytes 49160 | tf_op jit(solution)/shard_map/ppermute | solution.py:100

commit v5 on v0

--- a/solution.py
+++ b/solution.py
@@ -14,9 +14,6 @@
 
 GRP_BITS = (2, 0, 1)
 BLK_BITS = (4, 3, 2, 1, 0)
-
-
-COL_SUB = 512
 
 
 def _accumulate(rows, rn, cols, w):
@@ -44,21 +41,22 @@
     scale_l = sl_ref[...]
     scale_d = sd_ref[...]
 
-    def one_block(b, carry):
+    group = 2 if x_ref.shape[0] % 2 == 0 else 1
+
+    def take(b, lo, width):
+        return jnp.concatenate([x_ref[b * group + i, :, lo:lo + width] for i in range(group)], 1)
+
+    def one_group(b, carry):
         acc_l, acc_d = carry
-        for c in range(0, nb, COL_SUB):
-            cols = x_ref[b, :, c:c + COL_SUB] * scale_l
-            w = x_ref[b, :, nb + c:nb + c + COL_SUB]
-            acc_l = acc_l + _accumulate(rows_l, rn_l, cols, w)
-        for c in range(0, nh, COL_SUB):
-            cols = x_ref[b, :, 2 * nb + c:2 * nb + c + COL_SUB] * scale_d
-            w = x_ref[b, :, 2 * nb + nh + c:2 * nb + nh + c + COL_SUB]
-            acc_d = acc_d + _accumulate(rows_d, rn_d, cols, w)
+        cols = take(b, 0, nb) * scale_l
+        acc_l = acc_l + _accumulate(rows_l, rn_l, cols, take(b, nb, nb))
+        cols = take(b, 2 * nb, nh) * scale_d
+        acc_d = acc_d + _accumulate(rows_d, rn_d, cols, take(b, 2 * nb + nh, nh))
         return acc_l, acc_d
 
     zero_l = jnp.zeros(ol_ref.shape, jnp.float32)
     zero_d = jnp.zeros(od_ref.shape, jnp.float32)
-    acc_l, acc_d = lax.fori_loop(0, x_ref.shape[0], one_block, (zero_l, zero_d))
+    acc_l, acc_d = lax.fori_loop(0, x_ref.shape[0] // group, one_group, (zero_l, zero_d))
     ol_ref[...] += acc_l
     od_ref[...] += acc_d
 

time: 143 us -> 129 us (0.902)
  Pallas kernels: 54.2 us -> 40.2 us
    pallas_call x6, Pallas kernels: 54.2 us -> 40.2 us  [apply_piece(): pl.pallas_call(kern, grid=(n // per,), in_specs=[full((rl, feats)), full(...]
  transfers between devices with their start and end apart: 11 -> 11, of which waited for: 10 -> 10; matrix products, arithmetic and copies ran while one was open for 4% -> 5% of each run, Pallas kernels for 21% -> 18%
where the time goes in v5:
time: 129 us
  waiting for transfers between devices  50.3 us (39%)
  Pallas kernels  40.2 us (31%)
  starting transfers between devices  21.8 us (17%)
  local copies, waits for them, and re-layouts  7.79 us (6%)
  other arithmetic  5.33 us (4%)
  matrix products  2.13 us (2%)
    pallas_call x6, Pallas kernels, apply_piece(): pl.pallas_call(kern, grid=(n // per,), in_specs=[full((rl, feats)), full(...  40.2 us
    ppermute x5, waiting for transfers between devices, per_device(): other = lax.ppermute(buf, 'blk', [(i, i ^ mask) for i in range(blk_size)])  33.6 us
    ppermute x6, waiting for transfers between devices, gather_bits(): other = lax.ppermute(buf, axis, [(i, i ^ mask) for i in range(size)])  16.7 us
    ppermute x6, starting transfers between devices, gather_bits(): other = lax.ppermute(buf, axis, [(i, i ^ mask) for i in range(size)])  11.8 us
    ppermute x5, starting transfers between devices, per_device(): other = lax.ppermute(buf, 'blk', [(i, i ^ mask) for i in range(blk_size)])  10 us
    unnamed x44, local copies, waits for them, and re-layouts  3.45 us
  transfers between devices with their start and end apart: 11, of which 10 were waited for; matrix products, arithmetic and copies ran while one was open for 5% of the time, Pallas kernels for 18%

profile of v5, /device:TPU:16, one launch (start us, length us, event | category | flops | bytes accessed | tf_op | source)
XLA Modules:
  0.0 128.5 jit_solution(10550759072847270328)
XLA Ops:
  0.6 0.8 reshape.60
  2.8 3.1 %collective-permute-start = (f32[1,2624]{1,0:T(1,128)S(1)}, f32[1,2624]{1,0:T(1,128)S(1)}, u32[]{:S(2)}, u32[]{:S(2)}) collective-permute-start(f32[1,2624]{1,0:T(1,128)S(1)} %broadcast_in_dim.10), channel_id=1, source_target_pairs={{0,4},{1,5},{2,6},{3,7},{4,0},{5,1},{6,2},{7,3},{8,12},{9,13},{10,... | collective-permute-start | bytes 31496 | tf_op jit(solution)/shard_map/ppermute | solution.py:96
  5.9 2.2 %collective-permute-done = f32[1,2624]{1,0:T(1,128)S(1)} collective-permute-done((f32[1,2624]{1,0:T(1,128)S(1)}, f32[1,2624]{1,0:T(1,128)S(1)}, u32[]{:S(2)}, u32[]{:S(2)}) %collective-permute-start) | collective-permute-done | bytes 10528 | tf_op jit(solution)/shard_map/ppermute | solution.py:96
  8.1 2.1 %collective-permute-start.1 = (f32[2,2624]{1,0:T(2,128)S(1)}, f32[2,2624]{1,0:T(2,128)S(1)}, u32[]{:S(2)}, u32[]{:S(2)}) collective-permute-start(f32[2,2624]{1,0:T(2,128)S(1)} %pad_maximum_fusion.6), channel_id=1, source_target_pairs={{0,1},{1,0},{2,3},{3,2},{4,5},{5,4},{6,7},{7,6},{8,9},{9,8},{10,11... | collective-permute-start | bytes 62984 | tf_op jit(solution)/shard_map/ppermute | solution.py:96
  10.2 3.3 %collective-permute-done.1 = f32[2,2624]{1,0:T(2,128)S(1)} collective-permute-done((f32[2,2624]{1,0:T(2,128)S(1)}, f32[2,2624]{1,0:T(2,128)S(1)}, u32[]{:S(2)}, u32[]{:S(2)}) %collective-permute-start.1) | collective-permute-done | bytes 21024 | tf_op jit(solution)/shard_map/ppermute | solution.py:96
  13.5 1.6 %collective-permute-start.2 = (f32[4,2624]{1,0:T(4,128)S(1)}, f32[4,2624]{1,0:T(4,128)S(1)}, u32[]{:S(2)}, u32[]{:S(2)}) collective-permute-start(f32[4,2624]{1,0:T(4,128)S(1)} %pad_maximum_fusion.4), channel_id=1, source_target_pairs={{0,2},{1,3},{2,0},{3,1},{4,6},{5,7},{6,4},{7,5},{8,10},{9,11},{10,... | collective-permute-start | bytes 125960 | tf_op jit(solution)/shard_map/ppermute | solution.py:96
  15.1 2.5 %collective-permute-done.2 = f32[4,2624]{1,0:T(4,128)S(1)} collective-permute-done((f32[4,2624]{1,0:T(4,128)S(1)}, f32[4,2624]{1,0:T(4,128)S(1)}, u32[]{:S(2)}, u32[]{:S(2)}) %collective-permute-start.2) | collective-permute-done | bytes 42016 | tf_op jit(solution)/shard_map/ppermute | solution.py:96
  18.2 0.7 fusion.1
  18.9 1.0 fusion
  20.0 7.3 %collective-permute-start.3 = (f32[1,8,3072]{2,1,0:T(8,128)S(1)}, f32[1,8,3072]{2,1,0:T(8,128)S(1)}, u32[]{:S(2)}, u32[]{:S(2)}) collective-permute-start(f32[1,8,3072]{2,1,0:T(8,128)S(1)} %maximum_bitcast_fusion.x_ref), channel_id=1, source_target_pairs={{0,128},{8,136},{16,144},{24,152},{32,160},{40,168},{48,176},{56,1... | collective-permute-start | bytes 294920 | tf_op jit(solution)/shard_map/ppermute | solution.py:162
  27.2 3.5 %collective-permute-done.3.x_ref = f32[1,8,3072]{2,1,0:T(8,128)S(1)} collective-permute-done((f32[1,8,3072]{2,1,0:T(8,128)S(1)}, f32[1,8,3072]{2,1,0:T(8,128)S(1)}, u32[]{:S(2)}, u32[]{:S(2)}) %collective-permute-start.3) | collective-permute-done | bytes 98336 | tf_op jit(solution)/shard_map/ppermute | solution.py:162
  30.8 1.3 %collective-permute-start.4 = (f32[2,8,3072]{2,1,0:T(8,128)S(1)}, f32[2,8,3072]{2,1,0:T(8,128)S(1)}, u32[]{:S(2)}, u32[]{:S(2)}) collective-permute-start(f32[2,8,3072]{2,1,0:T(8,128)S(1)} %pad_maximum_fusion.2), channel_id=1, source_target_pairs={{0,64},{8,72},{16,80},{24,88},{32,96},{40,104},{48,112},{56,120},{... | collective-permute-start | bytes 589832 | tf_op jit(solution)/shard_map/ppermute | solution.py:162
  32.0 7.7 %collective-permute-done.4.x_ref = f32[2,8,3072]{2,1,0:T(8,128)S(1)} collective-permute-done((f32[2,8,3072]{2,1,0:T(8,128)S(1)}, f32[2,8,3072]{2,1,0:T(8,128)S(1)}, u32[]{:S(2)}, u32[]{:S(2)}) %collective-permute-start.4) | collective-permute-done | bytes 196640 | tf_op jit(solution)/shard_map/ppermute | solution.py:162
  40.5 8.8 %collective-permute-done.5.x_ref = f32[4,8,3072]{2,1,0:T(8,128)S(1)} collective-permute-done((f32[4,8,3072]{2,1,0:T(8,128)S(1)}, f32[4,8,3072]{2,1,0:T(8,128)S(1)}, u32[]{:S(2)}, u32[]{:S(2)}) %collective-permute-start.5) | collective-permute-done | bytes 393248 | tf_op jit(solution)/shard_map/ppermute | solution.py:162
  49.4 1.4 %collective-permute-start.6 = (f32[8,8,3072]{2,1,0:T(8,128)S(1)}, f32[8,8,3072]{2,1,0:T(8,128)S(1)}, u32[]{:S(2)}, u32[]{:S(2)}) collective-permute-start(f32[8,8,3072]{2,1,0:T(8,128)S(1)} %pad_maximum_fusion), channel_id=1, source_target_pairs={{0,16},{8,24},{16,0},{24,8},{32,48},{40,56},{48,32},{56,40},{64,80... | collective-permute-start | bytes 2359304 | tf_op jit(solution)/shard_map/ppermute | solution.py:162
  52.1 0.8 constant_dynamic-update-slice_fusion.1
  52.9 13.6 %collective-permute-done.6.x_ref = f32[8,8,3072]{2,1,0:T(8,128)S(1)} collective-permute-done((f32[8,8,3072]{2,1,0:T(8,128)S(1)}, f32[8,8,3072]{2,1,0:T(8,128)S(1)}, u32[]{:S(2)}, u32[]{:S(2)}) %collective-permute-start.6) | collective-permute-done | bytes 786464 | tf_op jit(solution)/shard_map/ppermute | solution.py:162
  66.5 1.0 constant_dynamic-update-slice_fusion
  67.6 0.7 copy.62
  70.4 2.8 %shard_map.77 = (f32[8,128]{1,0:T(8,128)}, f32[8,64]{1,0:T(8,128)}) custom-call(f32[128,8]{1,0:T(8,128)} %bitcast.40, f32[64,8]{1,0:T(8,128)} %multiply_bitcast_fusion.rd_ref, f32[8,1]{1,0:T(8,128)} %copy.68.sl_ref, f32[8,1]{1,0:T(8,128)} %copy.69.sd_ref, f32[1,8,3072]{2,1,0:T(8,128)} %copy-done.3), custom_call_target="tpu_custom_call" | custom-call | tf_op jit(solution)/shard_map/pallas_call | solution.py:71
  73.2 2.8 %shard_map.78 = (f32[8,128]{1,0:T(8,128)}, f32[8,64]{1,0:T(8,128)}) custom-call(f32[128,8]{1,0:T(8,128)} %bitcast.41, f32[64,8]{1,0:T(8,128)} %multiply_bitcast_fusion.rd_ref, f32[8,1]{1,0:T(8,128)} %copy.68.sl_ref, f32[8,1]{1,0:T(8,128)} %copy.69.sd_ref, f32[1,8,3072]{2,1,0:T(8,128)} %copy-done.4), custom_call_target="tpu_custom_call" | custom-call | tf_op jit(solution)/shard_map/pallas_call | solution.py:71
  76.0 3.4 %shard_map.79 = (f32[8,128]{1,0:T(8,128)}, f32[8,64]{1,0:T(8,128)}) custom-call(f32[128,8]{1,0:T(8,128)} %bitcast.42, f32[64,8]{1,0:T(8,128)} %multiply_bitcast_fusion.rd_ref, f32[8,1]{1,0:T(8,128)} %copy.68.sl_ref, f32[8,1]{1,0:T(8,128)} %copy.69.sd_ref, f32[2,8,3072]{2,1,0:T(8,128)} %copy-done.2), custom_call_target="tpu_custom_call" | custom-call | tf_op jit(solution)/shard_map/pallas_call | solution.py:71
  79.4 5.5 %shard_map.80 = (f32[8,128]{1,0:T(8,128)}, f32[8,64]{1,0:T(8,128)}) custom-call(f32[128,8]{1,0:T(8,128)} %bitcast.43, f32[64,8]{1,0:T(8,128)} %multiply_bitcast_fusion.rd_ref, f32[8,1]{1,0:T(8,128)} %copy.68.sl_ref, f32[8,1]{1,0:T(8,128)} %copy.69.sd_ref, f32[4,8,3072]{2,1,0:T(8,128)} %copy-done), custom_call_target="tpu_custom_call" | custom-call | tf_op jit(solution)/shard_map/pallas_call | solution.py:71
  84.9 9.1 %shard_map.81 = (f32[8,128]{1,0:T(8,128)}, f32[8,64]{1,0:T(8,128)}) custom-call(f32[128,8]{1,0:T(8,128)} %bitcast.44, f32[64,8]{1,0:T(8,128)} %multiply_bitcast_fusion.rd_ref, f32[8,1]{1,0:T(8,128)} %copy.68.sl_ref, f32[8,1]{1,0:T(8,128)} %copy.69.sd_ref, f32[8,8,3072]{2,1,0:T(8,128)} %copy-done.1), custom_call_target="tpu_custom_call" | custom-call | tf_op jit(solution)/shard_map/pallas_call | solution.py:71
  94.1 1.2 copy-done.5
  95.3 16.7 %shard_map.82 = (f32[8,128]{1,0:T(8,128)}, f32[8,64]{1,0:T(8,128)}) custom-call(f32[128,8]{1,0:T(8,128)} %bitcast.45, f32[64,8]{1,0:T(8,128)} %multiply_bitcast_fusion.rd_ref, f32[8,1]{1,0:T(8,128)} %copy.68.sl_ref, f32[8,1]{1,0:T(8,128)} %copy.69.sd_ref, f32[16,8,3072]{2,1,0:T(8,128)} %copy-done.5), custom_call_target="tpu_custom_call" | custom-call | tf_op jit(solution)/shard_map/pallas_call | solution.py:71
  112.7 3.0 %collective-permute-start.8 = (f32[1,8,128]{2,1,0:T(8,128)S(1)}, f32[1,8,128]{2,1,0:T(8,128)S(1)}, u32[]{:S(2)}, u32[]{:S(2)}) collective-permute-start(f32[1,8,128]{2,1,0:T(8,128)S(1)} %bitcast.52), channel_id=1, source_target_pairs={{0,4},{1,5},{2,6},{3,7},{4,0},{5,1},{6,2},{7,3},{8,12},{9,13},{10,... | collective-permute-start | bytes 12296 | tf_op jit(solution)/shard_map/ppermute | solution.py:96
  115.7 2.1 %collective-permute-done.8 = f32[1,8,128]{2,1,0:T(8,128)S(1)} collective-permute-done((f32[1,8,128]{2,1,0:T(8,128)S(1)}, f32[1,8,128]{2,1,0:T(8,128)S(1)}, u32[]{:S(2)}, u32[]{:S(2)}) %collective-permute-start.8) | collective-permute-done | bytes 4128 | tf_op jit(solution)/shard_map/ppermute | solution.py:96
  118.1 4.8 %collective-permute-done.9 = f32[2,8,128]{2,1,0:T(8,128)S(1)} collective-permute-done((f32[2,8,128]{2,1,0:T(8,128)S(1)}, f32[2,8,128]{2,1,0:T(8,128)S(1)}, u32[]{:S(2)}, u32[]{:S(2)}) %collective-permute-start.9) | collective-permute-done | bytes 8224 | tf_op jit(solution)/shard_map/ppermute | solution.py:96
  123.0 1.6 %collective-permute-start.10 = (f32[4,8,128]{2,1,0:T(8,128)S(1)}, f32[4,8,128]{2,1,0:T(8,128)S(1)}, u32[]{:S(2)}, u32[]{:S(2)}) collective-permute-start(f32[4,8,128]{2,1,0:T(8,128)S(1)} %pad_maximum_fusion.7), channel_id=1, source_target_pairs={{0,2},{1,3},{2,0},{3,1},{4,6},{5,7},{6,4},{7,5},{8,10},{9,11},{10,... | collective-permute-start | bytes 49160 | tf_op jit(solution)/shard_map/ppermute | solution.py:96
  124.9 1.8 %collective-permute-done.10 = f32[4,8,128]{2,1,0:T(8,128)S(1)} collective-permute-done((f32[4,8,128]{2,1,0:T(8,128)S(1)}, f32[4,8,128]{2,1,0:T(8,128)S(1)}, u32[]{:S(2)}, u32[]{:S(2)}) %collective-permute-start.10) | collective-permute-done | bytes 16416 | tf_op jit(solution)/shard_map/ppermute | solution.py:96
  127.2 1.3 %add_add_fusion = f32[8,64]{1,0:T(8,128)} fusion(f32[8,64]{1,0:T(8,128)S(1)} %convolution_multiply_fusion.1, f32[8,64]{1,0:T(8,128)} %get-tuple-element.25, f32[8,64]{1,0:T(8,128)S(1)} %copy-done.17, f32[8,64]{1,0:T(8,128)S(1)} %copy-done.16, f32[8,64]{1,0:T(8,128)S(1)} %copy-done.15, f32[8,64]{1,0:T(8,128)S(1)} %copy-done.13, f32[8,64]{1,0:T(8,128)S(1)} %copy-done.14), kind=kLoop, calls=%fused_computation.38 | loop fusion | flops 3072 | bytes 16384 | tf_op jit(solution)/shard_map/add | solution.py:173
  (86 shorter events, 8.2 us)
Async XLA Ops:
  2.8 5.3 %collective-permute-start = (f32[1,2624]{1,0:T(1,128)S(1)}, f32[1,2624]{1,0:T(1,128)S(1)}, u32[]{:S(2)}, u32[]{:S(2)}) collective-permute-start(f32[1,2624]{1,0:T(1,128)S(1)} %broadcast_in_dim.10), channel_id=1, source_target_pairs={{0,4},{1,5},{2,6},{3,7},{4,0},{5,1},{6,2},{7,3},{8,12},{9,13},{10,... | collective-permute-start | bytes 31496 | tf_op jit(solution)/shard_map/ppermute | solution.py:96
  8.1 5.4 %collective-permute-start.1 = (f32[2,2624]{1,0:T(2,128)S(1)}, f32[2,2624]{1,0:T(2,128)S(1)}, u32[]{:S(2)}, u32[]{:S(2)}) collective-permute-start(f32[2,2624]{1,0:T(2,128)S(1)} %pad_maximum_fusion.6), channel_id=1, source_target_pairs={{0,1},{1,0},{2,3},{3,2},{4,5},{5,4},{6,7},{7,6},{8,9},{9,8},{10,11... | collective-permute-start | bytes 62984 | tf_op jit(solution)/shard_map/ppermute | solution.py:96
  13.5 4.1 %collective-permute-start.2 = (f32[4,2624]{1,0:T(4,128)S(1)}, f32[4,2624]{1,0:T(4,128)S(1)}, u32[]{:S(2)}, u32[]{:S(2)}) collective-permute-start(f32[4,2624]{1,0:T(4,128)S(1)} %pad_maximum_fusion.4), channel_id=1, source_target_pairs={{0,2},{1,3},{2,0},{3,1},{4,6},{5,7},{6,4},{7,5},{8,10},{9,11},{10,... | collective-permute-start | bytes 125960 | tf_op jit(solution)/shard_map/ppermute | solution.py:96
  20.0 31.5 %copy-start.3 = (f32[1,8,3072]{2,1,0:T(8,128)}, f32[1,8,3072]{2,1,0:T(8,128)S(1)}, u32[]{:S(2)}) copy-start(f32[1,8,3072]{2,1,0:T(8,128)S(1)} %maximum_bitcast_fusion.x_ref) | copy-start | bytes 294916
  20.0 10.8 %collective-permute-start.3 = (f32[1,8,3072]{2,1,0:T(8,128)S(1)}, f32[1,8,3072]{2,1,0:T(8,128)S(1)}, u32[]{:S(2)}, u32[]{:S(2)}) collective-permute-start(f32[1,8,3072]{2,1,0:T(8,128)S(1)} %maximum_bitcast_fusion.x_ref), channel_id=1, source_target_pairs={{0,128},{8,136},{16,144},{24,152},{32,160},{40,168},{48,176},{56,1... | collective-permute-start | bytes 294920 | tf_op jit(solution)/shard_map/ppermute | solution.py:162
  30.7 20.7 %copy-start.4 = (f32[1,8,3072]{2,1,0:T(8,128)}, f32[1,8,3072]{2,1,0:T(8,128)S(1)}, u32[]{:S(2)}) copy-start(f32[1,8,3072]{2,1,0:T(8,128)S(1)} %collective-permute-done.3.x_ref) | copy-start | bytes 294916
  30.8 9.0 %collective-permute-start.4 = (f32[2,8,3072]{2,1,0:T(8,128)S(1)}, f32[2,8,3072]{2,1,0:T(8,128)S(1)}, u32[]{:S(2)}, u32[]{:S(2)}) collective-permute-start(f32[2,8,3072]{2,1,0:T(8,128)S(1)} %pad_maximum_fusion.2), channel_id=1, source_target_pairs={{0,64},{8,72},{16,80},{24,88},{32,96},{40,104},{48,112},{56,120},{... | collective-permute-start | bytes 589832 | tf_op jit(solution)/shard_map/ppermute | solution.py:162
  39.8 12.4 %copy-start.2 = (f32[2,8,3072]{2,1,0:T(8,128)}, f32[2,8,3072]{2,1,0:T(8,128)S(1)}, u32[]{:S(2)}) copy-start(f32[2,8,3072]{2,1,0:T(8,128)S(1)} %collective-permute-done.4.x_ref) | copy-start | bytes 589828
  39.8 9.5 %collective-permute-start.5 = (f32[4,8,3072]{2,1,0:T(8,128)S(1)}, f32[4,8,3072]{2,1,0:T(8,128)S(1)}, u32[]{:S(2)}, u32[]{:S(2)}) collective-permute-start(f32[4,8,3072]{2,1,0:T(8,128)S(1)} %pad_maximum_fusion.1), channel_id=1, source_target_pairs={{0,32},{8,40},{16,48},{24,56},{32,0},{40,8},{48,16},{56,24},{64,96... | collective-permute-start | bytes 1179656 | tf_op jit(solution)/shard_map/ppermute | solution.py:162
  49.3 18.2 %copy-start = (f32[4,8,3072]{2,1,0:T(8,128)}, f32[4,8,3072]{2,1,0:T(8,128)S(1)}, u32[]{:S(2)}) copy-start(f32[4,8,3072]{2,1,0:T(8,128)S(1)} %collective-permute-done.5.x_ref) | copy-start | bytes 1179652
  49.4 18.1 %copy-start.7 = (f32[8,128]{1,0:T(8,128)S(1)}, f32[8,128]{1,0:T(8,128)}, u32[]{:S(2)}) copy-start(f32[8,128]{1,0:T(8,128)} %param.6) | copy-start | bytes 12292
  49.4 18.1 %copy-start.19 = (f32[8]{0:T(128)S(1)}, f32[8]{0:T(128)}, u32[]{:S(2)}) copy-start(f32[8]{0:T(128)} %param.10) | copy-start | bytes 100
  49.4 19.6 %copy-start.18 = (f32[8]{0:T(128)S(1)}, f32[8]{0:T(128)}, u32[]{:S(2)}) copy-start(f32[8]{0:T(128)} %param.11) | copy-start | bytes 100
  49.4 17.1 %collective-permute-start.6 = (f32[8,8,3072]{2,1,0:T(8,128)S(1)}, f32[8,8,3072]{2,1,0:T(8,128)S(1)}, u32[]{:S(2)}, u32[]{:S(2)}) collective-permute-start(f32[8,8,3072]{2,1,0:T(8,128)S(1)} %pad_maximum_fusion), channel_id=1, source_target_pairs={{0,16},{8,24},{16,0},{24,8},{32,48},{40,56},{48,32},{56,40},{64,80... | collective-permute-start | bytes 2359304 | tf_op jit(solution)/shard_map/ppermute | solution.py:162
  66.5 18.4 %copy-start.1 = (f32[8,8,3072]{2,1,0:T(8,128)}, f32[8,8,3072]{2,1,0:T(8,128)S(1)}, u32[]{:S(2)}) copy-start(f32[8,8,3072]{2,1,0:T(8,128)S(1)} %collective-permute-done.6.x_ref) | copy-start | bytes 2359300
  67.5 26.6 %collective-permute-start.7 = (f32[16,8,3072]{2,1,0:T(8,128)}, f32[16,8,3072]{2,1,0:T(8,128)S(1)}, u32[]{:S(2)}, u32[]{:S(2)}) collective-permute-start(f32[16,8,3072]{2,1,0:T(8,128)} %constant_dynamic-update-slice_fusion), channel_id=1, source_target_pairs={{0,8},{8,0},{16,24},{24,16},{32,40},{40,32},{48,56},{56,48},{64,72... | collective-permute-start | bytes 4718600 | tf_op jit(solution)/shard_map/ppermute | solution.py:162
  79.4 32.5 %copy-start.8 = (f32[8,128]{1,0:T(8,128)S(1)}, f32[8,128]{1,0:T(8,128)}, u32[]{:S(2)}) copy-start(f32[8,128]{1,0:T(8,128)} %get-tuple-element.14) | copy-start | bytes 12292
  79.4 32.5 %copy-start.9 = (f32[8,128]{1,0:T(8,128)S(1)}, f32[8,128]{1,0:T(8,128)}, u32[]{:S(2)}) copy-start(f32[8,128]{1,0:T(8,128)} %get-tuple-element.15) | copy-start | bytes 12292
  79.4 32.5 %copy-start.10 = (f32[8,128]{1,0:T(8,128)S(1)}, f32[8,128]{1,0:T(8,128)}, u32[]{:S(2)}) copy-start(f32[8,128]{1,0:T(8,128)} %get-tuple-element.16) | copy-start | bytes 12292
  84.9 27.1 %copy-start.11 = (f32[8,128]{1,0:T(8,128)S(1)}, f32[8,128]{1,0:T(8,128)}, u32[]{:S(2)}) copy-start(f32[8,128]{1,0:T(8,128)} %get-tuple-element.17) | copy-start | bytes 12292
  94.0 17.9 %copy-start.12 = (f32[8,128]{1,0:T(8,128)S(1)}, f32[8,128]{1,0:T(8,128)}, u32[]{:S(2)}) copy-start(f32[8,128]{1,0:T(8,128)} %get-tuple-element.18) | copy-start | bytes 12292
  94.0 33.1 %copy-start.13 = (f32[8,64]{1,0:T(8,128)S(1)}, f32[8,64]{1,0:T(8,128)}, u32[]{:S(2)}) copy-start(f32[8,64]{1,0:T(8,128)} %get-tuple-element.20) | copy-start | bytes 6148
  94.0 33.1 %copy-start.14 = (f32[8,64]{1,0:T(8,128)S(1)}, f32[8,64]{1,0:T(8,128)}, u32[]{:S(2)}) copy-start(f32[8,64]{1,0:T(8,128)} %get-tuple-element.21) | copy-start | bytes 6148
  94.1 33.1 %copy-start.15 = (f32[8,64]{1,0:T(8,128)S(1)}, f32[8,64]{1,0:T(8,128)}, u32[]{:S(2)}) copy-start(f32[8,64]{1,0:T(8,128)} %get-tuple-element.22) | copy-start | bytes 6148
  94.1 33.1 %copy-start.16 = (f32[8,64]{1,0:T(8,128)S(1)}, f32[8,64]{1,0:T(8,128)}, u32[]{:S(2)}) copy-start(f32[8,64]{1,0:T(8,128)} %get-tuple-element.23) | copy-start | bytes 6148
  94.1 33.1 %copy-start.17 = (f32[8,64]{1,0:T(8,128)S(1)}, f32[8,64]{1,0:T(8,128)}, u32[]{:S(2)}) copy-start(f32[8,64]{1,0:T(8,128)} %get-tuple-element.24) | copy-start | bytes 6148
  94.1 1.2 copy-start.5
  112.7 15.9 %copy-start.6 = (f32[8,128]{1,0:T(8,128)}, f32[8,128]{1,0:T(8,128)S(1)}, u32[]{:S(2)}) copy-start(f32[8,128]{1,0:T(8,128)S(1)} %add_add_fusion.1) | copy-start | bytes 12292
  112.7 5.1 %collective-permute-start.8 = (f32[1,8,128]{2,1,0:T(8,128)S(1)}, f32[1,8,128]{2,1,0:T(8,128)S(1)}, u32[]{:S(2)}, u32[]{:S(2)}) collective-permute-start(f32[1,8,128]{2,1,0:T(8,128)S(1)} %bitcast.52), channel_id=1, source_target_pairs={{0,4},{1,5},{2,6},{3,7},{4,0},{5,1},{6,2},{7,3},{8,12},{9,13},{10,... | collective-permute-start | bytes 12296 | tf_op jit(solution)/shard_map/ppermute | solution.py:96
  117.8 5.2 %collective-permute-start.9 = (f32[2,8,128]{2,1,0:T(8,128)S(1)}, f32[2,8,128]{2,1,0:T(8,128)S(1)}, u32[]{:S(2)}, u32[]{:S(2)}) collective-permute-start(f32[2,8,128]{2,1,0:T(8,128)S(1)} %pad_maximum_fusion.9), channel_id=1, source_target_pairs={{0,1},{1,0},{2,3},{3,2},{4,5},{5,4},{6,7},{7,6},{8,9},{9,8},{10,11... | collective-permute-start | bytes 24584 | tf_op jit(solution)/shard_map/ppermute | solution.py:96
  123.0 3.8 %collective-permute-start.10 = (f32[4,8,128]{2,1,0:T(8,128)S(1)}, f32[4,8,128]{2,1,0:T(8,128)S(1)}, u32[]{:S(2)}, u32[]{:S(2)}) collective-permute-start(f32[4,8,128]{2,1,0:T(8,128)S(1)} %pad_maximum_fusion.7), channel_id=1, source_target_pairs={{0,2},{1,3},{2,0},{3,1},{4,6},{5,7},{6,4},{7,5},{8,10},{9,11},{10,... | collective-permute-start | bytes 49160 | tf_op jit(solution)/shard_map/ppermute | solution.py:96

commit v6 on v5

--- a/solution.py
+++ b/solution.py
@@ -1,4 +1,5 @@
 import functools
+import math
 
 import jax
 import jax.numpy as jnp
@@ -41,7 +42,7 @@
     scale_l = sl_ref[...]
     scale_d = sd_ref[...]
 
-    group = 2 if x_ref.shape[0] % 2 == 0 else 1
+    group = math.gcd(x_ref.shape[0], 8)
 
     def take(b, lo, width):
         return jnp.concatenate([x_ref[b * group + i, :, lo:lo + width] for i in range(group)], 1)
@@ -64,7 +65,7 @@
 def apply_piece(rows_low, rows_diff, inv_len_low, inv_len_diff, piece, nb, nh, interpret=False):
     n, feats, width = piece.shape
     probes = piece.shape[1]
-    per = min(n, 4)
+    per = min(n, 8)
     rl, rd = rows_low.shape[1], rows_diff.shape[1]
     kern = functools.partial(_piece_kernel, nb=nb, nh=nh)
     full = lambda shape: pl.BlockSpec(shape, lambda j: (0,) * len(shape))

time: 129 us -> 126 us (0.977)
  Pallas kernels: 40.2 us -> 37.2 us
    pallas_call x6, Pallas kernels: 40.2 us -> 37.2 us  [apply_piece(): pl.pallas_call(kern, grid=(n // per,), in_specs=[full((rl, feats)), full(...]
where the time goes in v6:
time: 126 us; the launch traced here: 125 us
  waiting for transfers between devices  50.3 us (40%)
  Pallas kernels  37.2 us (30%)
  starting transfers between devices  21.8 us (17%)
  local copies, waits for them, and re-layouts  7.79 us (6%)
  other arithmetic  5.33 us (4%)
  matrix products  2.13 us (2%)
    pallas_call x6, Pallas kernels, apply_piece(): pl.pallas_call(kern, grid=(n // per,), in_specs=[full((rl, feats)), full(...  37.2 us
    ppermute x5, waiting for transfers between devices, per_device(): other = lax.ppermute(buf, 'blk', [(i, i ^ mask) for i in range(blk_size)])  33.6 us
    ppermute x6, waiting for transfers between devices, gather_bits(): other = lax.ppermute(buf, axis, [(i, i ^ mask) for i in range(size)])  16.7 us
    ppermute x6, starting transfers between devices, gather_bits(): other = lax.ppermute(buf, axis, [(i, i ^ mask) for i in range(size)])  11.8 us
    ppermute x5, starting transfers between devices, per_device(): other = lax.ppermute(buf, 'blk', [(i, i ^ mask) for i in range(blk_size)])  10 us
    unnamed x44, local copies, waits for them, and re-layouts  3.45 us
  transfers between devices with their start and end apart: 11, of which 10 were waited for; matrix products, arithmetic and copies ran while one was open for 5% of the time, Pallas kernels for 18%

profile of v6, /device:TPU:16, one launch (start us, length us, event | category | flops | bytes accessed | tf_op | source)
XLA Modules:
  0.0 125.5 jit_solution(9667459528049150173)
XLA Ops:
  0.6 0.8 reshape.60
  2.8 3.1 %collective-permute-start = (f32[1,2624]{1,0:T(1,128)S(1)}, f32[1,2624]{1,0:T(1,128)S(1)}, u32[]{:S(2)}, u32[]{:S(2)}) collective-permute-start(f32[1,2624]{1,0:T(1,128)S(1)} %broadcast_in_dim.10), channel_id=1, source_target_pairs={{0,4},{1,5},{2,6},{3,7},{4,0},{5,1},{6,2},{7,3},{8,12},{9,13},{10,... | collective-permute-start | bytes 31496 | tf_op jit(solution)/shard_map/ppermute | solution.py:97
  5.9 2.2 %collective-permute-done = f32[1,2624]{1,0:T(1,128)S(1)} collective-permute-done((f32[1,2624]{1,0:T(1,128)S(1)}, f32[1,2624]{1,0:T(1,128)S(1)}, u32[]{:S(2)}, u32[]{:S(2)}) %collective-permute-start) | collective-permute-done | bytes 10528 | tf_op jit(solution)/shard_map/ppermute | solution.py:97
  8.1 2.1 %collective-permute-start.1 = (f32[2,2624]{1,0:T(2,128)S(1)}, f32[2,2624]{1,0:T(2,128)S(1)}, u32[]{:S(2)}, u32[]{:S(2)}) collective-permute-start(f32[2,2624]{1,0:T(2,128)S(1)} %pad_maximum_fusion.6), channel_id=1, source_target_pairs={{0,1},{1,0},{2,3},{3,2},{4,5},{5,4},{6,7},{7,6},{8,9},{9,8},{10,11... | collective-permute-start | bytes 62984 | tf_op jit(solution)/shard_map/ppermute | solution.py:97
  10.2 3.3 %collective-permute-done.1 = f32[2,2624]{1,0:T(2,128)S(1)} collective-permute-done((f32[2,2624]{1,0:T(2,128)S(1)}, f32[2,2624]{1,0:T(2,128)S(1)}, u32[]{:S(2)}, u32[]{:S(2)}) %collective-permute-start.1) | collective-permute-done | bytes 21024 | tf_op jit(solution)/shard_map/ppermute | solution.py:97
  13.5 1.6 %collective-permute-start.2 = (f32[4,2624]{1,0:T(4,128)S(1)}, f32[4,2624]{1,0:T(4,128)S(1)}, u32[]{:S(2)}, u32[]{:S(2)}) collective-permute-start(f32[4,2624]{1,0:T(4,128)S(1)} %pad_maximum_fusion.4), channel_id=1, source_target_pairs={{0,2},{1,3},{2,0},{3,1},{4,6},{5,7},{6,4},{7,5},{8,10},{9,11},{10,... | collective-permute-start | bytes 125960 | tf_op jit(solution)/shard_map/ppermute | solution.py:97
  15.1 2.5 %collective-permute-done.2 = f32[4,2624]{1,0:T(4,128)S(1)} collective-permute-done((f32[4,2624]{1,0:T(4,128)S(1)}, f32[4,2624]{1,0:T(4,128)S(1)}, u32[]{:S(2)}, u32[]{:S(2)}) %collective-permute-start.2) | collective-permute-done | bytes 42016 | tf_op jit(solution)/shard_map/ppermute | solution.py:97
  18.2 0.7 fusion.1
  18.9 1.0 fusion
  20.0 7.3 %collective-permute-start.3 = (f32[1,8,3072]{2,1,0:T(8,128)S(1)}, f32[1,8,3072]{2,1,0:T(8,128)S(1)}, u32[]{:S(2)}, u32[]{:S(2)}) collective-permute-start(f32[1,8,3072]{2,1,0:T(8,128)S(1)} %maximum_bitcast_fusion.x_ref), channel_id=1, source_target_pairs={{0,128},{8,136},{16,144},{24,152},{32,160},{40,168},{48,176},{56,1... | collective-permute-start | bytes 294920 | tf_op jit(solution)/shard_map/ppermute | solution.py:163
  27.2 3.5 %collective-permute-done.3.x_ref = f32[1,8,3072]{2,1,0:T(8,128)S(1)} collective-permute-done((f32[1,8,3072]{2,1,0:T(8,128)S(1)}, f32[1,8,3072]{2,1,0:T(8,128)S(1)}, u32[]{:S(2)}, u32[]{:S(2)}) %collective-permute-start.3) | collective-permute-done | bytes 98336 | tf_op jit(solution)/shard_map/ppermute | solution.py:163
  30.8 1.3 %collective-permute-start.4 = (f32[2,8,3072]{2,1,0:T(8,128)S(1)}, f32[2,8,3072]{2,1,0:T(8,128)S(1)}, u32[]{:S(2)}, u32[]{:S(2)}) collective-permute-start(f32[2,8,3072]{2,1,0:T(8,128)S(1)} %pad_maximum_fusion.2), channel_id=1, source_target_pairs={{0,64},{8,72},{16,80},{24,88},{32,96},{40,104},{48,112},{56,120},{... | collective-permute-start | bytes 589832 | tf_op jit(solution)/shard_map/ppermute | solution.py:163
  32.0 7.7 %collective-permute-done.4.x_ref = f32[2,8,3072]{2,1,0:T(8,128)S(1)} collective-permute-done((f32[2,8,3072]{2,1,0:T(8,128)S(1)}, f32[2,8,3072]{2,1,0:T(8,128)S(1)}, u32[]{:S(2)}, u32[]{:S(2)}) %collective-permute-start.4) | collective-permute-done | bytes 196640 | tf_op jit(solution)/shard_map/ppermute | solution.py:163
  40.5 8.8 %collective-permute-done.5.x_ref = f32[4,8,3072]{2,1,0:T(8,128)S(1)} collective-permute-done((f32[4,8,3072]{2,1,0:T(8,128)S(1)}, f32[4,8,3072]{2,1,0:T(8,128)S(1)}, u32[]{:S(2)}, u32[]{:S(2)}) %collective-permute-start.5) | collective-permute-done | bytes 393248 | tf_op jit(solution)/shard_map/ppermute | solution.py:163
  49.4 1.4 %collective-permute-start.6 = (f32[8,8,3072]{2,1,0:T(8,128)S(1)}, f32[8,8,3072]{2,1,0:T(8,128)S(1)}, u32[]{:S(2)}, u32[]{:S(2)}) collective-permute-start(f32[8,8,3072]{2,1,0:T(8,128)S(1)} %pad_maximum_fusion), channel_id=1, source_target_pairs={{0,16},{8,24},{16,0},{24,8},{32,48},{40,56},{48,32},{56,40},{64,80... | collective-permute-start | bytes 2359304 | tf_op jit(solution)/shard_map/ppermute | solution.py:163
  52.1 0.8 constant_dynamic-update-slice_fusion.1
  52.9 13.6 %collective-permute-done.6.x_ref = f32[8,8,3072]{2,1,0:T(8,128)S(1)} collective-permute-done((f32[8,8,3072]{2,1,0:T(8,128)S(1)}, f32[8,8,3072]{2,1,0:T(8,128)S(1)}, u32[]{:S(2)}, u32[]{:S(2)}) %collective-permute-start.6) | collective-permute-done | bytes 786464 | tf_op jit(solution)/shard_map/ppermute | solution.py:163
  66.5 1.0 constant_dynamic-update-slice_fusion
  67.6 0.7 copy.62
  70.4 2.8 %shard_map.77 = (f32[8,128]{1,0:T(8,128)}, f32[8,64]{1,0:T(8,128)}) custom-call(f32[128,8]{1,0:T(8,128)} %bitcast.40, f32[64,8]{1,0:T(8,128)} %multiply_bitcast_fusion.rd_ref, f32[8,1]{1,0:T(8,128)} %copy.68.sl_ref, f32[8,1]{1,0:T(8,128)} %copy.69.sd_ref, f32[1,8,3072]{2,1,0:T(8,128)} %copy-done.3), custom_call_target="tpu_custom_call" | custom-call | tf_op jit(solution)/shard_map/pallas_call | solution.py:72
  73.2 2.8 %shard_map.78 = (f32[8,128]{1,0:T(8,128)}, f32[8,64]{1,0:T(8,128)}) custom-call(f32[128,8]{1,0:T(8,128)} %bitcast.41, f32[64,8]{1,0:T(8,128)} %multiply_bitcast_fusion.rd_ref, f32[8,1]{1,0:T(8,128)} %copy.68.sl_ref, f32[8,1]{1,0:T(8,128)} %copy.69.sd_ref, f32[1,8,3072]{2,1,0:T(8,128)} %copy-done.4), custom_call_target="tpu_custom_call" | custom-call | tf_op jit(solution)/shard_map/pallas_call | solution.py:72
  76.0 3.4 %shard_map.79 = (f32[8,128]{1,0:T(8,128)}, f32[8,64]{1,0:T(8,128)}) custom-call(f32[128,8]{1,0:T(8,128)} %bitcast.42, f32[64,8]{1,0:T(8,128)} %multiply_bitcast_fusion.rd_ref, f32[8,1]{1,0:T(8,128)} %copy.68.sl_ref, f32[8,1]{1,0:T(8,128)} %copy.69.sd_ref, f32[2,8,3072]{2,1,0:T(8,128)} %copy-done.2), custom_call_target="tpu_custom_call" | custom-call | tf_op jit(solution)/shard_map/pallas_call | solution.py:72
  79.4 5.0 %shard_map.80 = (f32[8,128]{1,0:T(8,128)}, f32[8,64]{1,0:T(8,128)}) custom-call(f32[128,8]{1,0:T(8,128)} %bitcast.43, f32[64,8]{1,0:T(8,128)} %multiply_bitcast_fusion.rd_ref, f32[8,1]{1,0:T(8,128)} %copy.68.sl_ref, f32[8,1]{1,0:T(8,128)} %copy.69.sd_ref, f32[4,8,3072]{2,1,0:T(8,128)} %copy-done), custom_call_target="tpu_custom_call" | custom-call | tf_op jit(solution)/shard_map/pallas_call | solution.py:72
  84.4 8.5 %shard_map.81 = (f32[8,128]{1,0:T(8,128)}, f32[8,64]{1,0:T(8,128)}) custom-call(f32[128,8]{1,0:T(8,128)} %bitcast.44, f32[64,8]{1,0:T(8,128)} %multiply_bitcast_fusion.rd_ref, f32[8,1]{1,0:T(8,128)} %copy.68.sl_ref, f32[8,1]{1,0:T(8,128)} %copy.69.sd_ref, f32[8,8,3072]{2,1,0:T(8,128)} %copy-done.1), custom_call_target="tpu_custom_call" | custom-call | tf_op jit(solution)/shard_map/pallas_call | solution.py:72
  93.0 1.2 copy-done.5
  94.2 14.7 %shard_map.82 = (f32[8,128]{1,0:T(8,128)}, f32[8,64]{1,0:T(8,128)}) custom-call(f32[128,8]{1,0:T(8,128)} %bitcast.45, f32[64,8]{1,0:T(8,128)} %multiply_bitcast_fusion.rd_ref, f32[8,1]{1,0:T(8,128)} %copy.68.sl_ref, f32[8,1]{1,0:T(8,128)} %copy.69.sd_ref, f32[16,8,3072]{2,1,0:T(8,128)} %copy-done.5), custom_call_target="tpu_custom_call" | custom-call | tf_op jit(solution)/shard_map/pallas_call | solution.py:72
  109.6 3.0 %collective-permute-start.8 = (f32[1,8,128]{2,1,0:T(8,128)S(1)}, f32[1,8,128]{2,1,0:T(8,128)S(1)}, u32[]{:S(2)}, u32[]{:S(2)}) collective-permute-start(f32[1,8,128]{2,1,0:T(8,128)S(1)} %bitcast.52), channel_id=1, source_target_pairs={{0,4},{1,5},{2,6},{3,7},{4,0},{5,1},{6,2},{7,3},{8,12},{9,13},{10,... | collective-permute-start | bytes 12296 | tf_op jit(solution)/shard_map/ppermute | solution.py:97
  112.7 2.1 %collective-permute-done.8 = f32[1,8,128]{2,1,0:T(8,128)S(1)} collective-permute-done((f32[1,8,128]{2,1,0:T(8,128)S(1)}, f32[1,8,128]{2,1,0:T(8,128)S(1)}, u32[]{:S(2)}, u32[]{:S(2)}) %collective-permute-start.8) | collective-permute-done | bytes 4128 | tf_op jit(solution)/shard_map/ppermute | solution.py:97
  115.1 4.8 %collective-permute-done.9 = f32[2,8,128]{2,1,0:T(8,128)S(1)} collective-permute-done((f32[2,8,128]{2,1,0:T(8,128)S(1)}, f32[2,8,128]{2,1,0:T(8,128)S(1)}, u32[]{:S(2)}, u32[]{:S(2)}) %collective-permute-start.9) | collective-permute-done | bytes 8224 | tf_op jit(solution)/shard_map/ppermute | solution.py:97
  119.9 1.6 %collective-permute-start.10 = (f32[4,8,128]{2,1,0:T(8,128)S(1)}, f32[4,8,128]{2,1,0:T(8,128)S(1)}, u32[]{:S(2)}, u32[]{:S(2)}) collective-permute-start(f32[4,8,128]{2,1,0:T(8,128)S(1)} %pad_maximum_fusion.7), channel_id=1, source_target_pairs={{0,2},{1,3},{2,0},{3,1},{4,6},{5,7},{6,4},{7,5},{8,10},{9,11},{10,... | collective-permute-start | bytes 49160 | tf_op jit(solution)/shard_map/ppermute | solution.py:97
  121.9 1.9 %collective-permute-done.10 = f32[4,8,128]{2,1,0:T(8,128)S(1)} collective-permute-done((f32[4,8,128]{2,1,0:T(8,128)S(1)}, f32[4,8,128]{2,1,0:T(8,128)S(1)}, u32[]{:S(2)}, u32[]{:S(2)}) %collective-permute-start.10) | collective-permute-done | bytes 16416 | tf_op jit(solution)/shard_map/ppermute | solution.py:97
  124.2 1.3 %add_add_fusion = f32[8,64]{1,0:T(8,128)} fusion(f32[8,64]{1,0:T(8,128)S(1)} %convolution_multiply_fusion.1, f32[8,64]{1,0:T(8,128)} %get-tuple-element.25, f32[8,64]{1,0:T(8,128)S(1)} %copy-done.17, f32[8,64]{1,0:T(8,128)S(1)} %copy-done.16, f32[8,64]{1,0:T(8,128)S(1)} %copy-done.15, f32[8,64]{1,0:T(8,128)S(1)} %copy-done.13, f32[8,64]{1,0:T(8,128)S(1)} %copy-done.14), kind=kLoop, calls=%fused_computation.38 | loop fusion | flops 3072 | bytes 16384 | tf_op jit(solution)/shard_map/add | solution.py:174
  (86 shorter events, 8.2 us)
Async XLA Ops:
  2.8 5.3 %collective-permute-start = (f32[1,2624]{1,0:T(1,128)S(1)}, f32[1,2624]{1,0:T(1,128)S(1)}, u32[]{:S(2)}, u32[]{:S(2)}) collective-permute-start(f32[1,2624]{1,0:T(1,128)S(1)} %broadcast_in_dim.10), channel_id=1, source_target_pairs={{0,4},{1,5},{2,6},{3,7},{4,0},{5,1},{6,2},{7,3},{8,12},{9,13},{10,... | collective-permute-start | bytes 31496 | tf_op jit(solution)/shard_map/ppermute | solution.py:97
  8.1 5.4 %collective-permute-start.1 = (f32[2,2624]{1,0:T(2,128)S(1)}, f32[2,2624]{1,0:T(2,128)S(1)}, u32[]{:S(2)}, u32[]{:S(2)}) collective-permute-start(f32[2,2624]{1,0:T(2,128)S(1)} %pad_maximum_fusion.6), channel_id=1, source_target_pairs={{0,1},{1,0},{2,3},{3,2},{4,5},{5,4},{6,7},{7,6},{8,9},{9,8},{10,11... | collective-permute-start | bytes 62984 | tf_op jit(solution)/shard_map/ppermute | solution.py:97
  13.5 4.1 %collective-permute-start.2 = (f32[4,2624]{1,0:T(4,128)S(1)}, f32[4,2624]{1,0:T(4,128)S(1)}, u32[]{:S(2)}, u32[]{:S(2)}) collective-permute-start(f32[4,2624]{1,0:T(4,128)S(1)} %pad_maximum_fusion.4), channel_id=1, source_target_pairs={{0,2},{1,3},{2,0},{3,1},{4,6},{5,7},{6,4},{7,5},{8,10},{9,11},{10,... | collective-permute-start | bytes 125960 | tf_op jit(solution)/shard_map/ppermute | solution.py:97
  20.0 31.5 %copy-start.3 = (f32[1,8,3072]{2,1,0:T(8,128)}, f32[1,8,3072]{2,1,0:T(8,128)S(1)}, u32[]{:S(2)}) copy-start(f32[1,8,3072]{2,1,0:T(8,128)S(1)} %maximum_bitcast_fusion.x_ref) | copy-start | bytes 294916
  20.0 10.8 %collective-permute-start.3 = (f32[1,8,3072]{2,1,0:T(8,128)S(1)}, f32[1,8,3072]{2,1,0:T(8,128)S(1)}, u32[]{:S(2)}, u32[]{:S(2)}) collective-permute-start(f32[1,8,3072]{2,1,0:T(8,128)S(1)} %maximum_bitcast_fusion.x_ref), channel_id=1, source_target_pairs={{0,128},{8,136},{16,144},{24,152},{32,160},{40,168},{48,176},{56,1... | collective-permute-start | bytes 294920 | tf_op jit(solution)/shard_map/ppermute | solution.py:163
  30.7 20.7 %copy-start.4 = (f32[1,8,3072]{2,1,0:T(8,128)}, f32[1,8,3072]{2,1,0:T(8,128)S(1)}, u32[]{:S(2)}) copy-start(f32[1,8,3072]{2,1,0:T(8,128)S(1)} %collective-permute-done.3.x_ref) | copy-start | bytes 294916
  30.8 9.0 %collective-permute-start.4 = (f32[2,8,3072]{2,1,0:T(8,128)S(1)}, f32[2,8,3072]{2,1,0:T(8,128)S(1)}, u32[]{:S(2)}, u32[]{:S(2)}) collective-permute-start(f32[2,8,3072]{2,1,0:T(8,128)S(1)} %pad_maximum_fusion.2), channel_id=1, source_target_pairs={{0,64},{8,72},{16,80},{24,88},{32,96},{40,104},{48,112},{56,120},{... | collective-permute-start | bytes 589832 | tf_op jit(solution)/shard_map/ppermute | solution.py:163
  39.8 12.4 %copy-start.2 = (f32[2,8,3072]{2,1,0:T(8,128)}, f32[2,8,3072]{2,1,0:T(8,128)S(1)}, u32[]{:S(2)}) copy-start(f32[2,8,3072]{2,1,0:T(8,128)S(1)} %collective-permute-done.4.x_ref) | copy-start | bytes 589828
  39.8 9.5 %collective-permute-start.5 = (f32[4,8,3072]{2,1,0:T(8,128)S(1)}, f32[4,8,3072]{2,1,0:T(8,128)S(1)}, u32[]{:S(2)}, u32[]{:S(2)}) collective-permute-start(f32[4,8,3072]{2,1,0:T(8,128)S(1)} %pad_maximum_fusion.1), channel_id=1, source_target_pairs={{0,32},{8,40},{16,48},{24,56},{32,0},{40,8},{48,16},{56,24},{64,96... | collective-permute-start | bytes 1179656 | tf_op jit(solution)/shard_map/ppermute | solution.py:163
  49.3 18.2 %copy-start = (f32[4,8,3072]{2,1,0:T(8,128)}, f32[4,8,3072]{2,1,0:T(8,128)S(1)}, u32[]{:S(2)}) copy-start(f32[4,8,3072]{2,1,0:T(8,128)S(1)} %collective-permute-done.5.x_ref) | copy-start | bytes 1179652
  49.4 18.1 %copy-start.7 = (f32[8,128]{1,0:T(8,128)S(1)}, f32[8,128]{1,0:T(8,128)}, u32[]{:S(2)}) copy-start(f32[8,128]{1,0:T(8,128)} %param.6) | copy-start | bytes 12292
  49.4 18.1 %copy-start.19 = (f32[8]{0:T(128)S(1)}, f32[8]{0:T(128)}, u32[]{:S(2)}) copy-start(f32[8]{0:T(128)} %param.10) | copy-start | bytes 100
  49.4 19.6 %copy-start.18 = (f32[8]{0:T(128)S(1)}, f32[8]{0:T(128)}, u32[]{:S(2)}) copy-start(f32[8]{0:T(128)} %param.11) | copy-start | bytes 100
  49.4 17.1 %collective-permute-start.6 = (f32[8,8,3072]{2,1,0:T(8,128)S(1)}, f32[8,8,3072]{2,1,0:T(8,128)S(1)}, u32[]{:S(2)}, u32[]{:S(2)}) collective-permute-start(f32[8,8,3072]{2,1,0:T(8,128)S(1)} %pad_maximum_fusion), channel_id=1, source_target_pairs={{0,16},{8,24},{16,0},{24,8},{32,48},{40,56},{48,32},{56,40},{64,80... | collective-permute-start | bytes 2359304 | tf_op jit(solution)/shard_map/ppermute | solution.py:163
  66.5 17.9 %copy-start.1 = (f32[8,8,3072]{2,1,0:T(8,128)}, f32[8,8,3072]{2,1,0:T(8,128)S(1)}, u32[]{:S(2)}) copy-start(f32[8,8,3072]{2,1,0:T(8,128)S(1)} %collective-permute-done.6.x_ref) | copy-start | bytes 2359300
  67.5 25.5 %collective-permute-start.7 = (f32[16,8,3072]{2,1,0:T(8,128)}, f32[16,8,3072]{2,1,0:T(8,128)S(1)}, u32[]{:S(2)}, u32[]{:S(2)}) collective-permute-start(f32[16,8,3072]{2,1,0:T(8,128)} %constant_dynamic-update-slice_fusion), channel_id=1, source_target_pairs={{0,8},{8,0},{16,24},{24,16},{32,40},{40,32},{48,56},{56,48},{64,72... | collective-permute-start | bytes 4718600 | tf_op jit(solution)/shard_map/ppermute | solution.py:163
  79.4 29.5 %copy-start.8 = (f32[8,128]{1,0:T(8,128)S(1)}, f32[8,128]{1,0:T(8,128)}, u32[]{:S(2)}) copy-start(f32[8,128]{1,0:T(8,128)} %get-tuple-element.14) | copy-start | bytes 12292
  79.4 29.5 %copy-start.9 = (f32[8,128]{1,0:T(8,128)S(1)}, f32[8,128]{1,0:T(8,128)}, u32[]{:S(2)}) copy-start(f32[8,128]{1,0:T(8,128)} %get-tuple-element.15) | copy-start | bytes 12292
  79.4 29.5 %copy-start.10 = (f32[8,128]{1,0:T(8,128)S(1)}, f32[8,128]{1,0:T(8,128)}, u32[]{:S(2)}) copy-start(f32[8,128]{1,0:T(8,128)} %get-tuple-element.16) | copy-start | bytes 12292
  84.4 24.5 %copy-start.11 = (f32[8,128]{1,0:T(8,128)S(1)}, f32[8,128]{1,0:T(8,128)}, u32[]{:S(2)}) copy-start(f32[8,128]{1,0:T(8,128)} %get-tuple-element.17) | copy-start | bytes 12292
  92.9 16.0 %copy-start.12 = (f32[8,128]{1,0:T(8,128)S(1)}, f32[8,128]{1,0:T(8,128)}, u32[]{:S(2)}) copy-start(f32[8,128]{1,0:T(8,128)} %get-tuple-element.18) | copy-start | bytes 12292
  93.0 31.2 %copy-start.13 = (f32[8,64]{1,0:T(8,128)S(1)}, f32[8,64]{1,0:T(8,128)}, u32[]{:S(2)}) copy-start(f32[8,64]{1,0:T(8,128)} %get-tuple-element.20) | copy-start | bytes 6148
  93.0 31.2 %copy-start.14 = (f32[8,64]{1,0:T(8,128)S(1)}, f32[8,64]{1,0:T(8,128)}, u32[]{:S(2)}) copy-start(f32[8,64]{1,0:T(8,128)} %get-tuple-element.21) | copy-start | bytes 6148
  93.0 31.2 %copy-start.15 = (f32[8,64]{1,0:T(8,128)S(1)}, f32[8,64]{1,0:T(8,128)}, u32[]{:S(2)}) copy-start(f32[8,64]{1,0:T(8,128)} %get-tuple-element.22) | copy-start | bytes 6148
  93.0 31.2 %copy-start.16 = (f32[8,64]{1,0:T(8,128)S(1)}, f32[8,64]{1,0:T(8,128)}, u32[]{:S(2)}) copy-start(f32[8,64]{1,0:T(8,128)} %get-tuple-element.23) | copy-start | bytes 6148
  93.0 31.2 %copy-start.17 = (f32[8,64]{1,0:T(8,128)S(1)}, f32[8,64]{1,0:T(8,128)}, u32[]{:S(2)}) copy-start(f32[8,64]{1,0:T(8,128)} %get-tuple-element.24) | copy-start | bytes 6148
  93.0 1.2 copy-start.5
  109.6 15.9 %copy-start.6 = (f32[8,128]{1,0:T(8,128)}, f32[8,128]{1,0:T(8,128)S(1)}, u32[]{:S(2)}) copy-start(f32[8,128]{1,0:T(8,128)S(1)} %add_add_fusion.1) | copy-start | bytes 12292
  109.6 5.1 %collective-permute-start.8 = (f32[1,8,128]{2,1,0:T(8,128)S(1)}, f32[1,8,128]{2,1,0:T(8,128)S(1)}, u32[]{:S(2)}, u32[]{:S(2)}) collective-permute-start(f32[1,8,128]{2,1,0:T(8,128)S(1)} %bitcast.52), channel_id=1, source_target_pairs={{0,4},{1,5},{2,6},{3,7},{4,0},{5,1},{6,2},{7,3},{8,12},{9,13},{10,... | collective-permute-start | bytes 12296 | tf_op jit(solution)/shard_map/ppermute | solution.py:97
  114.8 5.2 %collective-permute-start.9 = (f32[2,8,128]{2,1,0:T(8,128)S(1)}, f32[2,8,128]{2,1,0:T(8,128)S(1)}, u32[]{:S(2)}, u32[]{:S(2)}) collective-permute-start(f32[2,8,128]{2,1,0:T(8,128)S(1)} %pad_maximum_fusion.9), channel_id=1, source_target_pairs={{0,1},{1,0},{2,3},{3,2},{4,5},{5,4},{6,7},{7,6},{8,9},{9,8},{10,11... | collective-permute-start | bytes 24584 | tf_op jit(solution)/shard_map/ppermute | solution.py:97
  119.9 3.8 %collective-permute-start.10 = (f32[4,8,128]{2,1,0:T(8,128)S(1)}, f32[4,8,128]{2,1,0:T(8,128)S(1)}, u32[]{:S(2)}, u32[]{:S(2)}) collective-permute-start(f32[4,8,128]{2,1,0:T(8,128)S(1)} %pad_maximum_fusion.7), channel_id=1, source_target_pairs={{0,2},{1,3},{2,0},{3,1},{4,6},{5,7},{6,4},{7,5},{8,10},{9,11},{10,... | collective-permute-start | bytes 49160 | tf_op jit(solution)/shard_map/ppermute | solution.py:97

commit v7 on v6

--- a/solution.py
+++ b/solution.py
@@ -148,12 +148,11 @@
 
     own_high = lax.axis_index("grp") * highs_dev
     high_feats = lax.dynamic_slice_in_dim(high_feats_block, own_high, highs_dev, 1)
-    pick_own = lax.dynamic_slice_in_dim(pick, own_high, highs_dev, 1)
 
     wide = jnp.concatenate([feats_block, mixed_block, high_feats_block, highp_block], 1)
     nb = width
     nh = high_feats_block.shape[1]
-    rows_low = low_sites * inv_len_low[:, None]
+    rows_low = jnp.concatenate([low_sites, high_feats], 1) * inv_len_low[:, None]
     rows_diff = high_feats * inv_len_diff[:, None]
 
     buf = wide[None]
@@ -167,12 +166,9 @@
         if bit != BLK_BITS[-1]:
             buf = jnp.concatenate([buf, other], 0)
     new_diff = VAR_DIFF * new_diff
-    low_block = unblock(gather_bits(new_low, "grp", grp_size, GRP_BITS), probes_n)
-    high_part = jnp.dot(
-        low_block, pick_own, precision=lax.Precision.HIGHEST, preferred_element_type=jnp.float32
-    )
+    high_part = new_low[:, rows_dev:]
     high_out = RHO * high_part + new_diff
-    return (new_low, high_out)
+    return (new_low[:, :rows_dev], high_out)
 
 
 def solution(mesh):

time: 126 us -> 123 us (0.976); the launches traced: 125 us -> 121 us
  Pallas kernels: 37.2 us -> 46.3 us
  waiting for transfers between devices: 50.3 us -> 41.5 us
  starting transfers between devices: 21.8 us -> 16.9 us
    pallas_call x6, Pallas kernels: 37.2 us -> 46.3 us  [apply_piece(): pl.pallas_call(kern, grid=(n // per,), in_specs=[full((rl, feats)), full(...]
    ppermute x6 -> x3, waiting for transfers between devices: 16.7 us -> 7.95 us  [gather_bits(): other = lax.ppermute(buf, axis, [(i, i ^ mask) for i in range(size)])]
    ppermute x6 -> x3, starting transfers between devices: 11.8 us -> 6.82 us  [gather_bits(): other = lax.ppermute(buf, axis, [(i, i ^ mask) for i in range(size)])]
    unnamed x44 -> x42, local copies, waits for them, and re-layouts: 3.45 us -> 3.44 us
  transfers between devices with their start and end apart: 11 -> 8, of which waited for: 10 -> 7; matrix products, arithmetic and copies ran while one was open for 5% -> 5% of each run, Pallas kernels for 18% -> 22%
where the time goes in v7:
time: 123 us; the launch traced here: 121 us
  Pallas kernels  46.3 us (38%)
  waiting for transfers between devices  41.5 us (34%)
  starting transfers between devices  16.9 us (14%)
  local copies, waits for them, and re-layouts  8.43 us (7%)
  other arithmetic  4.95 us (4%)
  matrix products  1.75 us (1%)
    pallas_call x6, Pallas kernels, apply_piece(): pl.pallas_call(kern, grid=(n // per,), in_specs=[full((rl, feats)), full(...  46.3 us
    ppermute x5, waiting for transfers between devices, per_device(): other = lax.ppermute(buf, 'blk', [(i, i ^ mask) for i in range(blk_size)])  33.6 us
    ppermute x5, starting transfers between devices, per_device(): other = lax.ppermute(buf, 'blk', [(i, i ^ mask) for i in range(blk_size)])  10 us
    ppermute x3, waiting for transfers between devices, gather_bits(): other = lax.ppermute(buf, axis, [(i, i ^ mask) for i in range(size)])  7.95 us
    ppermute x3, starting transfers between devices, gather_bits(): other = lax.ppermute(buf, axis, [(i, i ^ mask) for i in range(size)])  6.82 us
    unnamed x42, local copies, waits for them, and re-layouts  3.44 us
  transfers between devices with their start and end apart: 8, of which 7 were waited for; matrix products, arithmetic and copies ran while one was open for 5% of the time, Pallas kernels for 22%

profile of v7, /device:TPU:16, one launch (start us, length us, event | category | flops | bytes accessed | tf_op | source)
XLA Modules:
  0.0 120.7 jit_solution(13716207935229715123)
XLA Ops:
  0.6 0.8 reshape.51
  2.0 0.7 pad_maximum_fusion.6
  2.8 3.1 %collective-permute-start = (f32[1,2624]{1,0:T(1,128)S(1)}, f32[1,2624]{1,0:T(1,128)S(1)}, u32[]{:S(2)}, u32[]{:S(2)}) collective-permute-start(f32[1,2624]{1,0:T(1,128)S(1)} %broadcast_in_dim.8), channel_id=1, source_target_pairs={{0,4},{1,5},{2,6},{3,7},{4,0},{5,1},{6,2},{7,3},{8,12},{9,13},{10,... | collective-permute-start | bytes 31496 | tf_op jit(solution)/shard_map/ppermute | solution.py:97
  5.9 2.2 %collective-permute-done = f32[1,2624]{1,0:T(1,128)S(1)} collective-permute-done((f32[1,2624]{1,0:T(1,128)S(1)}, f32[1,2624]{1,0:T(1,128)S(1)}, u32[]{:S(2)}, u32[]{:S(2)}) %collective-permute-start) | collective-permute-done | bytes 10528 | tf_op jit(solution)/shard_map/ppermute | solution.py:97
  8.1 2.1 %collective-permute-start.1 = (f32[2,2624]{1,0:T(2,128)S(1)}, f32[2,2624]{1,0:T(2,128)S(1)}, u32[]{:S(2)}, u32[]{:S(2)}) collective-permute-start(f32[2,2624]{1,0:T(2,128)S(1)} %pad_maximum_fusion.5), channel_id=1, source_target_pairs={{0,1},{1,0},{2,3},{3,2},{4,5},{5,4},{6,7},{7,6},{8,9},{9,8},{10,11... | collective-permute-start | bytes 62984 | tf_op jit(solution)/shard_map/ppermute | solution.py:97
  10.2 3.3 %collective-permute-done.1 = f32[2,2624]{1,0:T(2,128)S(1)} collective-permute-done((f32[2,2624]{1,0:T(2,128)S(1)}, f32[2,2624]{1,0:T(2,128)S(1)}, u32[]{:S(2)}, u32[]{:S(2)}) %collective-permute-start.1) | collective-permute-done | bytes 21024 | tf_op jit(solution)/shard_map/ppermute | solution.py:97
  13.5 1.6 %collective-permute-start.2 = (f32[4,2624]{1,0:T(4,128)S(1)}, f32[4,2624]{1,0:T(4,128)S(1)}, u32[]{:S(2)}, u32[]{:S(2)}) collective-permute-start(f32[4,2624]{1,0:T(4,128)S(1)} %pad_maximum_fusion.4), channel_id=1, source_target_pairs={{0,2},{1,3},{2,0},{3,1},{4,6},{5,7},{6,4},{7,5},{8,10},{9,11},{10,... | collective-permute-start | bytes 125960 | tf_op jit(solution)/shard_map/ppermute | solution.py:97
  15.1 2.5 %collective-permute-done.2 = f32[4,2624]{1,0:T(4,128)S(1)} collective-permute-done((f32[4,2624]{1,0:T(4,128)S(1)}, f32[4,2624]{1,0:T(4,128)S(1)}, u32[]{:S(2)}, u32[]{:S(2)}) %collective-permute-start.2) | collective-permute-done | bytes 42016 | tf_op jit(solution)/shard_map/ppermute | solution.py:97
  18.2 0.7 fusion.1
  18.9 1.0 fusion.3
  20.0 7.3 %collective-permute-start.3 = (f32[1,8,3072]{2,1,0:T(8,128)S(1)}, f32[1,8,3072]{2,1,0:T(8,128)S(1)}, u32[]{:S(2)}, u32[]{:S(2)}) collective-permute-start(f32[1,8,3072]{2,1,0:T(8,128)S(1)} %maximum_bitcast_fusion.x_ref), channel_id=1, source_target_pairs={{0,128},{8,136},{16,144},{24,152},{32,160},{40,168},{48,176},{56,1... | collective-permute-start | bytes 294920 | tf_op jit(solution)/shard_map/ppermute | solution.py:162
  27.2 3.5 %collective-permute-done.3.x_ref = f32[1,8,3072]{2,1,0:T(8,128)S(1)} collective-permute-done((f32[1,8,3072]{2,1,0:T(8,128)S(1)}, f32[1,8,3072]{2,1,0:T(8,128)S(1)}, u32[]{:S(2)}, u32[]{:S(2)}) %collective-permute-start.3) | collective-permute-done | bytes 98336 | tf_op jit(solution)/shard_map/ppermute | solution.py:162
  30.8 1.3 %collective-permute-start.4 = (f32[2,8,3072]{2,1,0:T(8,128)S(1)}, f32[2,8,3072]{2,1,0:T(8,128)S(1)}, u32[]{:S(2)}, u32[]{:S(2)}) collective-permute-start(f32[2,8,3072]{2,1,0:T(8,128)S(1)} %pad_maximum_fusion.2), channel_id=1, source_target_pairs={{0,64},{8,72},{16,80},{24,88},{32,96},{40,104},{48,112},{56,120},{... | collective-permute-start | bytes 589832 | tf_op jit(solution)/shard_map/ppermute | solution.py:162
  32.0 7.7 %collective-permute-done.4.x_ref = f32[2,8,3072]{2,1,0:T(8,128)S(1)} collective-permute-done((f32[2,8,3072]{2,1,0:T(8,128)S(1)}, f32[2,8,3072]{2,1,0:T(8,128)S(1)}, u32[]{:S(2)}, u32[]{:S(2)}) %collective-permute-start.4) | collective-permute-done | bytes 196640 | tf_op jit(solution)/shard_map/ppermute | solution.py:162
  40.5 8.8 %collective-permute-done.5.x_ref = f32[4,8,3072]{2,1,0:T(8,128)S(1)} collective-permute-done((f32[4,8,3072]{2,1,0:T(8,128)S(1)}, f32[4,8,3072]{2,1,0:T(8,128)S(1)}, u32[]{:S(2)}, u32[]{:S(2)}) %collective-permute-start.5) | collective-permute-done | bytes 393248 | tf_op jit(solution)/shard_map/ppermute | solution.py:162
  49.4 1.4 %collective-permute-start.6 = (f32[8,8,3072]{2,1,0:T(8,128)S(1)}, f32[8,8,3072]{2,1,0:T(8,128)S(1)}, u32[]{:S(2)}, u32[]{:S(2)}) collective-permute-start(f32[8,8,3072]{2,1,0:T(8,128)S(1)} %pad_maximum_fusion), channel_id=1, source_target_pairs={{0,16},{8,24},{16,0},{24,8},{32,48},{40,56},{48,32},{56,40},{64,80... | collective-permute-start | bytes 2359304 | tf_op jit(solution)/shard_map/ppermute | solution.py:162
  51.4 0.7 constant_dynamic-update-slice_fusion.2
  52.1 0.8 constant_dynamic-update-slice_fusion.1
  52.9 13.6 %collective-permute-done.6.x_ref = f32[8,8,3072]{2,1,0:T(8,128)S(1)} collective-permute-done((f32[8,8,3072]{2,1,0:T(8,128)S(1)}, f32[8,8,3072]{2,1,0:T(8,128)S(1)}, u32[]{:S(2)}, u32[]{:S(2)}) %collective-permute-start.6) | collective-permute-done | bytes 786464 | tf_op jit(solution)/shard_map/ppermute | solution.py:162
  66.5 1.0 constant_dynamic-update-slice_fusion
  67.5 0.7 copy.84.sl_ref
  68.2 0.7 copy.85.sd_ref
  69.1 0.8 copy.81
  70.5 2.9 %shard_map.77 = (f32[8,192]{1,0:T(8,128)}, f32[8,64]{1,0:T(8,128)}) custom-call(f32[192,8]{1,0:T(8,128)} %bitcast.28, f32[64,8]{1,0:T(8,128)} %multiply_bitcast_fusion.rd_ref, f32[8,1]{1,0:T(8,128)} %copy.84.sl_ref, f32[8,1]{1,0:T(8,128)} %copy.85.sd_ref, f32[1,8,3072]{2,1,0:T(8,128)} %copy-done.3), custom_call_target="tpu_custom_call" | custom-call | tf_op jit(solution)/shard_map/pallas_call | solution.py:72
  73.4 2.9 %shard_map.78 = (f32[8,192]{1,0:T(8,128)}, f32[8,64]{1,0:T(8,128)}) custom-call(f32[192,8]{1,0:T(8,128)} %bitcast.29, f32[64,8]{1,0:T(8,128)} %multiply_bitcast_fusion.rd_ref, f32[8,1]{1,0:T(8,128)} %copy.84.sl_ref, f32[8,1]{1,0:T(8,128)} %copy.85.sd_ref, f32[1,8,3072]{2,1,0:T(8,128)} %copy-done.4), custom_call_target="tpu_custom_call" | custom-call | tf_op jit(solution)/shard_map/pallas_call | solution.py:72
  76.3 3.9 %shard_map.79 = (f32[8,192]{1,0:T(8,128)}, f32[8,64]{1,0:T(8,128)}) custom-call(f32[192,8]{1,0:T(8,128)} %bitcast.30, f32[64,8]{1,0:T(8,128)} %multiply_bitcast_fusion.rd_ref, f32[8,1]{1,0:T(8,128)} %copy.84.sl_ref, f32[8,1]{1,0:T(8,128)} %copy.85.sd_ref, f32[2,8,3072]{2,1,0:T(8,128)} %copy-done.2), custom_call_target="tpu_custom_call" | custom-call | tf_op jit(solution)/shard_map/pallas_call | solution.py:72
  80.3 6.2 %shard_map.80 = (f32[8,192]{1,0:T(8,128)}, f32[8,64]{1,0:T(8,128)}) custom-call(f32[192,8]{1,0:T(8,128)} %bitcast.31, f32[64,8]{1,0:T(8,128)} %multiply_bitcast_fusion.rd_ref, f32[8,1]{1,0:T(8,128)} %copy.84.sl_ref, f32[8,1]{1,0:T(8,128)} %copy.85.sd_ref, f32[4,8,3072]{2,1,0:T(8,128)} %copy-done), custom_call_target="tpu_custom_call" | custom-call | tf_op jit(solution)/shard_map/pallas_call | solution.py:72
  86.5 10.9 %shard_map.81 = (f32[8,192]{1,0:T(8,128)}, f32[8,64]{1,0:T(8,128)}) custom-call(f32[192,8]{1,0:T(8,128)} %bitcast.32, f32[64,8]{1,0:T(8,128)} %multiply_bitcast_fusion.rd_ref, f32[8,1]{1,0:T(8,128)} %copy.84.sl_ref, f32[8,1]{1,0:T(8,128)} %copy.85.sd_ref, f32[8,8,3072]{2,1,0:T(8,128)} %copy-done.1), custom_call_target="tpu_custom_call" | custom-call | tf_op jit(solution)/shard_map/pallas_call | solution.py:72
  97.4 1.2 copy-done.5
  98.6 19.4 %shard_map.82 = (f32[8,192]{1,0:T(8,128)}, f32[8,64]{1,0:T(8,128)}) custom-call(f32[192,8]{1,0:T(8,128)} %bitcast.33, f32[64,8]{1,0:T(8,128)} %multiply_bitcast_fusion.rd_ref, f32[8,1]{1,0:T(8,128)} %copy.84.sl_ref, f32[8,1]{1,0:T(8,128)} %copy.85.sd_ref, f32[16,8,3072]{2,1,0:T(8,128)} %copy-done.5), custom_call_target="tpu_custom_call" | custom-call | tf_op jit(solution)/shard_map/pallas_call | solution.py:72
  118.0 0.7 add_add_fusion
  119.4 1.3 %fusion.6 = f32[8,64]{1,0:T(8,128)} fusion(f32[8,192]{1,0:T(8,128)S(1)} %add_add_fusion, f32[8,64]{1,0:T(8,128)} %get-tuple-element.25, f32[8,64]{1,0:T(8,128)S(1)} %copy-done.16, f32[8,64]{1,0:T(8,128)S(1)} %copy-done.15, f32[8,64]{1,0:T(8,128)S(1)} %copy-done.14, f32[8,64]{1,0:T(8,128)S(1)} %copy-done.12, f32[8,64]{1,0:T(8,128)S(1)} %copy-done.13), kind=kLoop, calls=%fused_computation.33 | loop fusion | flops 3584 | bytes 16384 | tf_op jit(solution)/shard_map/add | solution.py:170
  (70 shorter events, 4.3 us)
Async XLA Ops:
  2.8 5.3 %collective-permute-start = (f32[1,2624]{1,0:T(1,128)S(1)}, f32[1,2624]{1,0:T(1,128)S(1)}, u32[]{:S(2)}, u32[]{:S(2)}) collective-permute-start(f32[1,2624]{1,0:T(1,128)S(1)} %broadcast_in_dim.8), channel_id=1, source_target_pairs={{0,4},{1,5},{2,6},{3,7},{4,0},{5,1},{6,2},{7,3},{8,12},{9,13},{10,... | collective-permute-start | bytes 31496 | tf_op jit(solution)/shard_map/ppermute | solution.py:97
  8.1 5.4 %collective-permute-start.1 = (f32[2,2624]{1,0:T(2,128)S(1)}, f32[2,2624]{1,0:T(2,128)S(1)}, u32[]{:S(2)}, u32[]{:S(2)}) collective-permute-start(f32[2,2624]{1,0:T(2,128)S(1)} %pad_maximum_fusion.5), channel_id=1, source_target_pairs={{0,1},{1,0},{2,3},{3,2},{4,5},{5,4},{6,7},{7,6},{8,9},{9,8},{10,11... | collective-permute-start | bytes 62984 | tf_op jit(solution)/shard_map/ppermute | solution.py:97
  13.5 4.1 %collective-permute-start.2 = (f32[4,2624]{1,0:T(4,128)S(1)}, f32[4,2624]{1,0:T(4,128)S(1)}, u32[]{:S(2)}, u32[]{:S(2)}) collective-permute-start(f32[4,2624]{1,0:T(4,128)S(1)} %pad_maximum_fusion.4), channel_id=1, source_target_pairs={{0,2},{1,3},{2,0},{3,1},{4,6},{5,7},{6,4},{7,5},{8,10},{9,11},{10,... | collective-permute-start | bytes 125960 | tf_op jit(solution)/shard_map/ppermute | solution.py:97
  20.0 31.5 %copy-start.3 = (f32[1,8,3072]{2,1,0:T(8,128)}, f32[1,8,3072]{2,1,0:T(8,128)S(1)}, u32[]{:S(2)}) copy-start(f32[1,8,3072]{2,1,0:T(8,128)S(1)} %maximum_bitcast_fusion.x_ref) | copy-start | bytes 294916
  20.0 10.8 %collective-permute-start.3 = (f32[1,8,3072]{2,1,0:T(8,128)S(1)}, f32[1,8,3072]{2,1,0:T(8,128)S(1)}, u32[]{:S(2)}, u32[]{:S(2)}) collective-permute-start(f32[1,8,3072]{2,1,0:T(8,128)S(1)} %maximum_bitcast_fusion.x_ref), channel_id=1, source_target_pairs={{0,128},{8,136},{16,144},{24,152},{32,160},{40,168},{48,176},{56,1... | collective-permute-start | bytes 294920 | tf_op jit(solution)/shard_map/ppermute | solution.py:162
  30.7 20.7 %copy-start.4 = (f32[1,8,3072]{2,1,0:T(8,128)}, f32[1,8,3072]{2,1,0:T(8,128)S(1)}, u32[]{:S(2)}) copy-start(f32[1,8,3072]{2,1,0:T(8,128)S(1)} %collective-permute-done.3.x_ref) | copy-start | bytes 294916
  30.8 9.0 %collective-permute-start.4 = (f32[2,8,3072]{2,1,0:T(8,128)S(1)}, f32[2,8,3072]{2,1,0:T(8,128)S(1)}, u32[]{:S(2)}, u32[]{:S(2)}) collective-permute-start(f32[2,8,3072]{2,1,0:T(8,128)S(1)} %pad_maximum_fusion.2), channel_id=1, source_target_pairs={{0,64},{8,72},{16,80},{24,88},{32,96},{40,104},{48,112},{56,120},{... | collective-permute-start | bytes 589832 | tf_op jit(solution)/shard_map/ppermute | solution.py:162
  39.8 12.4 %copy-start.2 = (f32[2,8,3072]{2,1,0:T(8,128)}, f32[2,8,3072]{2,1,0:T(8,128)S(1)}, u32[]{:S(2)}) copy-start(f32[2,8,3072]{2,1,0:T(8,128)S(1)} %collective-permute-done.4.x_ref) | copy-start | bytes 589828
  39.8 9.5 %collective-permute-start.5 = (f32[4,8,3072]{2,1,0:T(8,128)S(1)}, f32[4,8,3072]{2,1,0:T(8,128)S(1)}, u32[]{:S(2)}, u32[]{:S(2)}) collective-permute-start(f32[4,8,3072]{2,1,0:T(8,128)S(1)} %pad_maximum_fusion.1), channel_id=1, source_target_pairs={{0,32},{8,40},{16,48},{24,56},{32,0},{40,8},{48,16},{56,24},{64,96... | collective-permute-start | bytes 1179656 | tf_op jit(solution)/shard_map/ppermute | solution.py:162
  49.3 18.2 %copy-start = (f32[4,8,3072]{2,1,0:T(8,128)}, f32[4,8,3072]{2,1,0:T(8,128)S(1)}, u32[]{:S(2)}) copy-start(f32[4,8,3072]{2,1,0:T(8,128)S(1)} %collective-permute-done.5.x_ref) | copy-start | bytes 1179652
  49.4 18.2 %copy-start.18 = (f32[8]{0:T(128)S(1)}, f32[8]{0:T(128)}, u32[]{:S(2)}) copy-start(f32[8]{0:T(128)} %param.10) | copy-start | bytes 100
  49.4 18.8 %copy-start.17 = (f32[8]{0:T(128)S(1)}, f32[8]{0:T(128)}, u32[]{:S(2)}) copy-start(f32[8]{0:T(128)} %param.11) | copy-start | bytes 100
  49.4 19.7 %copy-start.6 = (f32[8,128]{1,0:T(8,128)S(1)}, f32[8,128]{1,0:T(8,128)}, u32[]{:S(2)}) copy-start(f32[8,128]{1,0:T(8,128)} %param.6) | copy-start | bytes 12292
  49.4 17.1 %collective-permute-start.6 = (f32[8,8,3072]{2,1,0:T(8,128)S(1)}, f32[8,8,3072]{2,1,0:T(8,128)S(1)}, u32[]{:S(2)}, u32[]{:S(2)}) collective-permute-start(f32[8,8,3072]{2,1,0:T(8,128)S(1)} %pad_maximum_fusion), channel_id=1, source_target_pairs={{0,16},{8,24},{16,0},{24,8},{32,48},{40,56},{48,32},{56,40},{64,80... | collective-permute-start | bytes 2359304 | tf_op jit(solution)/shard_map/ppermute | solution.py:162
  66.5 20.0 %copy-start.1 = (f32[8,8,3072]{2,1,0:T(8,128)}, f32[8,8,3072]{2,1,0:T(8,128)S(1)}, u32[]{:S(2)}) copy-start(f32[8,8,3072]{2,1,0:T(8,128)S(1)} %collective-permute-done.6.x_ref) | copy-start | bytes 2359300
  67.5 29.9 %collective-permute-start.7 = (f32[16,8,3072]{2,1,0:T(8,128)}, f32[16,8,3072]{2,1,0:T(8,128)S(1)}, u32[]{:S(2)}, u32[]{:S(2)}) collective-permute-start(f32[16,8,3072]{2,1,0:T(8,128)} %constant_dynamic-update-slice_fusion), channel_id=1, source_target_pairs={{0,8},{8,0},{16,24},{24,16},{32,40},{40,32},{48,56},{56,48},{64,72... | collective-permute-start | bytes 4718600 | tf_op jit(solution)/shard_map/ppermute | solution.py:162
  80.3 37.7 %copy-start.7 = (f32[8,192]{1,0:T(8,128)S(1)}, f32[8,192]{1,0:T(8,128)}, u32[]{:S(2)}) copy-start(f32[8,192]{1,0:T(8,128)} %get-tuple-element.14) | copy-start | bytes 18436
  80.3 37.7 %copy-start.8 = (f32[8,192]{1,0:T(8,128)S(1)}, f32[8,192]{1,0:T(8,128)}, u32[]{:S(2)}) copy-start(f32[8,192]{1,0:T(8,128)} %get-tuple-element.15) | copy-start | bytes 18436
  80.3 37.7 %copy-start.9 = (f32[8,192]{1,0:T(8,128)S(1)}, f32[8,192]{1,0:T(8,128)}, u32[]{:S(2)}) copy-start(f32[8,192]{1,0:T(8,128)} %get-tuple-element.16) | copy-start | bytes 18436
  80.3 39.0 %copy-start.12 = (f32[8,64]{1,0:T(8,128)S(1)}, f32[8,64]{1,0:T(8,128)}, u32[]{:S(2)}) copy-start(f32[8,64]{1,0:T(8,128)} %get-tuple-element.20) | copy-start | bytes 6148
  80.3 39.0 %copy-start.13 = (f32[8,64]{1,0:T(8,128)S(1)}, f32[8,64]{1,0:T(8,128)}, u32[]{:S(2)}) copy-start(f32[8,64]{1,0:T(8,128)} %get-tuple-element.21) | copy-start | bytes 6148
  80.3 39.0 %copy-start.14 = (f32[8,64]{1,0:T(8,128)S(1)}, f32[8,64]{1,0:T(8,128)}, u32[]{:S(2)}) copy-start(f32[8,64]{1,0:T(8,128)} %get-tuple-element.22) | copy-start | bytes 6148
  86.5 31.5 %copy-start.10 = (f32[8,192]{1,0:T(8,128)S(1)}, f32[8,192]{1,0:T(8,128)}, u32[]{:S(2)}) copy-start(f32[8,192]{1,0:T(8,128)} %get-tuple-element.17) | copy-start | bytes 18436
  86.5 32.9 %copy-start.15 = (f32[8,64]{1,0:T(8,128)S(1)}, f32[8,64]{1,0:T(8,128)}, u32[]{:S(2)}) copy-start(f32[8,64]{1,0:T(8,128)} %get-tuple-element.23) | copy-start | bytes 6148
  97.4 20.6 %copy-start.11 = (f32[8,192]{1,0:T(8,128)S(1)}, f32[8,192]{1,0:T(8,128)}, u32[]{:S(2)}) copy-start(f32[8,192]{1,0:T(8,128)} %get-tuple-element.18) | copy-start | bytes 18436
  97.4 21.9 %copy-start.16 = (f32[8,64]{1,0:T(8,128)S(1)}, f32[8,64]{1,0:T(8,128)}, u32[]{:S(2)}) copy-start(f32[8,64]{1,0:T(8,128)} %get-tuple-element.24) | copy-start | bytes 6148
  97.4 1.2 copy-start.5

commit v8 on v7

--- a/solution.py
+++ b/solution.py
@@ -29,7 +29,7 @@
     )
 
 
-def _piece_kernel(rl_ref, rd_ref, sl_ref, sd_ref, x_ref, ol_ref, od_ref, *, nb, nh):
+def _piece_kernel(rl_ref, rd_ref, x_ref, ol_ref, od_ref, *, nb, nh):
     @pl.when(pl.program_id(0) == 0)
     def _init():
         ol_ref[...] = jnp.zeros(ol_ref.shape, jnp.float32)
@@ -39,8 +39,6 @@
     rows_d = rd_ref[...]
     rn_l = jnp.sum(rows_l * rows_l, axis=1, keepdims=True)
     rn_d = jnp.sum(rows_d * rows_d, axis=1, keepdims=True)
-    scale_l = sl_ref[...]
-    scale_d = sd_ref[...]
 
     group = math.gcd(x_ref.shape[0], 8)
 
@@ -49,9 +47,9 @@
 
     def one_group(b, carry):
         acc_l, acc_d = carry
-        cols = take(b, 0, nb) * scale_l
+        cols = take(b, 0, nb)
         acc_l = acc_l + _accumulate(rows_l, rn_l, cols, take(b, nb, nb))
-        cols = take(b, 2 * nb, nh) * scale_d
+        cols = take(b, 2 * nb, nh)
         acc_d = acc_d + _accumulate(rows_d, rn_d, cols, take(b, 2 * nb + nh, nh))
         return acc_l, acc_d
 
@@ -62,7 +60,7 @@
     od_ref[...] += acc_d
 
 
-def apply_piece(rows_low, rows_diff, inv_len_low, inv_len_diff, piece, nb, nh, interpret=False):
+def apply_piece(rows_low, rows_diff, piece, nb, nh, interpret=False):
     n, feats, width = piece.shape
     probes = piece.shape[1]
     per = min(n, 8)
@@ -75,8 +73,6 @@
         in_specs=[
             full((rl, feats)),
             full((rd, feats)),
-            full((feats, 1)),
-            full((feats, 1)),
             pl.BlockSpec((per, feats, width), lambda j: (j, 0, 0)),
         ],
         out_specs=[full((probes, rl)), full((probes, rd))],
@@ -86,7 +82,7 @@
         ],
         compiler_params=pltpu.CompilerParams(dimension_semantics=("arbitrary",)),
         interpret=interpret,
-    )(rows_low.T, rows_diff.T, inv_len_low[:, None], inv_len_diff[:, None], piece)
+    )(rows_low.T, rows_diff.T, piece)
 
 
 def gather_bits(x, axis, size, bits):
@@ -149,18 +145,20 @@
     own_high = lax.axis_index("grp") * highs_dev
     high_feats = lax.dynamic_slice_in_dim(high_feats_block, own_high, highs_dev, 1)
 
-    wide = jnp.concatenate([feats_block, mixed_block, high_feats_block, highp_block], 1)
+    wide = jnp.concatenate(
+        [feats_block * inv_len_low[:, None], mixed_block, high_feats_block * inv_len_diff[:, None], highp_block], 1
+    )
     nb = width
     nh = high_feats_block.shape[1]
     rows_low = jnp.concatenate([low_sites, high_feats], 1) * inv_len_low[:, None]
     rows_diff = high_feats * inv_len_diff[:, None]
 
     buf = wide[None]
-    new_low, new_diff = apply_piece(rows_low, rows_diff, inv_len_low, inv_len_diff, buf, nb, nh)
+    new_low, new_diff = apply_piece(rows_low, rows_diff, buf, nb, nh)
     for bit in BLK_BITS:
         mask = 1 << bit
         other = lax.ppermute(buf, "blk", [(i, i ^ mask) for i in range(blk_size)])
-        part_low, part_diff = apply_piece(rows_low, rows_diff, inv_len_low, inv_len_diff, other, nb, nh)
+        part_low, part_diff = apply_piece(rows_low, rows_diff, other, nb, nh)
         new_low = new_low + part_low
         new_diff = new_diff + part_diff
         if bit != BLK_BITS[-1]:

time: 123 us -> 121 us (0.984)
  local copies, waits for them, and re-layouts: 8.43 us -> 7.1 us
    broadcast_in_dim x2 -> x0, local copies, waits for them, and re-layouts: 1.35 us -> none  [the longest x1 0.67 us: per_device(): inv_len_low[:, None]]
  transfers between devices with their start and end apart: 8 -> 8, of which waited for: 7 -> 7; matrix products, arithmetic and copies ran while one was open for 5% -> 4% of each run, Pallas kernels for 22% -> 22%
where the time goes in v8:
time: 121 us; the launch traced here: 120 us
  Pallas kernels  45.7 us (38%)
  waiting for transfers between devices  41.5 us (34%)
  starting transfers between devices  16.9 us (14%)
  local copies, waits for them, and re-layouts  7.1 us (6%)
  other arithmetic  5.67 us (5%)
  matrix products  1.75 us (1%)
    pallas_call x6, Pallas kernels, apply_piece(): pl.pallas_call(kern, grid=(n // per,), in_specs=[full((rl, feats)), full(...  45.7 us
    ppermute x5, waiting for transfers between devices, per_device(): other = lax.ppermute(buf, 'blk', [(i, i ^ mask) for i in range(blk_size)])  33.6 us
    ppermute x5, starting transfers between devices, per_device(): other = lax.ppermute(buf, 'blk', [(i, i ^ mask) for i in range(blk_size)])  10 us
    ppermute x3, waiting for transfers between devices, gather_bits(): other = lax.ppermute(buf, axis, [(i, i ^ mask) for i in range(size)])  7.95 us
    ppermute x3, starting transfers between devices, gather_bits(): other = lax.ppermute(buf, axis, [(i, i ^ mask) for i in range(size)])  6.82 us
    unnamed x42, local copies, waits for them, and re-layouts  3.44 us
  transfers between devices with their start and end apart: 8, of which 7 were waited for; matrix products, arithmetic and copies ran while one was open for 4% of the time, Pallas kernels for 22%

profile of v8, /device:TPU:16, one launch (start us, length us, event | category | flops | bytes accessed | tf_op | source)
XLA Modules:
  0.0 119.5 jit_solution(12568148551229694511)
XLA Ops:
  0.6 0.8 reshape.51
  1.4 0.7 convert_element_type.12
  2.1 0.7 pad_maximum_fusion.6
  2.8 3.1 %collective-permute-start = (f32[1,2624]{1,0:T(1,128)S(1)}, f32[1,2624]{1,0:T(1,128)S(1)}, u32[]{:S(2)}, u32[]{:S(2)}) collective-permute-start(f32[1,2624]{1,0:T(1,128)S(1)} %broadcast_in_dim.4), channel_id=1, source_target_pairs={{0,4},{1,5},{2,6},{3,7},{4,0},{5,1},{6,2},{7,3},{8,12},{9,13},{10,... | collective-permute-start | bytes 31496 | tf_op jit(solution)/shard_map/ppermute | solution.py:93
  5.9 2.2 %collective-permute-done = f32[1,2624]{1,0:T(1,128)S(1)} collective-permute-done((f32[1,2624]{1,0:T(1,128)S(1)}, f32[1,2624]{1,0:T(1,128)S(1)}, u32[]{:S(2)}, u32[]{:S(2)}) %collective-permute-start) | collective-permute-done | bytes 10528 | tf_op jit(solution)/shard_map/ppermute | solution.py:93
  8.1 2.1 %collective-permute-start.1 = (f32[2,2624]{1,0:T(2,128)S(1)}, f32[2,2624]{1,0:T(2,128)S(1)}, u32[]{:S(2)}, u32[]{:S(2)}) collective-permute-start(f32[2,2624]{1,0:T(2,128)S(1)} %pad_maximum_fusion.5), channel_id=1, source_target_pairs={{0,1},{1,0},{2,3},{3,2},{4,5},{5,4},{6,7},{7,6},{8,9},{9,8},{10,11... | collective-permute-start | bytes 62984 | tf_op jit(solution)/shard_map/ppermute | solution.py:93
  10.2 3.3 %collective-permute-done.1 = f32[2,2624]{1,0:T(2,128)S(1)} collective-permute-done((f32[2,2624]{1,0:T(2,128)S(1)}, f32[2,2624]{1,0:T(2,128)S(1)}, u32[]{:S(2)}, u32[]{:S(2)}) %collective-permute-start.1) | collective-permute-done | bytes 21024 | tf_op jit(solution)/shard_map/ppermute | solution.py:93
  13.6 1.6 %collective-permute-start.2 = (f32[4,2624]{1,0:T(4,128)S(1)}, f32[4,2624]{1,0:T(4,128)S(1)}, u32[]{:S(2)}, u32[]{:S(2)}) collective-permute-start(f32[4,2624]{1,0:T(4,128)S(1)} %pad_maximum_fusion.4), channel_id=1, source_target_pairs={{0,2},{1,3},{2,0},{3,1},{4,6},{5,7},{6,4},{7,5},{8,10},{9,11},{10,... | collective-permute-start | bytes 125960 | tf_op jit(solution)/shard_map/ppermute | solution.py:93
  15.1 2.5 %collective-permute-done.2 = f32[4,2624]{1,0:T(4,128)S(1)} collective-permute-done((f32[4,2624]{1,0:T(4,128)S(1)}, f32[4,2624]{1,0:T(4,128)S(1)}, u32[]{:S(2)}, u32[]{:S(2)}) %collective-permute-start.2) | collective-permute-done | bytes 42016 | tf_op jit(solution)/shard_map/ppermute | solution.py:93
  18.2 0.7 bitcast_multiply_fusion
  18.9 0.7 broadcast_multiply_fusion
  19.6 1.0 fusion.3
  20.7 7.3 %collective-permute-start.3 = (f32[1,8,3072]{2,1,0:T(8,128)S(1)}, f32[1,8,3072]{2,1,0:T(8,128)S(1)}, u32[]{:S(2)}, u32[]{:S(2)}) collective-permute-start(f32[1,8,3072]{2,1,0:T(8,128)S(1)} %maximum_bitcast_fusion.x_ref), channel_id=1, source_target_pairs={{0,128},{8,136},{16,144},{24,152},{32,160},{40,168},{48,176},{56,1... | collective-permute-start | bytes 294920 | tf_op jit(solution)/shard_map/ppermute | solution.py:160
  28.0 3.5 %collective-permute-done.3.x_ref = f32[1,8,3072]{2,1,0:T(8,128)S(1)} collective-permute-done((f32[1,8,3072]{2,1,0:T(8,128)S(1)}, f32[1,8,3072]{2,1,0:T(8,128)S(1)}, u32[]{:S(2)}, u32[]{:S(2)}) %collective-permute-start.3) | collective-permute-done | bytes 98336 | tf_op jit(solution)/shard_map/ppermute | solution.py:160
  31.5 1.3 %collective-permute-start.4 = (f32[2,8,3072]{2,1,0:T(8,128)S(1)}, f32[2,8,3072]{2,1,0:T(8,128)S(1)}, u32[]{:S(2)}, u32[]{:S(2)}) collective-permute-start(f32[2,8,3072]{2,1,0:T(8,128)S(1)} %pad_maximum_fusion.2), channel_id=1, source_target_pairs={{0,64},{8,72},{16,80},{24,88},{32,96},{40,104},{48,112},{56,120},{... | collective-permute-start | bytes 589832 | tf_op jit(solution)/shard_map/ppermute | solution.py:160
  32.8 7.7 %collective-permute-done.4.x_ref = f32[2,8,3072]{2,1,0:T(8,128)S(1)} collective-permute-done((f32[2,8,3072]{2,1,0:T(8,128)S(1)}, f32[2,8,3072]{2,1,0:T(8,128)S(1)}, u32[]{:S(2)}, u32[]{:S(2)}) %collective-permute-start.4) | collective-permute-done | bytes 196640 | tf_op jit(solution)/shard_map/ppermute | solution.py:160
  41.3 8.8 %collective-permute-done.5.x_ref = f32[4,8,3072]{2,1,0:T(8,128)S(1)} collective-permute-done((f32[4,8,3072]{2,1,0:T(8,128)S(1)}, f32[4,8,3072]{2,1,0:T(8,128)S(1)}, u32[]{:S(2)}, u32[]{:S(2)}) %collective-permute-start.5) | collective-permute-done | bytes 393248 | tf_op jit(solution)/shard_map/ppermute | solution.py:160
  50.1 1.4 %collective-permute-start.6 = (f32[8,8,3072]{2,1,0:T(8,128)S(1)}, f32[8,8,3072]{2,1,0:T(8,128)S(1)}, u32[]{:S(2)}, u32[]{:S(2)}) collective-permute-start(f32[8,8,3072]{2,1,0:T(8,128)S(1)} %pad_maximum_fusion), channel_id=1, source_target_pairs={{0,16},{8,24},{16,0},{24,8},{32,48},{40,56},{48,32},{56,40},{64,80... | collective-permute-start | bytes 2359304 | tf_op jit(solution)/shard_map/ppermute | solution.py:160
  52.1 0.7 constant_dynamic-update-slice_fusion.2
  52.8 0.8 constant_dynamic-update-slice_fusion.1
  53.6 13.6 %collective-permute-done.6.x_ref = f32[8,8,3072]{2,1,0:T(8,128)S(1)} collective-permute-done((f32[8,8,3072]{2,1,0:T(8,128)S(1)}, f32[8,8,3072]{2,1,0:T(8,128)S(1)}, u32[]{:S(2)}, u32[]{:S(2)}) %collective-permute-start.6) | collective-permute-done | bytes 786464 | tf_op jit(solution)/shard_map/ppermute | solution.py:160
  67.2 1.0 constant_dynamic-update-slice_fusion
  68.5 0.8 copy.33
  69.9 2.8 %shard_map.77 = (f32[8,192]{1,0:T(8,128)}, f32[8,64]{1,0:T(8,128)}) custom-call(f32[192,8]{1,0:T(8,128)} %bitcast.28, f32[64,8]{1,0:T(8,128)} %multiply_bitcast_fusion.rd_ref, f32[1,8,3072]{2,1,0:T(8,128)} %copy-done.3), custom_call_target="tpu_custom_call" | custom-call | tf_op jit(solution)/shard_map/pallas_call | solution.py:70
  72.7 2.8 %shard_map.78 = (f32[8,192]{1,0:T(8,128)}, f32[8,64]{1,0:T(8,128)}) custom-call(f32[192,8]{1,0:T(8,128)} %bitcast.29, f32[64,8]{1,0:T(8,128)} %multiply_bitcast_fusion.rd_ref, f32[1,8,3072]{2,1,0:T(8,128)} %copy-done.4), custom_call_target="tpu_custom_call" | custom-call | tf_op jit(solution)/shard_map/pallas_call | solution.py:70
  75.5 3.8 %shard_map.79 = (f32[8,192]{1,0:T(8,128)}, f32[8,64]{1,0:T(8,128)}) custom-call(f32[192,8]{1,0:T(8,128)} %bitcast.30, f32[64,8]{1,0:T(8,128)} %multiply_bitcast_fusion.rd_ref, f32[2,8,3072]{2,1,0:T(8,128)} %copy-done.2), custom_call_target="tpu_custom_call" | custom-call | tf_op jit(solution)/shard_map/pallas_call | solution.py:70
  79.4 6.1 %shard_map.80 = (f32[8,192]{1,0:T(8,128)}, f32[8,64]{1,0:T(8,128)}) custom-call(f32[192,8]{1,0:T(8,128)} %bitcast.31, f32[64,8]{1,0:T(8,128)} %multiply_bitcast_fusion.rd_ref, f32[4,8,3072]{2,1,0:T(8,128)} %copy-done), custom_call_target="tpu_custom_call" | custom-call | tf_op jit(solution)/shard_map/pallas_call | solution.py:70
  85.5 10.8 %shard_map.81 = (f32[8,192]{1,0:T(8,128)}, f32[8,64]{1,0:T(8,128)}) custom-call(f32[192,8]{1,0:T(8,128)} %bitcast.32, f32[64,8]{1,0:T(8,128)} %multiply_bitcast_fusion.rd_ref, f32[8,8,3072]{2,1,0:T(8,128)} %copy-done.1), custom_call_target="tpu_custom_call" | custom-call | tf_op jit(solution)/shard_map/pallas_call | solution.py:70
  96.4 1.2 copy-done.5
  97.6 19.3 %shard_map.82 = (f32[8,192]{1,0:T(8,128)}, f32[8,64]{1,0:T(8,128)}) custom-call(f32[192,8]{1,0:T(8,128)} %bitcast.33, f32[64,8]{1,0:T(8,128)} %multiply_bitcast_fusion.rd_ref, f32[16,8,3072]{2,1,0:T(8,128)} %copy-done.5), custom_call_target="tpu_custom_call" | custom-call | tf_op jit(solution)/shard_map/pallas_call | solution.py:70
  116.9 0.7 add_add_fusion
  118.2 1.3 %fusion.8 = f32[8,64]{1,0:T(8,128)} fusion(f32[8,192]{1,0:T(8,128)S(1)} %add_add_fusion, f32[8,64]{1,0:T(8,128)} %get-tuple-element.25, f32[8,64]{1,0:T(8,128)S(1)} %copy-done.16, f32[8,64]{1,0:T(8,128)S(1)} %copy-done.15, f32[8,64]{1,0:T(8,128)S(1)} %copy-done.14, f32[8,64]{1,0:T(8,128)S(1)} %copy-done.12, f32[8,64]{1,0:T(8,128)S(1)} %copy-done.13), kind=kLoop, calls=%fused_computation.36 | loop fusion | flops 3584 | bytes 16384 | tf_op jit(solution)/shard_map/add | solution.py:168
  (68 shorter events, 3.6 us)
Async XLA Ops:
  0.6 18.3 %copy-start.18 = (f32[8]{0:T(128)S(1)}, f32[8]{0:T(128)}, u32[]{:S(2)}) copy-start(f32[8]{0:T(128)} %param.11) | copy-start | bytes 100
  2.8 5.3 %collective-permute-start = (f32[1,2624]{1,0:T(1,128)S(1)}, f32[1,2624]{1,0:T(1,128)S(1)}, u32[]{:S(2)}, u32[]{:S(2)}) collective-permute-start(f32[1,2624]{1,0:T(1,128)S(1)} %broadcast_in_dim.4), channel_id=1, source_target_pairs={{0,4},{1,5},{2,6},{3,7},{4,0},{5,1},{6,2},{7,3},{8,12},{9,13},{10,... | collective-permute-start | bytes 31496 | tf_op jit(solution)/shard_map/ppermute | solution.py:93
  8.1 5.4 %collective-permute-start.1 = (f32[2,2624]{1,0:T(2,128)S(1)}, f32[2,2624]{1,0:T(2,128)S(1)}, u32[]{:S(2)}, u32[]{:S(2)}) collective-permute-start(f32[2,2624]{1,0:T(2,128)S(1)} %pad_maximum_fusion.5), channel_id=1, source_target_pairs={{0,1},{1,0},{2,3},{3,2},{4,5},{5,4},{6,7},{7,6},{8,9},{9,8},{10,11... | collective-permute-start | bytes 62984 | tf_op jit(solution)/shard_map/ppermute | solution.py:93
  13.6 4.1 %collective-permute-start.2 = (f32[4,2624]{1,0:T(4,128)S(1)}, f32[4,2624]{1,0:T(4,128)S(1)}, u32[]{:S(2)}, u32[]{:S(2)}) collective-permute-start(f32[4,2624]{1,0:T(4,128)S(1)} %pad_maximum_fusion.4), channel_id=1, source_target_pairs={{0,2},{1,3},{2,0},{3,1},{4,6},{5,7},{6,4},{7,5},{8,10},{9,11},{10,... | collective-permute-start | bytes 125960 | tf_op jit(solution)/shard_map/ppermute | solution.py:93
  20.7 32.1 %copy-start.3 = (f32[1,8,3072]{2,1,0:T(8,128)}, f32[1,8,3072]{2,1,0:T(8,128)S(1)}, u32[]{:S(2)}) copy-start(f32[1,8,3072]{2,1,0:T(8,128)S(1)} %maximum_bitcast_fusion.x_ref) | copy-start | bytes 294916
  20.7 10.8 %collective-permute-start.3 = (f32[1,8,3072]{2,1,0:T(8,128)S(1)}, f32[1,8,3072]{2,1,0:T(8,128)S(1)}, u32[]{:S(2)}, u32[]{:S(2)}) collective-permute-start(f32[1,8,3072]{2,1,0:T(8,128)S(1)} %maximum_bitcast_fusion.x_ref), channel_id=1, source_target_pairs={{0,128},{8,136},{16,144},{24,152},{32,160},{40,168},{48,176},{56,1... | collective-permute-start | bytes 294920 | tf_op jit(solution)/shard_map/ppermute | solution.py:160
  31.5 21.4 %copy-start.4 = (f32[1,8,3072]{2,1,0:T(8,128)}, f32[1,8,3072]{2,1,0:T(8,128)S(1)}, u32[]{:S(2)}) copy-start(f32[1,8,3072]{2,1,0:T(8,128)S(1)} %collective-permute-done.3.x_ref) | copy-start | bytes 294916
  31.5 9.0 %collective-permute-start.4 = (f32[2,8,3072]{2,1,0:T(8,128)S(1)}, f32[2,8,3072]{2,1,0:T(8,128)S(1)}, u32[]{:S(2)}, u32[]{:S(2)}) collective-permute-start(f32[2,8,3072]{2,1,0:T(8,128)S(1)} %pad_maximum_fusion.2), channel_id=1, source_target_pairs={{0,64},{8,72},{16,80},{24,88},{32,96},{40,104},{48,112},{56,120},{... | collective-permute-start | bytes 589832 | tf_op jit(solution)/shard_map/ppermute | solution.py:160
  40.5 12.3 %copy-start.2 = (f32[2,8,3072]{2,1,0:T(8,128)}, f32[2,8,3072]{2,1,0:T(8,128)S(1)}, u32[]{:S(2)}) copy-start(f32[2,8,3072]{2,1,0:T(8,128)S(1)} %collective-permute-done.4.x_ref) | copy-start | bytes 589828
  40.5 9.5 %collective-permute-start.5 = (f32[4,8,3072]{2,1,0:T(8,128)S(1)}, f32[4,8,3072]{2,1,0:T(8,128)S(1)}, u32[]{:S(2)}, u32[]{:S(2)}) collective-permute-start(f32[4,8,3072]{2,1,0:T(8,128)S(1)} %pad_maximum_fusion.1), channel_id=1, source_target_pairs={{0,32},{8,40},{16,48},{24,56},{32,0},{40,8},{48,16},{56,24},{64,96... | collective-permute-start | bytes 1179656 | tf_op jit(solution)/shard_map/ppermute | solution.py:160
  50.1 18.2 %copy-start = (f32[4,8,3072]{2,1,0:T(8,128)}, f32[4,8,3072]{2,1,0:T(8,128)S(1)}, u32[]{:S(2)}) copy-start(f32[4,8,3072]{2,1,0:T(8,128)S(1)} %collective-permute-done.5.x_ref) | copy-start | bytes 1179652
  50.1 18.3 %copy-start.6 = (f32[8,128]{1,0:T(8,128)S(1)}, f32[8,128]{1,0:T(8,128)}, u32[]{:S(2)}) copy-start(f32[8,128]{1,0:T(8,128)} %param.6) | copy-start | bytes 12292
  50.1 18.3 %copy-start.17 = (f32[8]{0:T(128)S(1)}, f32[8]{0:T(128)}, u32[]{:S(2)}) copy-start(f32[8]{0:T(128)} %param.10) | copy-start | bytes 100
  50.1 17.1 %collective-permute-start.6 = (f32[8,8,3072]{2,1,0:T(8,128)S(1)}, f32[8,8,3072]{2,1,0:T(8,128)S(1)}, u32[]{:S(2)}, u32[]{:S(2)}) collective-permute-start(f32[8,8,3072]{2,1,0:T(8,128)S(1)} %pad_maximum_fusion), channel_id=1, source_target_pairs={{0,16},{8,24},{16,0},{24,8},{32,48},{40,56},{48,32},{56,40},{64,80... | collective-permute-start | bytes 2359304 | tf_op jit(solution)/shard_map/ppermute | solution.py:160
  67.2 18.3 %copy-start.1 = (f32[8,8,3072]{2,1,0:T(8,128)}, f32[8,8,3072]{2,1,0:T(8,128)S(1)}, u32[]{:S(2)}) copy-start(f32[8,8,3072]{2,1,0:T(8,128)S(1)} %collective-permute-done.6.x_ref) | copy-start | bytes 2359300
  68.3 28.1 %collective-permute-start.7 = (f32[16,8,3072]{2,1,0:T(8,128)}, f32[16,8,3072]{2,1,0:T(8,128)S(1)}, u32[]{:S(2)}, u32[]{:S(2)}) collective-permute-start(f32[16,8,3072]{2,1,0:T(8,128)} %constant_dynamic-update-slice_fusion), channel_id=1, source_target_pairs={{0,8},{8,0},{16,24},{24,16},{32,40},{40,32},{48,56},{56,48},{64,72... | collective-permute-start | bytes 4718600 | tf_op jit(solution)/shard_map/ppermute | solution.py:160
  79.4 37.5 %copy-start.7 = (f32[8,192]{1,0:T(8,128)S(1)}, f32[8,192]{1,0:T(8,128)}, u32[]{:S(2)}) copy-start(f32[8,192]{1,0:T(8,128)} %get-tuple-element.14) | copy-start | bytes 18436
  79.4 37.5 %copy-start.8 = (f32[8,192]{1,0:T(8,128)S(1)}, f32[8,192]{1,0:T(8,128)}, u32[]{:S(2)}) copy-start(f32[8,192]{1,0:T(8,128)} %get-tuple-element.15) | copy-start | bytes 18436
  79.4 37.5 %copy-start.9 = (f32[8,192]{1,0:T(8,128)S(1)}, f32[8,192]{1,0:T(8,128)}, u32[]{:S(2)}) copy-start(f32[8,192]{1,0:T(8,128)} %get-tuple-element.16) | copy-start | bytes 18436
  79.4 38.9 %copy-start.12 = (f32[8,64]{1,0:T(8,128)S(1)}, f32[8,64]{1,0:T(8,128)}, u32[]{:S(2)}) copy-start(f32[8,64]{1,0:T(8,128)} %get-tuple-element.20) | copy-start | bytes 6148
  79.4 38.8 %copy-start.13 = (f32[8,64]{1,0:T(8,128)S(1)}, f32[8,64]{1,0:T(8,128)}, u32[]{:S(2)}) copy-start(f32[8,64]{1,0:T(8,128)} %get-tuple-element.21) | copy-start | bytes 6148
  79.4 38.8 %copy-start.14 = (f32[8,64]{1,0:T(8,128)S(1)}, f32[8,64]{1,0:T(8,128)}, u32[]{:S(2)}) copy-start(f32[8,64]{1,0:T(8,128)} %get-tuple-element.22) | copy-start | bytes 6148
  85.5 31.4 %copy-start.10 = (f32[8,192]{1,0:T(8,128)S(1)}, f32[8,192]{1,0:T(8,128)}, u32[]{:S(2)}) copy-start(f32[8,192]{1,0:T(8,128)} %get-tuple-element.17) | copy-start | bytes 18436
  85.5 32.7 %copy-start.15 = (f32[8,64]{1,0:T(8,128)S(1)}, f32[8,64]{1,0:T(8,128)}, u32[]{:S(2)}) copy-start(f32[8,64]{1,0:T(8,128)} %get-tuple-element.23) | copy-start | bytes 6148
  96.4 20.5 %copy-start.11 = (f32[8,192]{1,0:T(8,128)S(1)}, f32[8,192]{1,0:T(8,128)}, u32[]{:S(2)}) copy-start(f32[8,192]{1,0:T(8,128)} %get-tuple-element.18) | copy-start | bytes 18436
  96.4 21.9 %copy-start.16 = (f32[8,64]{1,0:T(8,128)S(1)}, f32[8,64]{1,0:T(8,128)}, u32[]{:S(2)}) copy-start(f32[8,64]{1,0:T(8,128)} %get-tuple-element.24) | copy-start | bytes 6148
  96.4 1.2 copy-start.5

commit v9 on v8

--- a/solution.py
+++ b/solution.py
@@ -17,12 +17,13 @@
 BLK_BITS = (4, 3, 2, 1, 0)
 
 
-def _accumulate(rows, rn, cols, w):
-    inner = jnp.dot(rows, cols, precision=lax.Precision.HIGHEST, preferred_element_type=jnp.float32)
+def _accumulate(rows_m2, rn, cols, w):
+    inner_m2 = jnp.dot(rows_m2, cols, precision=lax.Precision.HIGHEST, preferred_element_type=jnp.float32)
     cn = jnp.sum(cols * cols, axis=0, keepdims=True)
-    square = rn + cn - 2.0 * inner
+    square = (rn + cn) + inner_m2
     dist = jnp.sqrt(jnp.maximum(square, 0.0))
-    tile = (1.0 + SQRT_THREE * dist) * jnp.exp(-SQRT_THREE * dist)
+    scaled = SQRT_THREE * dist
+    tile = (1.0 + scaled) * jnp.exp(-scaled)
     return lax.dot_general(
         w, tile, (((1,), (1,)), ((), ())),
         precision=lax.Precision.HIGH, preferred_element_type=jnp.float32,
@@ -39,6 +40,8 @@
     rows_d = rd_ref[...]
     rn_l = jnp.sum(rows_l * rows_l, axis=1, keepdims=True)
     rn_d = jnp.sum(rows_d * rows_d, axis=1, keepdims=True)
+    rows_l = -2.0 * rows_l
+    rows_d = -2.0 * rows_d
 
     group = math.gcd(x_ref.shape[0], 8)
 

time: 121 us -> 121 us (level)
  no operation moved by 1% of the time
where the time goes in v9:
time: 121 us; the launch traced here: 120 us
  Pallas kernels  45.7 us (38%)
  waiting for transfers between devices  41.5 us (34%)
  starting transfers between devices  16.9 us (14%)
  local copies, waits for them, and re-layouts  7.1 us (6%)
  other arithmetic  5.67 us (5%)
  matrix products  1.75 us (1%)
    pallas_call x6, Pallas kernels, apply_piece(): pl.pallas_call(kern, grid=(n // per,), in_specs=[full((rl, feats)), full(...  45.7 us
    ppermute x5, waiting for transfers between devices, per_device(): other = lax.ppermute(buf, 'blk', [(i, i ^ mask) for i in range(blk_size)])  33.6 us
    ppermute x5, starting transfers between devices, per_device(): other = lax.ppermute(buf, 'blk', [(i, i ^ mask) for i in range(blk_size)])  10 us
    ppermute x3, waiting for transfers between devices, gather_bits(): other = lax.ppermute(buf, axis, [(i, i ^ mask) for i in range(size)])  7.95 us
    ppermute x3, starting transfers between devices, gather_bits(): other = lax.ppermute(buf, axis, [(i, i ^ mask) for i in range(size)])  6.82 us
    unnamed x42, local copies, waits for them, and re-layouts  3.44 us
  transfers between devices with their start and end apart: 8, of which 7 were waited for; matrix products, arithmetic and copies ran while one was open for 4% of the time, Pallas kernels for 22%

profile of v9, /device:TPU:16, one launch (start us, length us, event | category | flops | bytes accessed | tf_op | source)
XLA Modules:
  0.0 119.5 jit_solution(6084081138011530593)
XLA Ops:
  0.6 0.8 reshape.51
  1.4 0.7 convert_element_type.12
  2.1 0.7 pad_maximum_fusion.6
  2.8 3.1 %collective-permute-start = (f32[1,2624]{1,0:T(1,128)S(1)}, f32[1,2624]{1,0:T(1,128)S(1)}, u32[]{:S(2)}, u32[]{:S(2)}) collective-permute-start(f32[1,2624]{1,0:T(1,128)S(1)} %broadcast_in_dim.4), channel_id=1, source_target_pairs={{0,4},{1,5},{2,6},{3,7},{4,0},{5,1},{6,2},{7,3},{8,12},{9,13},{10,... | collective-permute-start | bytes 31496 | tf_op jit(solution)/shard_map/ppermute | solution.py:96
  5.9 2.2 %collective-permute-done = f32[1,2624]{1,0:T(1,128)S(1)} collective-permute-done((f32[1,2624]{1,0:T(1,128)S(1)}, f32[1,2624]{1,0:T(1,128)S(1)}, u32[]{:S(2)}, u32[]{:S(2)}) %collective-permute-start) | collective-permute-done | bytes 10528 | tf_op jit(solution)/shard_map/ppermute | solution.py:96
  8.1 2.1 %collective-permute-start.1 = (f32[2,2624]{1,0:T(2,128)S(1)}, f32[2,2624]{1,0:T(2,128)S(1)}, u32[]{:S(2)}, u32[]{:S(2)}) collective-permute-start(f32[2,2624]{1,0:T(2,128)S(1)} %pad_maximum_fusion.5), channel_id=1, source_target_pairs={{0,1},{1,0},{2,3},{3,2},{4,5},{5,4},{6,7},{7,6},{8,9},{9,8},{10,11... | collective-permute-start | bytes 62984 | tf_op jit(solution)/shard_map/ppermute | solution.py:96
  10.2 3.3 %collective-permute-done.1 = f32[2,2624]{1,0:T(2,128)S(1)} collective-permute-done((f32[2,2624]{1,0:T(2,128)S(1)}, f32[2,2624]{1,0:T(2,128)S(1)}, u32[]{:S(2)}, u32[]{:S(2)}) %collective-permute-start.1) | collective-permute-done | bytes 21024 | tf_op jit(solution)/shard_map/ppermute | solution.py:96
  13.6 1.6 %collective-permute-start.2 = (f32[4,2624]{1,0:T(4,128)S(1)}, f32[4,2624]{1,0:T(4,128)S(1)}, u32[]{:S(2)}, u32[]{:S(2)}) collective-permute-start(f32[4,2624]{1,0:T(4,128)S(1)} %pad_maximum_fusion.4), channel_id=1, source_target_pairs={{0,2},{1,3},{2,0},{3,1},{4,6},{5,7},{6,4},{7,5},{8,10},{9,11},{10,... | collective-permute-start | bytes 125960 | tf_op jit(solution)/shard_map/ppermute | solution.py:96
  15.1 2.5 %collective-permute-done.2 = f32[4,2624]{1,0:T(4,128)S(1)} collective-permute-done((f32[4,2624]{1,0:T(4,128)S(1)}, f32[4,2624]{1,0:T(4,128)S(1)}, u32[]{:S(2)}, u32[]{:S(2)}) %collective-permute-start.2) | collective-permute-done | bytes 42016 | tf_op jit(solution)/shard_map/ppermute | solution.py:96
  18.2 0.7 bitcast_multiply_fusion
  18.9 0.7 broadcast_multiply_fusion
  19.6 1.0 fusion.3
  20.7 7.3 %collective-permute-start.3 = (f32[1,8,3072]{2,1,0:T(8,128)S(1)}, f32[1,8,3072]{2,1,0:T(8,128)S(1)}, u32[]{:S(2)}, u32[]{:S(2)}) collective-permute-start(f32[1,8,3072]{2,1,0:T(8,128)S(1)} %maximum_bitcast_fusion.x_ref), channel_id=1, source_target_pairs={{0,128},{8,136},{16,144},{24,152},{32,160},{40,168},{48,176},{56,1... | collective-permute-start | bytes 294920 | tf_op jit(solution)/shard_map/ppermute | solution.py:163
  28.0 3.5 %collective-permute-done.3.x_ref = f32[1,8,3072]{2,1,0:T(8,128)S(1)} collective-permute-done((f32[1,8,3072]{2,1,0:T(8,128)S(1)}, f32[1,8,3072]{2,1,0:T(8,128)S(1)}, u32[]{:S(2)}, u32[]{:S(2)}) %collective-permute-start.3) | collective-permute-done | bytes 98336 | tf_op jit(solution)/shard_map/ppermute | solution.py:163
  31.5 1.3 %collective-permute-start.4 = (f32[2,8,3072]{2,1,0:T(8,128)S(1)}, f32[2,8,3072]{2,1,0:T(8,128)S(1)}, u32[]{:S(2)}, u32[]{:S(2)}) collective-permute-start(f32[2,8,3072]{2,1,0:T(8,128)S(1)} %pad_maximum_fusion.2), channel_id=1, source_target_pairs={{0,64},{8,72},{16,80},{24,88},{32,96},{40,104},{48,112},{56,120},{... | collective-permute-start | bytes 589832 | tf_op jit(solution)/shard_map/ppermute | solution.py:163
  32.8 7.7 %collective-permute-done.4.x_ref = f32[2,8,3072]{2,1,0:T(8,128)S(1)} collective-permute-done((f32[2,8,3072]{2,1,0:T(8,128)S(1)}, f32[2,8,3072]{2,1,0:T(8,128)S(1)}, u32[]{:S(2)}, u32[]{:S(2)}) %collective-permute-start.4) | collective-permute-done | bytes 196640 | tf_op jit(solution)/shard_map/ppermute | solution.py:163
  41.3 8.8 %collective-permute-done.5.x_ref = f32[4,8,3072]{2,1,0:T(8,128)S(1)} collective-permute-done((f32[4,8,3072]{2,1,0:T(8,128)S(1)}, f32[4,8,3072]{2,1,0:T(8,128)S(1)}, u32[]{:S(2)}, u32[]{:S(2)}) %collective-permute-start.5) | collective-permute-done | bytes 393248 | tf_op jit(solution)/shard_map/ppermute | solution.py:163
  50.1 1.4 %collective-permute-start.6 = (f32[8,8,3072]{2,1,0:T(8,128)S(1)}, f32[8,8,3072]{2,1,0:T(8,128)S(1)}, u32[]{:S(2)}, u32[]{:S(2)}) collective-permute-start(f32[8,8,3072]{2,1,0:T(8,128)S(1)} %pad_maximum_fusion), channel_id=1, source_target_pairs={{0,16},{8,24},{16,0},{24,8},{32,48},{40,56},{48,32},{56,40},{64,80... | collective-permute-start | bytes 2359304 | tf_op jit(solution)/shard_map/ppermute | solution.py:163
  52.1 0.7 constant_dynamic-update-slice_fusion.2
  52.8 0.8 constant_dynamic-update-slice_fusion.1
  53.6 13.6 %collective-permute-done.6.x_ref = f32[8,8,3072]{2,1,0:T(8,128)S(1)} collective-permute-done((f32[8,8,3072]{2,1,0:T(8,128)S(1)}, f32[8,8,3072]{2,1,0:T(8,128)S(1)}, u32[]{:S(2)}, u32[]{:S(2)}) %collective-permute-start.6) | collective-permute-done | bytes 786464 | tf_op jit(solution)/shard_map/ppermute | solution.py:163
  67.2 1.0 constant_dynamic-update-slice_fusion
  68.5 0.8 copy.33
  69.9 2.8 %shard_map.77 = (f32[8,192]{1,0:T(8,128)}, f32[8,64]{1,0:T(8,128)}) custom-call(f32[192,8]{1,0:T(8,128)} %bitcast.28, f32[64,8]{1,0:T(8,128)} %multiply_bitcast_fusion.rd_ref, f32[1,8,3072]{2,1,0:T(8,128)} %copy-done.3), custom_call_target="tpu_custom_call" | custom-call | tf_op jit(solution)/shard_map/pallas_call | solution.py:73
  72.7 2.8 %shard_map.78 = (f32[8,192]{1,0:T(8,128)}, f32[8,64]{1,0:T(8,128)}) custom-call(f32[192,8]{1,0:T(8,128)} %bitcast.29, f32[64,8]{1,0:T(8,128)} %multiply_bitcast_fusion.rd_ref, f32[1,8,3072]{2,1,0:T(8,128)} %copy-done.4), custom_call_target="tpu_custom_call" | custom-call | tf_op jit(solution)/shard_map/pallas_call | solution.py:73
  75.5 3.9 %shard_map.79 = (f32[8,192]{1,0:T(8,128)}, f32[8,64]{1,0:T(8,128)}) custom-call(f32[192,8]{1,0:T(8,128)} %bitcast.30, f32[64,8]{1,0:T(8,128)} %multiply_bitcast_fusion.rd_ref, f32[2,8,3072]{2,1,0:T(8,128)} %copy-done.2), custom_call_target="tpu_custom_call" | custom-call | tf_op jit(solution)/shard_map/pallas_call | solution.py:73
  79.5 6.1 %shard_map.80 = (f32[8,192]{1,0:T(8,128)}, f32[8,64]{1,0:T(8,128)}) custom-call(f32[192,8]{1,0:T(8,128)} %bitcast.31, f32[64,8]{1,0:T(8,128)} %multiply_bitcast_fusion.rd_ref, f32[4,8,3072]{2,1,0:T(8,128)} %copy-done), custom_call_target="tpu_custom_call" | custom-call | tf_op jit(solution)/shard_map/pallas_call | solution.py:73
  85.6 10.8 %shard_map.81 = (f32[8,192]{1,0:T(8,128)}, f32[8,64]{1,0:T(8,128)}) custom-call(f32[192,8]{1,0:T(8,128)} %bitcast.32, f32[64,8]{1,0:T(8,128)} %multiply_bitcast_fusion.rd_ref, f32[8,8,3072]{2,1,0:T(8,128)} %copy-done.1), custom_call_target="tpu_custom_call" | custom-call | tf_op jit(solution)/shard_map/pallas_call | solution.py:73
  96.4 1.2 copy-done.5
  97.6 19.3 %shard_map.82 = (f32[8,192]{1,0:T(8,128)}, f32[8,64]{1,0:T(8,128)}) custom-call(f32[192,8]{1,0:T(8,128)} %bitcast.33, f32[64,8]{1,0:T(8,128)} %multiply_bitcast_fusion.rd_ref, f32[16,8,3072]{2,1,0:T(8,128)} %copy-done.5), custom_call_target="tpu_custom_call" | custom-call | tf_op jit(solution)/shard_map/pallas_call | solution.py:73
  116.9 0.7 add_add_fusion
  118.2 1.3 %fusion.8 = f32[8,64]{1,0:T(8,128)} fusion(f32[8,192]{1,0:T(8,128)S(1)} %add_add_fusion, f32[8,64]{1,0:T(8,128)} %get-tuple-element.25, f32[8,64]{1,0:T(8,128)S(1)} %copy-done.16, f32[8,64]{1,0:T(8,128)S(1)} %copy-done.15, f32[8,64]{1,0:T(8,128)S(1)} %copy-done.14, f32[8,64]{1,0:T(8,128)S(1)} %copy-done.12, f32[8,64]{1,0:T(8,128)S(1)} %copy-done.13), kind=kLoop, calls=%fused_computation.36 | loop fusion | flops 3584 | bytes 16384 | tf_op jit(solution)/shard_map/add | solution.py:171
  (68 shorter events, 3.6 us)
Async XLA Ops:
  0.6 18.3 %copy-start.18 = (f32[8]{0:T(128)S(1)}, f32[8]{0:T(128)}, u32[]{:S(2)}) copy-start(f32[8]{0:T(128)} %param.11) | copy-start | bytes 100
  2.8 5.3 %collective-permute-start = (f32[1,2624]{1,0:T(1,128)S(1)}, f32[1,2624]{1,0:T(1,128)S(1)}, u32[]{:S(2)}, u32[]{:S(2)}) collective-permute-start(f32[1,2624]{1,0:T(1,128)S(1)} %broadcast_in_dim.4), channel_id=1, source_target_pairs={{0,4},{1,5},{2,6},{3,7},{4,0},{5,1},{6,2},{7,3},{8,12},{9,13},{10,... | collective-permute-start | bytes 31496 | tf_op jit(solution)/shard_map/ppermute | solution.py:96
  8.1 5.4 %collective-permute-start.1 = (f32[2,2624]{1,0:T(2,128)S(1)}, f32[2,2624]{1,0:T(2,128)S(1)}, u32[]{:S(2)}, u32[]{:S(2)}) collective-permute-start(f32[2,2624]{1,0:T(2,128)S(1)} %pad_maximum_fusion.5), channel_id=1, source_target_pairs={{0,1},{1,0},{2,3},{3,2},{4,5},{5,4},{6,7},{7,6},{8,9},{9,8},{10,11... | collective-permute-start | bytes 62984 | tf_op jit(solution)/shard_map/ppermute | solution.py:96
  13.6 4.1 %collective-permute-start.2 = (f32[4,2624]{1,0:T(4,128)S(1)}, f32[4,2624]{1,0:T(4,128)S(1)}, u32[]{:S(2)}, u32[]{:S(2)}) collective-permute-start(f32[4,2624]{1,0:T(4,128)S(1)} %pad_maximum_fusion.4), channel_id=1, source_target_pairs={{0,2},{1,3},{2,0},{3,1},{4,6},{5,7},{6,4},{7,5},{8,10},{9,11},{10,... | collective-permute-start | bytes 125960 | tf_op jit(solution)/shard_map/ppermute | solution.py:96
  20.7 32.1 %copy-start.3 = (f32[1,8,3072]{2,1,0:T(8,128)}, f32[1,8,3072]{2,1,0:T(8,128)S(1)}, u32[]{:S(2)}) copy-start(f32[1,8,3072]{2,1,0:T(8,128)S(1)} %maximum_bitcast_fusion.x_ref) | copy-start | bytes 294916
  20.7 10.8 %collective-permute-start.3 = (f32[1,8,3072]{2,1,0:T(8,128)S(1)}, f32[1,8,3072]{2,1,0:T(8,128)S(1)}, u32[]{:S(2)}, u32[]{:S(2)}) collective-permute-start(f32[1,8,3072]{2,1,0:T(8,128)S(1)} %maximum_bitcast_fusion.x_ref), channel_id=1, source_target_pairs={{0,128},{8,136},{16,144},{24,152},{32,160},{40,168},{48,176},{56,1... | collective-permute-start | bytes 294920 | tf_op jit(solution)/shard_map/ppermute | solution.py:163
  31.5 21.4 %copy-start.4 = (f32[1,8,3072]{2,1,0:T(8,128)}, f32[1,8,3072]{2,1,0:T(8,128)S(1)}, u32[]{:S(2)}) copy-start(f32[1,8,3072]{2,1,0:T(8,128)S(1)} %collective-permute-done.3.x_ref) | copy-start | bytes 294916
  31.5 9.0 %collective-permute-start.4 = (f32[2,8,3072]{2,1,0:T(8,128)S(1)}, f32[2,8,3072]{2,1,0:T(8,128)S(1)}, u32[]{:S(2)}, u32[]{:S(2)}) collective-permute-start(f32[2,8,3072]{2,1,0:T(8,128)S(1)} %pad_maximum_fusion.2), channel_id=1, source_target_pairs={{0,64},{8,72},{16,80},{24,88},{32,96},{40,104},{48,112},{56,120},{... | collective-permute-start | bytes 589832 | tf_op jit(solution)/shard_map/ppermute | solution.py:163
  40.5 12.3 %copy-start.2 = (f32[2,8,3072]{2,1,0:T(8,128)}, f32[2,8,3072]{2,1,0:T(8,128)S(1)}, u32[]{:S(2)}) copy-start(f32[2,8,3072]{2,1,0:T(8,128)S(1)} %collective-permute-done.4.x_ref) | copy-start | bytes 589828
  40.5 9.5 %collective-permute-start.5 = (f32[4,8,3072]{2,1,0:T(8,128)S(1)}, f32[4,8,3072]{2,1,0:T(8,128)S(1)}, u32[]{:S(2)}, u32[]{:S(2)}) collective-permute-start(f32[4,8,3072]{2,1,0:T(8,128)S(1)} %pad_maximum_fusion.1), channel_id=1, source_target_pairs={{0,32},{8,40},{16,48},{24,56},{32,0},{40,8},{48,16},{56,24},{64,96... | collective-permute-start | bytes 1179656 | tf_op jit(solution)/shard_map/ppermute | solution.py:163
  50.1 18.2 %copy-start = (f32[4,8,3072]{2,1,0:T(8,128)}, f32[4,8,3072]{2,1,0:T(8,128)S(1)}, u32[]{:S(2)}) copy-start(f32[4,8,3072]{2,1,0:T(8,128)S(1)} %collective-permute-done.5.x_ref) | copy-start | bytes 1179652
  50.1 18.3 %copy-start.6 = (f32[8,128]{1,0:T(8,128)S(1)}, f32[8,128]{1,0:T(8,128)}, u32[]{:S(2)}) copy-start(f32[8,128]{1,0:T(8,128)} %param.6) | copy-start | bytes 12292
  50.1 18.3 %copy-start.17 = (f32[8]{0:T(128)S(1)}, f32[8]{0:T(128)}, u32[]{:S(2)}) copy-start(f32[8]{0:T(128)} %param.10) | copy-start | bytes 100
  50.1 17.1 %collective-permute-start.6 = (f32[8,8,3072]{2,1,0:T(8,128)S(1)}, f32[8,8,3072]{2,1,0:T(8,128)S(1)}, u32[]{:S(2)}, u32[]{:S(2)}) collective-permute-start(f32[8,8,3072]{2,1,0:T(8,128)S(1)} %pad_maximum_fusion), channel_id=1, source_target_pairs={{0,16},{8,24},{16,0},{24,8},{32,48},{40,56},{48,32},{56,40},{64,80... | collective-permute-start | bytes 2359304 | tf_op jit(solution)/shard_map/ppermute | solution.py:163
  67.2 18.4 %copy-start.1 = (f32[8,8,3072]{2,1,0:T(8,128)}, f32[8,8,3072]{2,1,0:T(8,128)S(1)}, u32[]{:S(2)}) copy-start(f32[8,8,3072]{2,1,0:T(8,128)S(1)} %collective-permute-done.6.x_ref) | copy-start | bytes 2359300
  68.3 28.1 %collective-permute-start.7 = (f32[16,8,3072]{2,1,0:T(8,128)}, f32[16,8,3072]{2,1,0:T(8,128)S(1)}, u32[]{:S(2)}, u32[]{:S(2)}) collective-permute-start(f32[16,8,3072]{2,1,0:T(8,128)} %constant_dynamic-update-slice_fusion), channel_id=1, source_target_pairs={{0,8},{8,0},{16,24},{24,16},{32,40},{40,32},{48,56},{56,48},{64,72... | collective-permute-start | bytes 4718600 | tf_op jit(solution)/shard_map/ppermute | solution.py:163
  79.4 37.5 %copy-start.7 = (f32[8,192]{1,0:T(8,128)S(1)}, f32[8,192]{1,0:T(8,128)}, u32[]{:S(2)}) copy-start(f32[8,192]{1,0:T(8,128)} %get-tuple-element.14) | copy-start | bytes 18436
  79.4 37.5 %copy-start.8 = (f32[8,192]{1,0:T(8,128)S(1)}, f32[8,192]{1,0:T(8,128)}, u32[]{:S(2)}) copy-start(f32[8,192]{1,0:T(8,128)} %get-tuple-element.15) | copy-start | bytes 18436
  79.4 37.5 %copy-start.9 = (f32[8,192]{1,0:T(8,128)S(1)}, f32[8,192]{1,0:T(8,128)}, u32[]{:S(2)}) copy-start(f32[8,192]{1,0:T(8,128)} %get-tuple-element.16) | copy-start | bytes 18436
  79.4 38.8 %copy-start.12 = (f32[8,64]{1,0:T(8,128)S(1)}, f32[8,64]{1,0:T(8,128)}, u32[]{:S(2)}) copy-start(f32[8,64]{1,0:T(8,128)} %get-tuple-element.20) | copy-start | bytes 6148
  79.4 38.8 %copy-start.13 = (f32[8,64]{1,0:T(8,128)S(1)}, f32[8,64]{1,0:T(8,128)}, u32[]{:S(2)}) copy-start(f32[8,64]{1,0:T(8,128)} %get-tuple-element.21) | copy-start | bytes 6148
  79.4 38.8 %copy-start.14 = (f32[8,64]{1,0:T(8,128)S(1)}, f32[8,64]{1,0:T(8,128)}, u32[]{:S(2)}) copy-start(f32[8,64]{1,0:T(8,128)} %get-tuple-element.22) | copy-start | bytes 6148
  85.6 31.3 %copy-start.10 = (f32[8,192]{1,0:T(8,128)S(1)}, f32[8,192]{1,0:T(8,128)}, u32[]{:S(2)}) copy-start(f32[8,192]{1,0:T(8,128)} %get-tuple-element.17) | copy-start | bytes 18436
  85.6 32.6 %copy-start.15 = (f32[8,64]{1,0:T(8,128)S(1)}, f32[8,64]{1,0:T(8,128)}, u32[]{:S(2)}) copy-start(f32[8,64]{1,0:T(8,128)} %get-tuple-element.23) | copy-start | bytes 6148
  96.4 20.5 %copy-start.11 = (f32[8,192]{1,0:T(8,128)S(1)}, f32[8,192]{1,0:T(8,128)}, u32[]{:S(2)}) copy-start(f32[8,192]{1,0:T(8,128)} %get-tuple-element.18) | copy-start | bytes 18436
  96.4 21.8 %copy-start.16 = (f32[8,64]{1,0:T(8,128)S(1)}, f32[8,64]{1,0:T(8,128)}, u32[]{:S(2)}) copy-start(f32[8,64]{1,0:T(8,128)} %get-tuple-element.24) | copy-start | bytes 6148
  96.4 1.2 copy-start.5
